TPU v7x, 128 devices: a whole 4x4x4 slice. The times are simulated.
128 devices in a mesh: dev: 128 (over x, y, z, core).
Axes of the slice: x: 4, y: 4, z: 4, core: 2. Of those that a mesh axis runs over, the one named last changes fastest.
Arguments:
- right_sides: float32 [128, 256, 512], P('dev'), may hold values from -6 to 6
- diag_inverse: float32 [256, 512, 512], P('dev'), may hold values from -0.25 to 0.25
- factor_tiles: float32 [1024, 512, 512], P('dev'), may hold values from -0.09375 to 0.09375
- node_level: int32 [256], replicated, may hold values from 0 to 4, as said below
- tile_column: int32 [1024], replicated, may hold values from 0 to 255, as said below
- tile_row: int32 [1024], replicated, may hold values from 0 to 255, as said below
Outputs:
- solution: float32 [128, 256, 512], P('dev')
Inputs may be any that keep to these rules, and one draw needn't show every extreme that they name: `node_level`: supernode s is owned by device s // 2; the 2 supernodes of one device lie at different levels, and every level holds supernodes of two or more devices. `tile_column`: tile k is held by device k // 8; its column supernode lies at a lower level than its row supernode. Among one device's tiles whose column supernodes lie at one level there are at most 4 tiles, 2 distinct column supernodes and 2 distinct row supernodes; some device reaches all three bounds. A pair of supernodes may recur on several tiles. `tile_row`: drawn together with tile_column, under its bounds.
All inputs are finite; a program needn't handle non-finite values.
Results may differ from a plain program's by a relative error of at most 0.0001.
Values sent between devices are 32-bit elements; how exact they have to be, the bound alone decides.
No kernel may reach another device: no remote copies, remote signals or barrier semaphores. Data moves between devices by JAX's collectives and lax.ppermute only.
A program may use at most 128 MiB of HBM per device.

v0:
```python
import jax
import jax.numpy as jnp
from jax import lax
from jax.sharding import PartitionSpec as P

LEVELS = 5
ACTIVE = 4

product_precision = lax.Precision.HIGH
select_precision = lax.Precision.HIGHEST


def prefix_count(mask):
    m = mask.shape[-1]
    upto = jnp.arange(m)[:, None] <= jnp.arange(m)[None, :]
    return jnp.sum((upto & mask[..., :, None]).astype(jnp.int32), axis=-2)


def first_mask(mask):
    return mask & (prefix_count(mask) == 1)


def two_distinct(labels, active):
    l0 = jnp.sum(jnp.where(first_mask(active), labels[None], 0), axis=-1)
    other = active & (labels[None] != l0[..., None])
    l1 = jnp.sum(jnp.where(first_mask(other), labels[None], 0), axis=-1)
    ids = jnp.stack([l0, l1], axis=-1)
    valid = jnp.stack([jnp.any(active, axis=-1), jnp.any(other, axis=-1)], axis=-1)
    slot = (labels[None] != l0[..., None]).astype(jnp.int32)
    return ids, valid, slot


def a2a(x):
    return lax.all_to_all(x, "dev", split_axis=0, concat_axis=0, tiled=True)


def per_device(right_sides, diag_inverse, factor_tiles, node_level, tile_column, tile_row):
    devices = lax.axis_size("dev")
    myself = lax.axis_index("dev")
    per_owner = diag_inverse.shape[0]
    per_holder = factor_tiles.shape[0]
    block = factor_tiles.shape[1]
    supernodes = node_level.shape[0]
    tile_levels = LEVELS - 1

    rhs = right_sides[0].reshape(devices, per_owner, block)
    update = jnp.zeros_like(rhs)

    node_ids = jnp.arange(supernodes, dtype=jnp.int32)
    level_ids = jnp.arange(LEVELS, dtype=jnp.int32)
    tile_level = jnp.sum(jnp.where(tile_column[:, None] == node_ids[None, :], node_level[None, :], 0), axis=1)
    owner_levels = node_level.reshape(devices, per_owner)
    owner_at = owner_levels[None] == level_ids[:, None, None]
    my_owner_at = lax.dynamic_index_in_dim(owner_at, myself, 1, keepdims=False)
    my_slot = jnp.sum(jnp.where(my_owner_at, jnp.arange(per_owner, dtype=jnp.int32)[None], 0), axis=-1)
    owner_slot = jnp.sum(jnp.where(owner_at, jnp.arange(per_owner, dtype=jnp.int32)[None, None], 0), axis=-1)

    holder_levels = tile_level.reshape(devices, per_holder)
    active = holder_levels[None] == level_ids[:tile_levels, None, None]
    col_ids, col_valid, col_slot = two_distinct(tile_column.reshape(devices, per_holder), active)
    row_ids, row_valid, row_slot = two_distinct(tile_row.reshape(devices, per_holder), active)
    targets = jnp.where(row_valid, row_ids, -1).reshape(tile_levels, devices * 2)
    col_owner = col_ids // per_owner

    mine = lax.dynamic_index_in_dim(active, myself, 1, keepdims=False)
    mine_cs = lax.dynamic_index_in_dim(col_slot, myself, 1, keepdims=False)
    mine_rs = lax.dynamic_index_in_dim(row_slot, myself, 1, keepdims=False)
    order = prefix_count(mine) - 1
    hit = mine[:, None, :] & (order[:, None, :] == jnp.arange(ACTIVE, dtype=jnp.int32)[None, :, None])
    present = jnp.any(hit, axis=-1)
    tile_ids = jnp.arange(per_holder, dtype=jnp.int32)
    slot_tile = jnp.sum(jnp.where(hit, tile_ids[None, None, :], 0), axis=-1)
    slot_cs = jnp.sum(jnp.where(hit, mine_cs[:, None, :], 0), axis=-1)
    slot_rs = jnp.sum(jnp.where(hit, mine_rs[:, None, :], 0), axis=-1)
    row_mask = present[..., None] & (slot_rs[..., None] == jnp.arange(2, dtype=jnp.int32))

    owner_node = jnp.arange(devices, dtype=jnp.int32)[None, :] * per_owner + owner_slot

    def at_level(table, current):
        return lax.dynamic_index_in_dim(table, current, 0, keepdims=False)

    def residual(current, update, coming_prev, targets_prev):
        residue = jnp.sum(jnp.where(at_level(owner_at, current)[:, :, None], rhs - update, 0.0), axis=1)
        if coming_prev is not None:
            pick_rows = (at_level(owner_node, current)[:, None] == targets_prev[None, :]).astype(jnp.float32)
            residue = residue - jnp.dot(pick_rows, coming_prev, precision=select_precision,
                                        preferred_element_type=jnp.float32)
            onehot = (node_ids[:, None] == targets_prev[None, :]).astype(jnp.float32)
            added = jnp.dot(onehot, coming_prev, precision=select_precision,
                            preferred_element_type=jnp.float32)
            update = update + added.reshape(devices, per_owner, block)
        return residue, update

    def solve(current, residue):
        gathered = a2a(residue)
        inverse = lax.dynamic_index_in_dim(diag_inverse, at_level(my_slot, current), 0, keepdims=False)
        solved = jnp.dot(gathered, inverse, precision=product_precision,
                         preferred_element_type=jnp.float32)
        return a2a(solved)

    def tiles(current, returned):
        carried = jnp.take(returned, at_level(col_owner, current).reshape(-1), axis=0,
                           mode="clip").reshape(devices, 2, block)
        blocks = a2a(carried)
        factors = jnp.take(factor_tiles, at_level(slot_tile, current), axis=0, mode="clip")
        sources = jnp.where(at_level(slot_cs, current)[None, :, None] == 0,
                            blocks[:, 0:1, :], blocks[:, 1:2, :])
        terms = jnp.einsum("rtb,tbc->rtc", sources, factors, precision=product_precision,
                           preferred_element_type=jnp.float32)
        mask = at_level(row_mask, current)
        products = jnp.stack(
            [jnp.sum(jnp.where(mask[None, :, j, None], terms, 0.0), axis=1) for j in range(2)], axis=1)
        return a2a(products).reshape(devices * 2, block), at_level(targets, current)

    residue, update = residual(0, update, None, None)
    first = solve(0, residue)
    coming, coming_targets = tiles(0, first)

    def middle(current, carry):
        update, coming, coming_targets, kept = carry
        residue, update = residual(current, update, coming, coming_targets)
        returned = solve(current, residue)
        kept = lax.dynamic_update_index_in_dim(kept, returned, current - 1, 0)
        coming, coming_targets = tiles(current, returned)
        return update, coming, coming_targets, kept

    kept = jnp.zeros((tile_levels - 1, devices, block), jnp.float32)
    update, coming, coming_targets, kept = lax.fori_loop(
        1, tile_levels, middle, (update, coming, coming_targets, kept))
    residue, _ = residual(LEVELS - 1, update, coming, coming_targets)
    last = solve(LEVELS - 1, residue)

    solved_rows = [first] + [kept[i] for i in range(tile_levels - 1)] + [last]
    solution = solved_rows[0][:, None, :]
    for current in range(1, LEVELS):
        solution = jnp.where(owner_at[current][:, :, None], solved_rows[current][:, None, :], solution)
    return solution.reshape(1, supernodes, block)


def solution(mesh):
    placed = (P("dev", None, None), P("dev", None, None), P("dev", None, None), P(), P(), P())
    return jax.shard_map(
        per_device, mesh=mesh, in_specs=placed, out_specs=P("dev", None, None), check_vma=False
    )
```

profile of v0, /device:TPU:1, one launch (start us, length us, event | category | flops | bytes accessed | tf_op | source)
XLA Modules:
  0.0 387.4 jit_solution(8637847253854369653)
XLA Ops:
  10.1 11.5 %all-to-all-start.4 = ((f32[128,1,512]{2,1,0:T(1,128)}), f32[128,1,512]{2,1,0:T(1,128)S(1)}, u32[]{:S(2)}, u32[]{:S(2)}) async-start(f32[128,1,512]{2,1,0:T(1,128)} %all_to_all.110), calls=%async_computation.4 | async-start | bytes 524288 | tf_op jit(solution)/shard_map/all_to_all | solution.py:34
  24.1 8.3 %all-to-all-done.4 = f32[128,1,512]{2,1,0:T(1,128)S(1)} async-done(((f32[128,1,512]{2,1,0:T(1,128)}), f32[128,1,512]{2,1,0:T(1,128)S(1)}, u32[]{:S(2)}, u32[]{:S(2)}) %all-to-all-start.4) | async-done | bytes 262176 | tf_op jit(solution)/shard_map/all_to_all | solution.py:34
  33.8 4.7 %all-to-all-start.5 = ((f32[128,1,512]{2,1,0:T(1,128)}), f32[128,1,512]{2,1,0:T(1,128)S(1)}, u32[]{:S(2)}, u32[]{:S(2)}) async-start(f32[128,1,512]{2,1,0:T(1,128)} %copy.139), calls=%async_computation.5 | async-start | bytes 524288 | tf_op jit(solution)/shard_map/all_to_all | solution.py:34
  39.0 10.3 %all-to-all-done.5 = f32[128,1,512]{2,1,0:T(1,128)S(1)} async-done(((f32[128,1,512]{2,1,0:T(1,128)}), f32[128,1,512]{2,1,0:T(1,128)S(1)}, u32[]{:S(2)}, u32[]{:S(2)}) %all-to-all-start.5) | async-done | bytes 262176 | tf_op jit(solution)/shard_map/all_to_all | solution.py:34
  51.4 4.7 %all-to-all-start.6 = ((f32[128,2,512]{2,1,0:T(2,128)}), f32[128,2,512]{2,1,0:T(2,128)S(1)}, u32[]{:S(2)}, u32[]{:S(2)}) async-start(f32[128,2,512]{2,1,0:T(2,128)} %reshape.391), calls=%async_computation.6 | async-start | bytes 1048576 | tf_op jit(solution)/shard_map/all_to_all | solution.py:34
  56.2 6.1 %gather_fusion.2 = f32[4,512,512]{2,1,0:T(8,128)} fusion(f32[8,512,512]{2,1,0:T(8,128)} %param.10, s32[1024]{0:T(1024)S(1)} %pad_clamp_fusion.3), kind=kCustom, calls=%fused_computation.2 | custom fusion | bytes 8388624 | tf_op jit(solution)/shard_map/jit(_take)/gather | solution.py:105
  62.7 7.1 %all-to-all-done.6 = f32[128,2,512]{2,1,0:T(2,128)S(1)} async-done(((f32[128,2,512]{2,1,0:T(2,128)}), f32[128,2,512]{2,1,0:T(2,128)S(1)}, u32[]{:S(2)}, u32[]{:S(2)}) %all-to-all-start.6) | async-done | bytes 524320 | tf_op jit(solution)/shard_map/all_to_all | solution.py:34
  70.2 5.8 %select_reduce_fusion.4 = (f32[512,128]{1,0:T(8,128)S(1)}, f32[512,128]{1,0:T(8,128)S(1)}) fusion(pred[4]{0:T(512)(128)(4,1)S(1)} %get-tuple-element.815, pred[4]{0:T(512)(128)(4,1)S(1)} %get-tuple-element.816, f32[4,512,512]{2,1,0:T(8,128)} %gather_fusion.2, f32[128,512]{1,0:T(8,128)S(1)} %bitcast.157, f32[128,512]{1,0:T(8,128)S(1)} %bitcast.156, ...), kind=kOutput, calls=%fused_computation.56 | convolution fusion | flops 806486016 | bytes 5242892 | tf_op jit(solution)/shard_map/rtb,tbc->rtc/dot_general | solution.py:108
  77.0 4.7 %all-to-all-start.7 = ((f32[128,2,512]{2,1,0:T(2,128)}), f32[128,2,512]{2,1,0:T(2,128)S(1)}, u32[]{:S(2)}, u32[]{:S(2)}) async-start(f32[128,2,512]{2,1,0:T(2,128)} %copy.145), calls=%async_computation.7 | async-start | bytes 1048576 | tf_op jit(solution)/shard_map/all_to_all | solution.py:34
  81.7 13.6 %all-to-all-done.7 = f32[128,2,512]{2,1,0:T(2,128)S(1)} async-done(((f32[128,2,512]{2,1,0:T(2,128)}), f32[128,2,512]{2,1,0:T(2,128)S(1)}, u32[]{:S(2)}, u32[]{:S(2)}) %all-to-all-start.7) | async-done | bytes 524320 | tf_op jit(solution)/shard_map/all_to_all | solution.py:34
  95.7 254.3 %while.26 = (s32[]{:T(128)}, f32[128,2,512]{2,1,0:T(2,128)}, f32[256,512]{1,0:T(8,128)S(1)}, s32[256]{0:T(256)S(1)}, f32[3,128,512]{2,0,1:T(4,128)}, /*index=5*/...) while((s32[]{:T(128)}, f32[128,2,512]{2,1,0:T(2,128)}, ...), condition=%wide.region_24.25_spmd.clone, body=%wide.region_20.24_spmd.clone.sunk | while | flops 1612679168 | bytes 34888540 | solution.py:128
  99.6 4.7 %all-to-all-start = ((f32[128,1,512]{2,1,0:T(1,128)}), f32[128,1,512]{2,1,0:T(1,128)S(1)}, u32[]{:S(2)}, u32[]{:S(2)}) async-start(f32[128,1,512]{2,1,0:T(1,128)} %copy.220), calls=%async_computation | async-start | bytes 524288 | tf_op jit(solution)/shard_map/while/body/eval_jaxpr/all_to_all | solution.py:34
  106.8 8.4 %all-to-all-done = f32[128,1,512]{2,1,0:T(1,128)S(1)} async-done(((f32[128,1,512]{2,1,0:T(1,128)}), f32[128,1,512]{2,1,0:T(1,128)S(1)}, u32[]{:S(2)}, u32[]{:S(2)}) %all-to-all-start) | async-done | bytes 262176 | tf_op jit(solution)/shard_map/while/body/eval_jaxpr/all_to_all | solution.py:34
  117.8 4.7 %all-to-all-start.1 = ((f32[128,1,512]{2,1,0:T(1,128)}), f32[128,1,512]{2,1,0:T(1,128)S(1)}, u32[]{:S(2)}, u32[]{:S(2)}) async-start(f32[128,1,512]{2,1,0:T(1,128)} %copy.221), calls=%async_computation.1 | async-start | bytes 524288 | tf_op jit(solution)/shard_map/while/body/eval_jaxpr/all_to_all | solution.py:34
  122.8 10.5 %all-to-all-done.1 = f32[128,1,512]{2,1,0:T(1,128)S(1)} async-done(((f32[128,1,512]{2,1,0:T(1,128)}), f32[128,1,512]{2,1,0:T(1,128)S(1)}, u32[]{:S(2)}, u32[]{:S(2)}) %all-to-all-start.1) | async-done | bytes 262176 | tf_op jit(solution)/shard_map/while/body/eval_jaxpr/all_to_all | solution.py:34
  135.4 4.7 %all-to-all-start.2 = ((f32[128,2,512]{2,1,0:T(2,128)}), f32[128,2,512]{2,1,0:T(2,128)S(1)}, u32[]{:S(2)}, u32[]{:S(2)}) async-start(f32[128,2,512]{2,1,0:T(2,128)} %reshape.459), calls=%async_computation.2 | async-start | bytes 1048576 | tf_op jit(solution)/shard_map/while/body/eval_jaxpr/all_to_all | solution.py:34
  140.2 6.1 %gather_fusion = f32[4,512,512]{2,1,0:T(8,128)} fusion(f32[8,512,512]{2,1,0:T(8,128)} %get-tuple-element.1050, s32[1024]{0:T(1024)S(1)} %pad_clamp_fusion.6), kind=kCustom, calls=%fused_computation.clone.clone.1 | custom fusion | bytes 8388624 | tf_op jit(solution)/shard_map/while/body/eval_jaxpr/jit(_take)/gather | solution.py:105
  146.5 7.2 %all-to-all-done.2 = f32[128,2,512]{2,1,0:T(2,128)S(1)} async-done(((f32[128,2,512]{2,1,0:T(2,128)}), f32[128,2,512]{2,1,0:T(2,128)S(1)}, u32[]{:S(2)}, u32[]{:S(2)}) %all-to-all-start.2) | async-done | bytes 524320 | tf_op jit(solution)/shard_map/while/body/eval_jaxpr/all_to_all | solution.py:34
  154.2 5.8 %select_reduce_fusion.19 = (f32[512,128]{1,0:T(8,128)S(1)}, f32[512,128]{1,0:T(8,128)S(1)}) fusion(pred[4]{0:T(512)(128)(4,1)S(1)} %get-tuple-element.992, pred[4]{0:T(512)(128)(4,1)S(1)} %get-tuple-element.993, f32[4,512,512]{2,1,0:T(8,128)} %gather_fusion, f32[128,512]{1,0:T(8,128)S(1)} %get-tuple-element.997, ...), kind=kOutput, calls=%fused_computation.10.clone.1 | convolution fusion | flops 806486016 | bytes 5242892 | tf_op jit(solution)/shard_map/while/body/eval_jaxpr/rtb,tbc->rtc/dot_general | solution.py:108
  161.0 4.7 %all-to-all-start.3 = ((f32[128,2,512]{2,1,0:T(2,128)}), f32[128,2,512]{2,1,0:T(2,128)S(1)}, u32[]{:S(2)}, u32[]{:S(2)}) async-start(f32[128,2,512]{2,1,0:T(2,128)} %copy.224), calls=%async_computation.3 | async-start | bytes 1048576 | tf_op jit(solution)/shard_map/while/body/eval_jaxpr/all_to_all | solution.py:34
  165.7 6.1 %dynamic_update_slice.19 = f32[3,128,512]{2,0,1:T(4,128)} dynamic-update-slice(f32[3,128,512]{2,0,1:T(4,128)} %get-tuple-element.1026, f32[1,128,512]{2,0,1:T(1,128)S(1)} %bitcast.153, s32[]{:T(128)S(6)} %copy.231, s32[]{:T(128)} %constant.218.clone.1..sunk, s32[]{:T(128)} %constant.218.clone.1..sunk) | dynamic-update-slice | bytes 524292 | tf_op jit(solution)/shard_map/while/body/eval_jaxpr/jit(dynamic_update_index_in_dim)/dynamic_update_slice | solution.py:123
  171.8 7.5 %all-to-all-done.3 = f32[128,2,512]{2,1,0:T(2,128)S(1)} async-done(((f32[128,2,512]{2,1,0:T(2,128)}), f32[128,2,512]{2,1,0:T(2,128)S(1)}, u32[]{:S(2)}, u32[]{:S(2)}) %all-to-all-start.3) | async-done | bytes 524320 | tf_op jit(solution)/shard_map/while/body/eval_jaxpr/all_to_all | solution.py:34
  184.6 4.7 %all-to-all-start = ((f32[128,1,512]{2,1,0:T(1,128)}), f32[128,1,512]{2,1,0:T(1,128)S(1)}, u32[]{:S(2)}, u32[]{:S(2)}) async-start(f32[128,1,512]{2,1,0:T(1,128)} %copy.220), calls=%async_computation | async-start | bytes 524288 | tf_op jit(solution)/shard_map/while/body/eval_jaxpr/all_to_all | solution.py:34
  191.8 8.4 %all-to-all-done = f32[128,1,512]{2,1,0:T(1,128)S(1)} async-done(((f32[128,1,512]{2,1,0:T(1,128)}), f32[128,1,512]{2,1,0:T(1,128)S(1)}, u32[]{:S(2)}, u32[]{:S(2)}) %all-to-all-start) | async-done | bytes 262176 | tf_op jit(solution)/shard_map/while/body/eval_jaxpr/all_to_all | solution.py:34
  202.8 4.7 %all-to-all-start.1 = ((f32[128,1,512]{2,1,0:T(1,128)}), f32[128,1,512]{2,1,0:T(1,128)S(1)}, u32[]{:S(2)}, u32[]{:S(2)}) async-start(f32[128,1,512]{2,1,0:T(1,128)} %copy.221), calls=%async_computation.1 | async-start | bytes 524288 | tf_op jit(solution)/shard_map/while/body/eval_jaxpr/all_to_all | solution.py:34
  207.8 10.5 %all-to-all-done.1 = f32[128,1,512]{2,1,0:T(1,128)S(1)} async-done(((f32[128,1,512]{2,1,0:T(1,128)}), f32[128,1,512]{2,1,0:T(1,128)S(1)}, u32[]{:S(2)}, u32[]{:S(2)}) %all-to-all-start.1) | async-done | bytes 262176 | tf_op jit(solution)/shard_map/while/body/eval_jaxpr/all_to_all | solution.py:34
  220.5 4.7 %all-to-all-start.2 = ((f32[128,2,512]{2,1,0:T(2,128)}), f32[128,2,512]{2,1,0:T(2,128)S(1)}, u32[]{:S(2)}, u32[]{:S(2)}) async-start(f32[128,2,512]{2,1,0:T(2,128)} %reshape.459), calls=%async_computation.2 | async-start | bytes 1048576 | tf_op jit(solution)/shard_map/while/body/eval_jaxpr/all_to_all | solution.py:34
  225.2 6.1 %gather_fusion = f32[4,512,512]{2,1,0:T(8,128)} fusion(f32[8,512,512]{2,1,0:T(8,128)} %get-tuple-element.1050, s32[1024]{0:T(1024)S(1)} %pad_clamp_fusion.6), kind=kCustom, calls=%fused_computation.clone.clone.1 | custom fusion | bytes 8388624 | tf_op jit(solution)/shard_map/while/body/eval_jaxpr/jit(_take)/gather | solution.py:105
  231.5 7.2 %all-to-all-done.2 = f32[128,2,512]{2,1,0:T(2,128)S(1)} async-done(((f32[128,2,512]{2,1,0:T(2,128)}), f32[128,2,512]{2,1,0:T(2,128)S(1)}, u32[]{:S(2)}, u32[]{:S(2)}) %all-to-all-start.2) | async-done | bytes 524320 | tf_op jit(solution)/shard_map/while/body/eval_jaxpr/all_to_all | solution.py:34
  239.2 5.8 %select_reduce_fusion.19 = (f32[512,128]{1,0:T(8,128)S(1)}, f32[512,128]{1,0:T(8,128)S(1)}) fusion(pred[4]{0:T(512)(128)(4,1)S(1)} %get-tuple-element.992, pred[4]{0:T(512)(128)(4,1)S(1)} %get-tuple-element.993, f32[4,512,512]{2,1,0:T(8,128)} %gather_fusion, f32[128,512]{1,0:T(8,128)S(1)} %get-tuple-element.997, ...), kind=kOutput, calls=%fused_computation.10.clone.1 | convolution fusion | flops 806486016 | bytes 5242892 | tf_op jit(solution)/shard_map/while/body/eval_jaxpr/rtb,tbc->rtc/dot_general | solution.py:108
  246.0 4.7 %all-to-all-start.3 = ((f32[128,2,512]{2,1,0:T(2,128)}), f32[128,2,512]{2,1,0:T(2,128)S(1)}, u32[]{:S(2)}, u32[]{:S(2)}) async-start(f32[128,2,512]{2,1,0:T(2,128)} %copy.224), calls=%async_computation.3 | async-start | bytes 1048576 | tf_op jit(solution)/shard_map/while/body/eval_jaxpr/all_to_all | solution.py:34
  250.7 6.1 %dynamic_update_slice.19 = f32[3,128,512]{2,0,1:T(4,128)} dynamic-update-slice(f32[3,128,512]{2,0,1:T(4,128)} %get-tuple-element.1026, f32[1,128,512]{2,0,1:T(1,128)S(1)} %bitcast.153, s32[]{:T(128)S(6)} %copy.231, s32[]{:T(128)} %constant.218.clone.1..sunk, s32[]{:T(128)} %constant.218.clone.1..sunk) | dynamic-update-slice | bytes 524292 | tf_op jit(solution)/shard_map/while/body/eval_jaxpr/jit(dynamic_update_index_in_dim)/dynamic_update_slice | solution.py:123
  256.8 7.5 %all-to-all-done.3 = f32[128,2,512]{2,1,0:T(2,128)S(1)} async-done(((f32[128,2,512]{2,1,0:T(2,128)}), f32[128,2,512]{2,1,0:T(2,128)S(1)}, u32[]{:S(2)}, u32[]{:S(2)}) %all-to-all-start.3) | async-done | bytes 524320 | tf_op jit(solution)/shard_map/while/body/eval_jaxpr/all_to_all | solution.py:34
  269.6 4.7 %all-to-all-start = ((f32[128,1,512]{2,1,0:T(1,128)}), f32[128,1,512]{2,1,0:T(1,128)S(1)}, u32[]{:S(2)}, u32[]{:S(2)}) async-start(f32[128,1,512]{2,1,0:T(1,128)} %copy.220), calls=%async_computation | async-start | bytes 524288 | tf_op jit(solution)/shard_map/while/body/eval_jaxpr/all_to_all | solution.py:34
  276.8 8.4 %all-to-all-done = f32[128,1,512]{2,1,0:T(1,128)S(1)} async-done(((f32[128,1,512]{2,1,0:T(1,128)}), f32[128,1,512]{2,1,0:T(1,128)S(1)}, u32[]{:S(2)}, u32[]{:S(2)}) %all-to-all-start) | async-done | bytes 262176 | tf_op jit(solution)/shard_map/while/body/eval_jaxpr/all_to_all | solution.py:34
  287.8 4.7 %all-to-all-start.1 = ((f32[128,1,512]{2,1,0:T(1,128)}), f32[128,1,512]{2,1,0:T(1,128)S(1)}, u32[]{:S(2)}, u32[]{:S(2)}) async-start(f32[128,1,512]{2,1,0:T(1,128)} %copy.221), calls=%async_computation.1 | async-start | bytes 524288 | tf_op jit(solution)/shard_map/while/body/eval_jaxpr/all_to_all | solution.py:34
  292.8 10.5 %all-to-all-done.1 = f32[128,1,512]{2,1,0:T(1,128)S(1)} async-done(((f32[128,1,512]{2,1,0:T(1,128)}), f32[128,1,512]{2,1,0:T(1,128)S(1)}, u32[]{:S(2)}, u32[]{:S(2)}) %all-to-all-start.1) | async-done | bytes 262176 | tf_op jit(solution)/shard_map/while/body/eval_jaxpr/all_to_all | solution.py:34
  305.5 4.7 %all-to-all-start.2 = ((f32[128,2,512]{2,1,0:T(2,128)}), f32[128,2,512]{2,1,0:T(2,128)S(1)}, u32[]{:S(2)}, u32[]{:S(2)}) async-start(f32[128,2,512]{2,1,0:T(2,128)} %reshape.459), calls=%async_computation.2 | async-start | bytes 1048576 | tf_op jit(solution)/shard_map/while/body/eval_jaxpr/all_to_all | solution.py:34
  310.2 6.1 %gather_fusion = f32[4,512,512]{2,1,0:T(8,128)} fusion(f32[8,512,512]{2,1,0:T(8,128)} %get-tuple-element.1050, s32[1024]{0:T(1024)S(1)} %pad_clamp_fusion.6), kind=kCustom, calls=%fused_computation.clone.clone.1 | custom fusion | bytes 8388624 | tf_op jit(solution)/shard_map/while/body/eval_jaxpr/jit(_take)/gather | solution.py:105
  316.5 7.2 %all-to-all-done.2 = f32[128,2,512]{2,1,0:T(2,128)S(1)} async-done(((f32[128,2,512]{2,1,0:T(2,128)}), f32[128,2,512]{2,1,0:T(2,128)S(1)}, u32[]{:S(2)}, u32[]{:S(2)}) %all-to-all-start.2) | async-done | bytes 524320 | tf_op jit(solution)/shard_map/while/body/eval_jaxpr/all_to_all | solution.py:34
  324.2 5.8 %select_reduce_fusion.19 = (f32[512,128]{1,0:T(8,128)S(1)}, f32[512,128]{1,0:T(8,128)S(1)}) fusion(pred[4]{0:T(512)(128)(4,1)S(1)} %get-tuple-element.992, pred[4]{0:T(512)(128)(4,1)S(1)} %get-tuple-element.993, f32[4,512,512]{2,1,0:T(8,128)} %gather_fusion, f32[128,512]{1,0:T(8,128)S(1)} %get-tuple-element.997, ...), kind=kOutput, calls=%fused_computation.10.clone.1 | convolution fusion | flops 806486016 | bytes 5242892 | tf_op jit(solution)/shard_map/while/body/eval_jaxpr/rtb,tbc->rtc/dot_general | solution.py:108
  331.0 4.7 %all-to-all-start.3 = ((f32[128,2,512]{2,1,0:T(2,128)}), f32[128,2,512]{2,1,0:T(2,128)S(1)}, u32[]{:S(2)}, u32[]{:S(2)}) async-start(f32[128,2,512]{2,1,0:T(2,128)} %copy.224), calls=%async_computation.3 | async-start | bytes 1048576 | tf_op jit(solution)/shard_map/while/body/eval_jaxpr/all_to_all | solution.py:34
  335.7 6.1 %dynamic_update_slice.19 = f32[3,128,512]{2,0,1:T(4,128)} dynamic-update-slice(f32[3,128,512]{2,0,1:T(4,128)} %get-tuple-element.1026, f32[1,128,512]{2,0,1:T(1,128)S(1)} %bitcast.153, s32[]{:T(128)S(6)} %copy.231, s32[]{:T(128)} %constant.218.clone.1..sunk, s32[]{:T(128)} %constant.218.clone.1..sunk) | dynamic-update-slice | bytes 524292 | tf_op jit(solution)/shard_map/while/body/eval_jaxpr/jit(dynamic_update_index_in_dim)/dynamic_update_slice | solution.py:123
  341.8 7.5 %all-to-all-done.3 = f32[128,2,512]{2,1,0:T(2,128)S(1)} async-done(((f32[128,2,512]{2,1,0:T(2,128)}), f32[128,2,512]{2,1,0:T(2,128)S(1)}, u32[]{:S(2)}, u32[]{:S(2)}) %all-to-all-start.3) | async-done | bytes 524320 | tf_op jit(solution)/shard_map/while/body/eval_jaxpr/all_to_all | solution.py:34
  353.3 4.7 %all-to-all-start.8 = ((f32[128,1,512]{2,1,0:T(1,128)}), f32[128,1,512]{2,1,0:T(1,128)S(1)}, u32[]{:S(2)}, u32[]{:S(2)}) async-start(f32[128,1,512]{2,1,0:T(1,128)} %copy.157), calls=%async_computation.8 | async-start | bytes 524288 | tf_op jit(solution)/shard_map/all_to_all | solution.py:34
  361.2 7.7 %all-to-all-done.8 = f32[128,1,512]{2,1,0:T(1,128)S(1)} async-done(((f32[128,1,512]{2,1,0:T(1,128)}), f32[128,1,512]{2,1,0:T(1,128)S(1)}, u32[]{:S(2)}, u32[]{:S(2)}) %all-to-all-start.8) | async-done | bytes 262176 | tf_op jit(solution)/shard_map/all_to_all | solution.py:34
  370.3 4.7 %all-to-all-start.9 = ((f32[128,1,512]{2,1,0:T(1,128)}), f32[128,1,512]{2,1,0:T(1,128)S(1)}, u32[]{:S(2)}, u32[]{:S(2)}) async-start(f32[128,1,512]{2,1,0:T(1,128)} %copy.158), calls=%async_computation.9 | async-start | bytes 524288 | tf_op jit(solution)/shard_map/all_to_all | solution.py:34
  379.5 6.3 %all-to-all-done.9 = f32[128,1,512]{2,1,0:T(1,128)S(1)} async-done(((f32[128,1,512]{2,1,0:T(1,128)}), f32[128,1,512]{2,1,0:T(1,128)S(1)}, u32[]{:S(2)}, u32[]{:S(2)}) %all-to-all-start.9) | async-done | bytes 262176 | tf_op jit(solution)/shard_map/all_to_all | solution.py:34
  (186 shorter events, 64.7 us)
Async XLA Ops:
  0.0 32.4 %copy-start = (f32[2,512,512]{2,1,0:T(8,128)S(1)}, f32[2,512,512]{2,1,0:T(8,128)}, u32[]{:S(2)}) copy-start(f32[2,512,512]{2,1,0:T(8,128)} %param.9) | copy-start | bytes 6291460
  10.1 22.3 %all-to-all-start.4 = ((f32[128,1,512]{2,1,0:T(1,128)}), f32[128,1,512]{2,1,0:T(1,128)S(1)}, u32[]{:S(2)}, u32[]{:S(2)}) async-start(f32[128,1,512]{2,1,0:T(1,128)} %all_to_all.110), calls=%async_computation.4 | async-start | bytes 524288 | tf_op jit(solution)/shard_map/all_to_all | solution.py:34
  33.8 15.5 %all-to-all-start.5 = ((f32[128,1,512]{2,1,0:T(1,128)}), f32[128,1,512]{2,1,0:T(1,128)S(1)}, u32[]{:S(2)}, u32[]{:S(2)}) async-start(f32[128,1,512]{2,1,0:T(1,128)} %copy.139), calls=%async_computation.5 | async-start | bytes 524288 | tf_op jit(solution)/shard_map/all_to_all | solution.py:34
  51.4 18.3 %all-to-all-start.6 = ((f32[128,2,512]{2,1,0:T(2,128)}), f32[128,2,512]{2,1,0:T(2,128)S(1)}, u32[]{:S(2)}, u32[]{:S(2)}) async-start(f32[128,2,512]{2,1,0:T(2,128)} %reshape.391), calls=%async_computation.6 | async-start | bytes 1048576 | tf_op jit(solution)/shard_map/all_to_all | solution.py:34
  77.0 18.4 %all-to-all-start.7 = ((f32[128,2,512]{2,1,0:T(2,128)}), f32[128,2,512]{2,1,0:T(2,128)S(1)}, u32[]{:S(2)}, u32[]{:S(2)}) async-start(f32[128,2,512]{2,1,0:T(2,128)} %copy.145), calls=%async_computation.7 | async-start | bytes 1048576 | tf_op jit(solution)/shard_map/all_to_all | solution.py:34
  99.6 15.6 %all-to-all-start = ((f32[128,1,512]{2,1,0:T(1,128)}), f32[128,1,512]{2,1,0:T(1,128)S(1)}, u32[]{:S(2)}, u32[]{:S(2)}) async-start(f32[128,1,512]{2,1,0:T(1,128)} %copy.220), calls=%async_computation | async-start | bytes 524288 | tf_op jit(solution)/shard_map/while/body/eval_jaxpr/all_to_all | solution.py:34
  117.8 15.5 %all-to-all-start.1 = ((f32[128,1,512]{2,1,0:T(1,128)}), f32[128,1,512]{2,1,0:T(1,128)S(1)}, u32[]{:S(2)}, u32[]{:S(2)}) async-start(f32[128,1,512]{2,1,0:T(1,128)} %copy.221), calls=%async_computation.1 | async-start | bytes 524288 | tf_op jit(solution)/shard_map/while/body/eval_jaxpr/all_to_all | solution.py:34
  135.4 18.3 %all-to-all-start.2 = ((f32[128,2,512]{2,1,0:T(2,128)}), f32[128,2,512]{2,1,0:T(2,128)S(1)}, u32[]{:S(2)}, u32[]{:S(2)}) async-start(f32[128,2,512]{2,1,0:T(2,128)} %reshape.459), calls=%async_computation.2 | async-start | bytes 1048576 | tf_op jit(solution)/shard_map/while/body/eval_jaxpr/all_to_all | solution.py:34
  161.0 18.4 %all-to-all-start.3 = ((f32[128,2,512]{2,1,0:T(2,128)}), f32[128,2,512]{2,1,0:T(2,128)S(1)}, u32[]{:S(2)}, u32[]{:S(2)}) async-start(f32[128,2,512]{2,1,0:T(2,128)} %copy.224), calls=%async_computation.3 | async-start | bytes 1048576 | tf_op jit(solution)/shard_map/while/body/eval_jaxpr/all_to_all | solution.py:34
  184.6 15.6 %all-to-all-start = ((f32[128,1,512]{2,1,0:T(1,128)}), f32[128,1,512]{2,1,0:T(1,128)S(1)}, u32[]{:S(2)}, u32[]{:S(2)}) async-start(f32[128,1,512]{2,1,0:T(1,128)} %copy.220), calls=%async_computation | async-start | bytes 524288 | tf_op jit(solution)/shard_map/while/body/eval_jaxpr/all_to_all | solution.py:34
  202.8 15.5 %all-to-all-start.1 = ((f32[128,1,512]{2,1,0:T(1,128)}), f32[128,1,512]{2,1,0:T(1,128)S(1)}, u32[]{:S(2)}, u32[]{:S(2)}) async-start(f32[128,1,512]{2,1,0:T(1,128)} %copy.221), calls=%async_computation.1 | async-start | bytes 524288 | tf_op jit(solution)/shard_map/while/body/eval_jaxpr/all_to_all | solution.py:34
  220.5 18.3 %all-to-all-start.2 = ((f32[128,2,512]{2,1,0:T(2,128)}), f32[128,2,512]{2,1,0:T(2,128)S(1)}, u32[]{:S(2)}, u32[]{:S(2)}) async-start(f32[128,2,512]{2,1,0:T(2,128)} %reshape.459), calls=%async_computation.2 | async-start | bytes 1048576 | tf_op jit(solution)/shard_map/while/body/eval_jaxpr/all_to_all | solution.py:34
  246.0 18.4 %all-to-all-start.3 = ((f32[128,2,512]{2,1,0:T(2,128)}), f32[128,2,512]{2,1,0:T(2,128)S(1)}, u32[]{:S(2)}, u32[]{:S(2)}) async-start(f32[128,2,512]{2,1,0:T(2,128)} %copy.224), calls=%async_computation.3 | async-start | bytes 1048576 | tf_op jit(solution)/shard_map/while/body/eval_jaxpr/all_to_all | solution.py:34
  269.6 15.6 %all-to-all-start = ((f32[128,1,512]{2,1,0:T(1,128)}), f32[128,1,512]{2,1,0:T(1,128)S(1)}, u32[]{:S(2)}, u32[]{:S(2)}) async-start(f32[128,1,512]{2,1,0:T(1,128)} %copy.220), calls=%async_computation | async-start | bytes 524288 | tf_op jit(solution)/shard_map/while/body/eval_jaxpr/all_to_all | solution.py:34
  287.8 15.5 %all-to-all-start.1 = ((f32[128,1,512]{2,1,0:T(1,128)}), f32[128,1,512]{2,1,0:T(1,128)S(1)}, u32[]{:S(2)}, u32[]{:S(2)}) async-start(f32[128,1,512]{2,1,0:T(1,128)} %copy.221), calls=%async_computation.1 | async-start | bytes 524288 | tf_op jit(solution)/shard_map/while/body/eval_jaxpr/all_to_all | solution.py:34
  305.5 18.3 %all-to-all-start.2 = ((f32[128,2,512]{2,1,0:T(2,128)}), f32[128,2,512]{2,1,0:T(2,128)S(1)}, u32[]{:S(2)}, u32[]{:S(2)}) async-start(f32[128,2,512]{2,1,0:T(2,128)} %reshape.459), calls=%async_computation.2 | async-start | bytes 1048576 | tf_op jit(solution)/shard_map/while/body/eval_jaxpr/all_to_all | solution.py:34
  331.0 18.4 %all-to-all-start.3 = ((f32[128,2,512]{2,1,0:T(2,128)}), f32[128,2,512]{2,1,0:T(2,128)S(1)}, u32[]{:S(2)}, u32[]{:S(2)}) async-start(f32[128,2,512]{2,1,0:T(2,128)} %copy.224), calls=%async_computation.3 | async-start | bytes 1048576 | tf_op jit(solution)/shard_map/while/body/eval_jaxpr/all_to_all | solution.py:34
  349.9 18.9 %copy-start.1 = (f32[2,512,512]{2,1,0:T(8,128)S(1)}, f32[2,512,512]{2,1,0:T(8,128)}, u32[]{:S(2)}) copy-start(f32[2,512,512]{2,1,0:T(8,128)} %get-tuple-element.1069) | copy-start | bytes 6291460
  353.3 15.6 %all-to-all-start.8 = ((f32[128,1,512]{2,1,0:T(1,128)}), f32[128,1,512]{2,1,0:T(1,128)S(1)}, u32[]{:S(2)}, u32[]{:S(2)}) async-start(f32[128,1,512]{2,1,0:T(1,128)} %copy.157), calls=%async_computation.8 | async-start | bytes 524288 | tf_op jit(solution)/shard_map/all_to_all | solution.py:34
  370.3 15.5 %all-to-all-start.9 = ((f32[128,1,512]{2,1,0:T(1,128)}), f32[128,1,512]{2,1,0:T(1,128)S(1)}, u32[]{:S(2)}, u32[]{:S(2)}) async-start(f32[128,1,512]{2,1,0:T(1,128)} %copy.158), calls=%async_computation.9 | async-start | bytes 524288 | tf_op jit(solution)/shard_map/all_to_all | solution.py:34
where the time goes:
time: 390 us; the launch traced here: 387 us
  waiting for transfers between devices  154 us (39%)
  starting transfers between devices  91.5 us (23%)
  local copies, waits for them, and re-layouts  85 us (22%)
  matrix products  31.4 us (8%)
  other arithmetic  14.1 us (4%)
  loops' own time  6.56 us (2%)
  between operations  4.68 us (1%)
    all_to_all x18, waiting for transfers between devices, a2a(): return lax.all_to_all(x, 'dev', split_axis=0, concat_axis=0, tiled=True)  154 us
    all_to_all x18, starting transfers between devices, a2a(): return lax.all_to_all(x, 'dev', split_axis=0, concat_axis=0, tiled=True)  91.5 us
    gather x4, local copies, waits for them, and re-layouts, tiles(): jnp.take(factor_tiles, at_level(slot_tile, current), axis=0, mode='clip')  24.5 us
    dot_general x4, matrix products, tiles(): jnp.einsum('rtb,tbc->rtc', sources, factors, precision=product_precision,...  23 us
    dynamic_update_slice x3, local copies, waits for them, and re-layouts, middle(): kept = lax.dynamic_update_index_in_dim(kept, returned, current - 1, 0)  18.3 us
    reduce_sum x5, other arithmetic, residual(): jnp.sum(jnp.where(at_level(owner_at, current)[:, :, None], rhs - update,...  10 us
    all_to_all x10, local copies, waits for them, and re-layouts, a2a(): return lax.all_to_all(x, 'dev', split_axis=0, concat_axis=0, tiled=True)  9.57 us
  transfers between devices with their start and end apart: 18, of which 18 were waited for; matrix products, arithmetic and copies ran while one was open for 14% of the time, Pallas kernels for 0%

commit v1 on v0

--- a/solution.py
+++ b/solution.py
@@ -112,25 +112,23 @@
             [jnp.sum(jnp.where(mask[None, :, j, None], terms, 0.0), axis=1) for j in range(2)], axis=1)
         return a2a(products).reshape(devices * 2, block), at_level(targets, current)
 
-    residue, update = residual(0, update, None, None)
-    first = solve(0, residue)
-    coming, coming_targets = tiles(0, first)
-
-    def middle(current, carry):
+    def level(current, carry):
         update, coming, coming_targets, kept = carry
         residue, update = residual(current, update, coming, coming_targets)
         returned = solve(current, residue)
-        kept = lax.dynamic_update_index_in_dim(kept, returned, current - 1, 0)
+        kept = lax.dynamic_update_index_in_dim(kept, returned, current, 0)
         coming, coming_targets = tiles(current, returned)
         return update, coming, coming_targets, kept
 
-    kept = jnp.zeros((tile_levels - 1, devices, block), jnp.float32)
+    coming = jnp.zeros((devices * 2, block), jnp.float32)
+    coming_targets = jnp.full((devices * 2,), -1, jnp.int32)
+    kept = jnp.zeros((tile_levels, devices, block), jnp.float32)
     update, coming, coming_targets, kept = lax.fori_loop(
-        1, tile_levels, middle, (update, coming, coming_targets, kept))
+        0, tile_levels, level, (update, coming, coming_targets, kept))
     residue, _ = residual(LEVELS - 1, update, coming, coming_targets)
     last = solve(LEVELS - 1, residue)
 
-    solved_rows = [first] + [kept[i] for i in range(tile_levels - 1)] + [last]
+    solved_rows = [kept[i] for i in range(tile_levels)] + [last]
     solution = solved_rows[0][:, None, :]
     for current in range(1, LEVELS):
         solution = jnp.where(owner_at[current][:, :, None], solved_rows[current][:, None, :], solution)

time: 390 us -> 394 us (1.010)
  local copies, waits for them, and re-layouts: 85 us -> 92.8 us
  waiting for transfers between devices: 154 us -> 147 us
    all_to_all x18, waiting for transfers between devices: 154 us -> 147 us  [a2a(): return lax.all_to_all(x, 'dev', split_axis=0, concat_axis=0, tiled=True)]
    dynamic_update_slice x3 -> x4, local copies, waits for them, and re-layouts: 18.3 us -> 24.4 us  [level(): kept = lax.dynamic_update_index_in_dim(kept, returned, current, 0)]
  transfers between devices with their start and end apart: 18 -> 18, of which waited for: 18 -> 18; matrix products, arithmetic and copies ran while one was open for 14% -> 15% of each run, Pallas kernels for 0% -> 0%
where the time goes in v1:
time: 394 us; the launch traced here: 392 us
  waiting for transfers between devices  147 us (37%)
  local copies, waits for them, and re-layouts  92.8 us (24%)
  starting transfers between devices  91.5 us (23%)
  matrix products  33.4 us (8%)
  other arithmetic  16.1 us (4%)
  loops' own time  8.4 us (2%)
    all_to_all x18, waiting for transfers between devices, a2a(): return lax.all_to_all(x, 'dev', split_axis=0, concat_axis=0, tiled=True)  147 us
    all_to_all x18, starting transfers between devices, a2a(): return lax.all_to_all(x, 'dev', split_axis=0, concat_axis=0, tiled=True)  91.5 us
    gather x4, local copies, waits for them, and re-layouts, tiles(): jnp.take(factor_tiles, at_level(slot_tile, current), axis=0, mode='clip')  24.5 us
    dynamic_update_slice x4, local copies, waits for them, and re-layouts, level(): kept = lax.dynamic_update_index_in_dim(kept, returned, current, 0)  24.4 us
    dot_general x4, matrix products, tiles(): jnp.einsum('rtb,tbc->rtc', sources, factors, precision=product_precision,...  23 us
    reduce_sum x5, other arithmetic, residual(): jnp.sum(jnp.where(at_level(owner_at, current)[:, :, None], rhs - update,...  12.1 us
    all_to_all x10, local copies, waits for them, and re-layouts, a2a(): return lax.all_to_all(x, 'dev', split_axis=0, concat_axis=0, tiled=True)  9.65 us
    another operation x1, loops' own time, per_device(): lax.fori_loop(0, tile_levels, level, (update, coming, coming_targets, kept))  8.4 us
  transfers between devices with their start and end apart: 18, of which 18 were waited for; matrix products, arithmetic and copies ran while one was open for 15% of the time, Pallas kernels for 0%

profile of v1, /device:TPU:1, one launch (start us, length us, event | category | flops | bytes accessed | tf_op | source)
XLA Modules:
  0.0 391.7 jit_solution(15161401780458718612)
XLA Ops:
  8.3 345.9 %while.20 = (s32[]{:T(128)}, f32[128,2,512]{2,1,0:T(2,128)}, f32[256,512]{1,0:T(8,128)S(1)}, s32[256]{0:T(256)S(1)}, f32[4,128,512]{2,0,1:T(4,128)}, /*index=5*/...) while((s32[]{:T(128)}, f32[128,2,512]{2,1,0:T(2,128)}, ...), condition=%wide.region_21.22_spmd.clone, body=%wide.region_17.21_spmd.clone.sunk | while | flops 1612679168 | bytes 34888464 | solution.py:126
  12.2 11.5 %all-to-all-start = ((f32[128,1,512]{2,1,0:T(1,128)}), f32[128,1,512]{2,1,0:T(1,128)S(1)}, u32[]{:S(2)}, u32[]{:S(2)}) async-start(f32[128,1,512]{2,1,0:T(1,128)} %copy.180), calls=%async_computation | async-start | bytes 524288 | tf_op jit(solution)/shard_map/while/body/eval_jaxpr/all_to_all | solution.py:34
  26.2 8.3 %all-to-all-done = f32[128,1,512]{2,1,0:T(1,128)S(1)} async-done(((f32[128,1,512]{2,1,0:T(1,128)}), f32[128,1,512]{2,1,0:T(1,128)S(1)}, u32[]{:S(2)}, u32[]{:S(2)}) %all-to-all-start) | async-done | bytes 262176 | tf_op jit(solution)/shard_map/while/body/eval_jaxpr/all_to_all | solution.py:34
  37.1 4.7 %all-to-all-start.1 = ((f32[128,1,512]{2,1,0:T(1,128)}), f32[128,1,512]{2,1,0:T(1,128)S(1)}, u32[]{:S(2)}, u32[]{:S(2)}) async-start(f32[128,1,512]{2,1,0:T(1,128)} %copy.181), calls=%async_computation.1 | async-start | bytes 524288 | tf_op jit(solution)/shard_map/while/body/eval_jaxpr/all_to_all | solution.py:34
  42.1 10.5 %all-to-all-done.1 = f32[128,1,512]{2,1,0:T(1,128)S(1)} async-done(((f32[128,1,512]{2,1,0:T(1,128)}), f32[128,1,512]{2,1,0:T(1,128)S(1)}, u32[]{:S(2)}, u32[]{:S(2)}) %all-to-all-start.1) | async-done | bytes 262176 | tf_op jit(solution)/shard_map/while/body/eval_jaxpr/all_to_all | solution.py:34
  54.7 4.7 %all-to-all-start.2 = ((f32[128,2,512]{2,1,0:T(2,128)}), f32[128,2,512]{2,1,0:T(2,128)S(1)}, u32[]{:S(2)}, u32[]{:S(2)}) async-start(f32[128,2,512]{2,1,0:T(2,128)} %reshape.330), calls=%async_computation.2 | async-start | bytes 1048576 | tf_op jit(solution)/shard_map/while/body/eval_jaxpr/all_to_all | solution.py:34
  59.5 6.1 %gather_fusion = f32[4,512,512]{2,1,0:T(8,128)} fusion(f32[8,512,512]{2,1,0:T(8,128)} %get-tuple-element.669, s32[1024]{0:T(1024)S(1)} %pad_clamp_fusion.4), kind=kCustom, calls=%fused_computation.clone.clone.1 | custom fusion | bytes 8388624 | tf_op jit(solution)/shard_map/while/body/eval_jaxpr/jit(_take)/gather | solution.py:105
  65.8 7.2 %all-to-all-done.2 = f32[128,2,512]{2,1,0:T(2,128)S(1)} async-done(((f32[128,2,512]{2,1,0:T(2,128)}), f32[128,2,512]{2,1,0:T(2,128)S(1)}, u32[]{:S(2)}, u32[]{:S(2)}) %all-to-all-start.2) | async-done | bytes 524320 | tf_op jit(solution)/shard_map/while/body/eval_jaxpr/all_to_all | solution.py:34
  73.4 5.8 %select_reduce_fusion.16 = (f32[512,128]{1,0:T(8,128)S(1)}, f32[512,128]{1,0:T(8,128)S(1)}) fusion(pred[4]{0:T(512)(128)(4,1)S(1)} %get-tuple-element.615, pred[4]{0:T(512)(128)(4,1)S(1)} %get-tuple-element.616, f32[4,512,512]{2,1,0:T(8,128)} %gather_fusion, f32[128,512]{1,0:T(8,128)S(1)} %get-tuple-element.620, ...), kind=kOutput, calls=%fused_computation.8.clone.1 | convolution fusion | flops 806486016 | bytes 5242892 | tf_op jit(solution)/shard_map/while/body/eval_jaxpr/rtb,tbc->rtc/dot_general | solution.py:108
  80.2 4.7 %all-to-all-start.3 = ((f32[128,2,512]{2,1,0:T(2,128)}), f32[128,2,512]{2,1,0:T(2,128)S(1)}, u32[]{:S(2)}, u32[]{:S(2)}) async-start(f32[128,2,512]{2,1,0:T(2,128)} %copy.184), calls=%async_computation.3 | async-start | bytes 1048576 | tf_op jit(solution)/shard_map/while/body/eval_jaxpr/all_to_all | solution.py:34
  85.0 6.1 %dynamic_update_slice.10 = f32[4,128,512]{2,0,1:T(4,128)} dynamic-update-slice(f32[4,128,512]{2,0,1:T(4,128)} %get-tuple-element.647, f32[1,128,512]{2,0,1:T(1,128)S(1)} %bitcast.121, s32[]{:T(128)S(6)} %copy.191, s32[]{:T(128)} %constant.124.clone.1..sunk, s32[]{:T(128)} %constant.124.clone.1..sunk) | dynamic-update-slice | bytes 524292 | tf_op jit(solution)/shard_map/while/body/eval_jaxpr/jit(dynamic_update_index_in_dim)/dynamic_update_slice | solution.py:119
  91.1 7.5 %all-to-all-done.3 = f32[128,2,512]{2,1,0:T(2,128)S(1)} async-done(((f32[128,2,512]{2,1,0:T(2,128)}), f32[128,2,512]{2,1,0:T(2,128)S(1)}, u32[]{:S(2)}, u32[]{:S(2)}) %all-to-all-start.3) | async-done | bytes 524320 | tf_op jit(solution)/shard_map/while/body/eval_jaxpr/all_to_all | solution.py:34
  103.9 4.7 %all-to-all-start = ((f32[128,1,512]{2,1,0:T(1,128)}), f32[128,1,512]{2,1,0:T(1,128)S(1)}, u32[]{:S(2)}, u32[]{:S(2)}) async-start(f32[128,1,512]{2,1,0:T(1,128)} %copy.180), calls=%async_computation | async-start | bytes 524288 | tf_op jit(solution)/shard_map/while/body/eval_jaxpr/all_to_all | solution.py:34
  111.1 8.4 %all-to-all-done = f32[128,1,512]{2,1,0:T(1,128)S(1)} async-done(((f32[128,1,512]{2,1,0:T(1,128)}), f32[128,1,512]{2,1,0:T(1,128)S(1)}, u32[]{:S(2)}, u32[]{:S(2)}) %all-to-all-start) | async-done | bytes 262176 | tf_op jit(solution)/shard_map/while/body/eval_jaxpr/all_to_all | solution.py:34
  122.1 4.7 %all-to-all-start.1 = ((f32[128,1,512]{2,1,0:T(1,128)}), f32[128,1,512]{2,1,0:T(1,128)S(1)}, u32[]{:S(2)}, u32[]{:S(2)}) async-start(f32[128,1,512]{2,1,0:T(1,128)} %copy.181), calls=%async_computation.1 | async-start | bytes 524288 | tf_op jit(solution)/shard_map/while/body/eval_jaxpr/all_to_all | solution.py:34
  127.1 10.5 %all-to-all-done.1 = f32[128,1,512]{2,1,0:T(1,128)S(1)} async-done(((f32[128,1,512]{2,1,0:T(1,128)}), f32[128,1,512]{2,1,0:T(1,128)S(1)}, u32[]{:S(2)}, u32[]{:S(2)}) %all-to-all-start.1) | async-done | bytes 262176 | tf_op jit(solution)/shard_map/while/body/eval_jaxpr/all_to_all | solution.py:34
  139.7 4.7 %all-to-all-start.2 = ((f32[128,2,512]{2,1,0:T(2,128)}), f32[128,2,512]{2,1,0:T(2,128)S(1)}, u32[]{:S(2)}, u32[]{:S(2)}) async-start(f32[128,2,512]{2,1,0:T(2,128)} %reshape.330), calls=%async_computation.2 | async-start | bytes 1048576 | tf_op jit(solution)/shard_map/while/body/eval_jaxpr/all_to_all | solution.py:34
  144.5 6.1 %gather_fusion = f32[4,512,512]{2,1,0:T(8,128)} fusion(f32[8,512,512]{2,1,0:T(8,128)} %get-tuple-element.669, s32[1024]{0:T(1024)S(1)} %pad_clamp_fusion.4), kind=kCustom, calls=%fused_computation.clone.clone.1 | custom fusion | bytes 8388624 | tf_op jit(solution)/shard_map/while/body/eval_jaxpr/jit(_take)/gather | solution.py:105
  150.8 7.2 %all-to-all-done.2 = f32[128,2,512]{2,1,0:T(2,128)S(1)} async-done(((f32[128,2,512]{2,1,0:T(2,128)}), f32[128,2,512]{2,1,0:T(2,128)S(1)}, u32[]{:S(2)}, u32[]{:S(2)}) %all-to-all-start.2) | async-done | bytes 524320 | tf_op jit(solution)/shard_map/while/body/eval_jaxpr/all_to_all | solution.py:34
  158.5 5.8 %select_reduce_fusion.16 = (f32[512,128]{1,0:T(8,128)S(1)}, f32[512,128]{1,0:T(8,128)S(1)}) fusion(pred[4]{0:T(512)(128)(4,1)S(1)} %get-tuple-element.615, pred[4]{0:T(512)(128)(4,1)S(1)} %get-tuple-element.616, f32[4,512,512]{2,1,0:T(8,128)} %gather_fusion, f32[128,512]{1,0:T(8,128)S(1)} %get-tuple-element.620, ...), kind=kOutput, calls=%fused_computation.8.clone.1 | convolution fusion | flops 806486016 | bytes 5242892 | tf_op jit(solution)/shard_map/while/body/eval_jaxpr/rtb,tbc->rtc/dot_general | solution.py:108
  165.3 4.7 %all-to-all-start.3 = ((f32[128,2,512]{2,1,0:T(2,128)}), f32[128,2,512]{2,1,0:T(2,128)S(1)}, u32[]{:S(2)}, u32[]{:S(2)}) async-start(f32[128,2,512]{2,1,0:T(2,128)} %copy.184), calls=%async_computation.3 | async-start | bytes 1048576 | tf_op jit(solution)/shard_map/while/body/eval_jaxpr/all_to_all | solution.py:34
  170.0 6.1 %dynamic_update_slice.10 = f32[4,128,512]{2,0,1:T(4,128)} dynamic-update-slice(f32[4,128,512]{2,0,1:T(4,128)} %get-tuple-element.647, f32[1,128,512]{2,0,1:T(1,128)S(1)} %bitcast.121, s32[]{:T(128)S(6)} %copy.191, s32[]{:T(128)} %constant.124.clone.1..sunk, s32[]{:T(128)} %constant.124.clone.1..sunk) | dynamic-update-slice | bytes 524292 | tf_op jit(solution)/shard_map/while/body/eval_jaxpr/jit(dynamic_update_index_in_dim)/dynamic_update_slice | solution.py:119
  176.1 7.5 %all-to-all-done.3 = f32[128,2,512]{2,1,0:T(2,128)S(1)} async-done(((f32[128,2,512]{2,1,0:T(2,128)}), f32[128,2,512]{2,1,0:T(2,128)S(1)}, u32[]{:S(2)}, u32[]{:S(2)}) %all-to-all-start.3) | async-done | bytes 524320 | tf_op jit(solution)/shard_map/while/body/eval_jaxpr/all_to_all | solution.py:34
  188.9 4.7 %all-to-all-start = ((f32[128,1,512]{2,1,0:T(1,128)}), f32[128,1,512]{2,1,0:T(1,128)S(1)}, u32[]{:S(2)}, u32[]{:S(2)}) async-start(f32[128,1,512]{2,1,0:T(1,128)} %copy.180), calls=%async_computation | async-start | bytes 524288 | tf_op jit(solution)/shard_map/while/body/eval_jaxpr/all_to_all | solution.py:34
  196.1 8.4 %all-to-all-done = f32[128,1,512]{2,1,0:T(1,128)S(1)} async-done(((f32[128,1,512]{2,1,0:T(1,128)}), f32[128,1,512]{2,1,0:T(1,128)S(1)}, u32[]{:S(2)}, u32[]{:S(2)}) %all-to-all-start) | async-done | bytes 262176 | tf_op jit(solution)/shard_map/while/body/eval_jaxpr/all_to_all | solution.py:34
  207.1 4.7 %all-to-all-start.1 = ((f32[128,1,512]{2,1,0:T(1,128)}), f32[128,1,512]{2,1,0:T(1,128)S(1)}, u32[]{:S(2)}, u32[]{:S(2)}) async-start(f32[128,1,512]{2,1,0:T(1,128)} %copy.181), calls=%async_computation.1 | async-start | bytes 524288 | tf_op jit(solution)/shard_map/while/body/eval_jaxpr/all_to_all | solution.py:34
  212.1 10.5 %all-to-all-done.1 = f32[128,1,512]{2,1,0:T(1,128)S(1)} async-done(((f32[128,1,512]{2,1,0:T(1,128)}), f32[128,1,512]{2,1,0:T(1,128)S(1)}, u32[]{:S(2)}, u32[]{:S(2)}) %all-to-all-start.1) | async-done | bytes 262176 | tf_op jit(solution)/shard_map/while/body/eval_jaxpr/all_to_all | solution.py:34
  224.7 4.7 %all-to-all-start.2 = ((f32[128,2,512]{2,1,0:T(2,128)}), f32[128,2,512]{2,1,0:T(2,128)S(1)}, u32[]{:S(2)}, u32[]{:S(2)}) async-start(f32[128,2,512]{2,1,0:T(2,128)} %reshape.330), calls=%async_computation.2 | async-start | bytes 1048576 | tf_op jit(solution)/shard_map/while/body/eval_jaxpr/all_to_all | solution.py:34
  229.5 6.1 %gather_fusion = f32[4,512,512]{2,1,0:T(8,128)} fusion(f32[8,512,512]{2,1,0:T(8,128)} %get-tuple-element.669, s32[1024]{0:T(1024)S(1)} %pad_clamp_fusion.4), kind=kCustom, calls=%fused_computation.clone.clone.1 | custom fusion | bytes 8388624 | tf_op jit(solution)/shard_map/while/body/eval_jaxpr/jit(_take)/gather | solution.py:105
  235.8 7.2 %all-to-all-done.2 = f32[128,2,512]{2,1,0:T(2,128)S(1)} async-done(((f32[128,2,512]{2,1,0:T(2,128)}), f32[128,2,512]{2,1,0:T(2,128)S(1)}, u32[]{:S(2)}, u32[]{:S(2)}) %all-to-all-start.2) | async-done | bytes 524320 | tf_op jit(solution)/shard_map/while/body/eval_jaxpr/all_to_all | solution.py:34
  243.5 5.8 %select_reduce_fusion.16 = (f32[512,128]{1,0:T(8,128)S(1)}, f32[512,128]{1,0:T(8,128)S(1)}) fusion(pred[4]{0:T(512)(128)(4,1)S(1)} %get-tuple-element.615, pred[4]{0:T(512)(128)(4,1)S(1)} %get-tuple-element.616, f32[4,512,512]{2,1,0:T(8,128)} %gather_fusion, f32[128,512]{1,0:T(8,128)S(1)} %get-tuple-element.620, ...), kind=kOutput, calls=%fused_computation.8.clone.1 | convolution fusion | flops 806486016 | bytes 5242892 | tf_op jit(solution)/shard_map/while/body/eval_jaxpr/rtb,tbc->rtc/dot_general | solution.py:108
  250.3 4.7 %all-to-all-start.3 = ((f32[128,2,512]{2,1,0:T(2,128)}), f32[128,2,512]{2,1,0:T(2,128)S(1)}, u32[]{:S(2)}, u32[]{:S(2)}) async-start(f32[128,2,512]{2,1,0:T(2,128)} %copy.184), calls=%async_computation.3 | async-start | bytes 1048576 | tf_op jit(solution)/shard_map/while/body/eval_jaxpr/all_to_all | solution.py:34
  255.0 6.1 %dynamic_update_slice.10 = f32[4,128,512]{2,0,1:T(4,128)} dynamic-update-slice(f32[4,128,512]{2,0,1:T(4,128)} %get-tuple-element.647, f32[1,128,512]{2,0,1:T(1,128)S(1)} %bitcast.121, s32[]{:T(128)S(6)} %copy.191, s32[]{:T(128)} %constant.124.clone.1..sunk, s32[]{:T(128)} %constant.124.clone.1..sunk) | dynamic-update-slice | bytes 524292 | tf_op jit(solution)/shard_map/while/body/eval_jaxpr/jit(dynamic_update_index_in_dim)/dynamic_update_slice | solution.py:119
  261.1 7.5 %all-to-all-done.3 = f32[128,2,512]{2,1,0:T(2,128)S(1)} async-done(((f32[128,2,512]{2,1,0:T(2,128)}), f32[128,2,512]{2,1,0:T(2,128)S(1)}, u32[]{:S(2)}, u32[]{:S(2)}) %all-to-all-start.3) | async-done | bytes 524320 | tf_op jit(solution)/shard_map/while/body/eval_jaxpr/all_to_all | solution.py:34
  273.9 4.7 %all-to-all-start = ((f32[128,1,512]{2,1,0:T(1,128)}), f32[128,1,512]{2,1,0:T(1,128)S(1)}, u32[]{:S(2)}, u32[]{:S(2)}) async-start(f32[128,1,512]{2,1,0:T(1,128)} %copy.180), calls=%async_computation | async-start | bytes 524288 | tf_op jit(solution)/shard_map/while/body/eval_jaxpr/all_to_all | solution.py:34
  281.1 8.4 %all-to-all-done = f32[128,1,512]{2,1,0:T(1,128)S(1)} async-done(((f32[128,1,512]{2,1,0:T(1,128)}), f32[128,1,512]{2,1,0:T(1,128)S(1)}, u32[]{:S(2)}, u32[]{:S(2)}) %all-to-all-start) | async-done | bytes 262176 | tf_op jit(solution)/shard_map/while/body/eval_jaxpr/all_to_all | solution.py:34
  292.1 4.7 %all-to-all-start.1 = ((f32[128,1,512]{2,1,0:T(1,128)}), f32[128,1,512]{2,1,0:T(1,128)S(1)}, u32[]{:S(2)}, u32[]{:S(2)}) async-start(f32[128,1,512]{2,1,0:T(1,128)} %copy.181), calls=%async_computation.1 | async-start | bytes 524288 | tf_op jit(solution)/shard_map/while/body/eval_jaxpr/all_to_all | solution.py:34
  297.1 10.5 %all-to-all-done.1 = f32[128,1,512]{2,1,0:T(1,128)S(1)} async-done(((f32[128,1,512]{2,1,0:T(1,128)}), f32[128,1,512]{2,1,0:T(1,128)S(1)}, u32[]{:S(2)}, u32[]{:S(2)}) %all-to-all-start.1) | async-done | bytes 262176 | tf_op jit(solution)/shard_map/while/body/eval_jaxpr/all_to_all | solution.py:34
  314.5 6.1 %gather_fusion = f32[4,512,512]{2,1,0:T(8,128)} fusion(f32[8,512,512]{2,1,0:T(8,128)} %get-tuple-element.669, s32[1024]{0:T(1024)S(1)} %pad_clamp_fusion.4), kind=kCustom, calls=%fused_computation.clone.clone.1 | custom fusion | bytes 8388624 | tf_op jit(solution)/shard_map/while/body/eval_jaxpr/jit(_take)/gather | solution.py:105
  320.8 7.2 %all-to-all-done.2 = f32[128,2,512]{2,1,0:T(2,128)S(1)} async-done(((f32[128,2,512]{2,1,0:T(2,128)}), f32[128,2,512]{2,1,0:T(2,128)S(1)}, u32[]{:S(2)}, u32[]{:S(2)}) %all-to-all-start.2) | async-done | bytes 524320 | tf_op jit(solution)/shard_map/while/body/eval_jaxpr/all_to_all | solution.py:34
  328.5 5.8 %select_reduce_fusion.16 = (f32[512,128]{1,0:T(8,128)S(1)}, f32[512,128]{1,0:T(8,128)S(1)}) fusion(pred[4]{0:T(512)(128)(4,1)S(1)} %get-tuple-element.615, pred[4]{0:T(512)(128)(4,1)S(1)} %get-tuple-element.616, f32[4,512,512]{2,1,0:T(8,128)} %gather_fusion, f32[128,512]{1,0:T(8,128)S(1)} %get-tuple-element.620, ...), kind=kOutput, calls=%fused_computation.8.clone.1 | convolution fusion | flops 806486016 | bytes 5242892 | tf_op jit(solution)/shard_map/while/body/eval_jaxpr/rtb,tbc->rtc/dot_general | solution.py:108
  335.3 4.7 %all-to-all-start.3 = ((f32[128,2,512]{2,1,0:T(2,128)}), f32[128,2,512]{2,1,0:T(2,128)S(1)}, u32[]{:S(2)}, u32[]{:S(2)}) async-start(f32[128,2,512]{2,1,0:T(2,128)} %copy.184), calls=%async_computation.3 | async-start | bytes 1048576 | tf_op jit(solution)/shard_map/while/body/eval_jaxpr/all_to_all | solution.py:34
  340.0 6.1 %dynamic_update_slice.10 = f32[4,128,512]{2,0,1:T(4,128)} dynamic-update-slice(f32[4,128,512]{2,0,1:T(4,128)} %get-tuple-element.647, f32[1,128,512]{2,0,1:T(1,128)S(1)} %bitcast.121, s32[]{:T(128)S(6)} %copy.191, s32[]{:T(128)} %constant.124.clone.1..sunk, s32[]{:T(128)} %constant.124.clone.1..sunk) | dynamic-update-slice | bytes 524292 | tf_op jit(solution)/shard_map/while/body/eval_jaxpr/jit(dynamic_update_index_in_dim)/dynamic_update_slice | solution.py:119
  346.1 7.5 %all-to-all-done.3 = f32[128,2,512]{2,1,0:T(2,128)S(1)} async-done(((f32[128,2,512]{2,1,0:T(2,128)}), f32[128,2,512]{2,1,0:T(2,128)S(1)}, u32[]{:S(2)}, u32[]{:S(2)}) %all-to-all-start.3) | async-done | bytes 524320 | tf_op jit(solution)/shard_map/while/body/eval_jaxpr/all_to_all | solution.py:34
  357.5 4.7 %all-to-all-start.4 = ((f32[128,1,512]{2,1,0:T(1,128)}), f32[128,1,512]{2,1,0:T(1,128)S(1)}, u32[]{:S(2)}, u32[]{:S(2)}) async-start(f32[128,1,512]{2,1,0:T(1,128)} %copy.129), calls=%async_computation.4 | async-start | bytes 524288 | tf_op jit(solution)/shard_map/all_to_all | solution.py:34
  365.6 7.5 %all-to-all-done.4 = f32[128,1,512]{2,1,0:T(1,128)S(1)} async-done(((f32[128,1,512]{2,1,0:T(1,128)}), f32[128,1,512]{2,1,0:T(1,128)S(1)}, u32[]{:S(2)}, u32[]{:S(2)}) %all-to-all-start.4) | async-done | bytes 262176 | tf_op jit(solution)/shard_map/all_to_all | solution.py:34
  374.5 4.7 %all-to-all-start.5 = ((f32[128,1,512]{2,1,0:T(1,128)}), f32[128,1,512]{2,1,0:T(1,128)S(1)}, u32[]{:S(2)}, u32[]{:S(2)}) async-start(f32[128,1,512]{2,1,0:T(1,128)} %copy.130), calls=%async_computation.5 | async-start | bytes 524288 | tf_op jit(solution)/shard_map/all_to_all | solution.py:34
  385.1 4.9 %all-to-all-done.5 = f32[128,1,512]{2,1,0:T(1,128)S(1)} async-done(((f32[128,1,512]{2,1,0:T(1,128)}), f32[128,1,512]{2,1,0:T(1,128)S(1)}, u32[]{:S(2)}, u32[]{:S(2)}) %all-to-all-start.5) | async-done | bytes 262176 | tf_op jit(solution)/shard_map/all_to_all | solution.py:34
  (191 shorter events, 75.1 us)
Async XLA Ops:
  12.2 22.3 %all-to-all-start = ((f32[128,1,512]{2,1,0:T(1,128)}), f32[128,1,512]{2,1,0:T(1,128)S(1)}, u32[]{:S(2)}, u32[]{:S(2)}) async-start(f32[128,1,512]{2,1,0:T(1,128)} %copy.180), calls=%async_computation | async-start | bytes 524288 | tf_op jit(solution)/shard_map/while/body/eval_jaxpr/all_to_all | solution.py:34
  37.1 15.5 %all-to-all-start.1 = ((f32[128,1,512]{2,1,0:T(1,128)}), f32[128,1,512]{2,1,0:T(1,128)S(1)}, u32[]{:S(2)}, u32[]{:S(2)}) async-start(f32[128,1,512]{2,1,0:T(1,128)} %copy.181), calls=%async_computation.1 | async-start | bytes 524288 | tf_op jit(solution)/shard_map/while/body/eval_jaxpr/all_to_all | solution.py:34
  54.7 18.3 %all-to-all-start.2 = ((f32[128,2,512]{2,1,0:T(2,128)}), f32[128,2,512]{2,1,0:T(2,128)S(1)}, u32[]{:S(2)}, u32[]{:S(2)}) async-start(f32[128,2,512]{2,1,0:T(2,128)} %reshape.330), calls=%async_computation.2 | async-start | bytes 1048576 | tf_op jit(solution)/shard_map/while/body/eval_jaxpr/all_to_all | solution.py:34
  80.2 18.4 %all-to-all-start.3 = ((f32[128,2,512]{2,1,0:T(2,128)}), f32[128,2,512]{2,1,0:T(2,128)S(1)}, u32[]{:S(2)}, u32[]{:S(2)}) async-start(f32[128,2,512]{2,1,0:T(2,128)} %copy.184), calls=%async_computation.3 | async-start | bytes 1048576 | tf_op jit(solution)/shard_map/while/body/eval_jaxpr/all_to_all | solution.py:34
  103.9 15.6 %all-to-all-start = ((f32[128,1,512]{2,1,0:T(1,128)}), f32[128,1,512]{2,1,0:T(1,128)S(1)}, u32[]{:S(2)}, u32[]{:S(2)}) async-start(f32[128,1,512]{2,1,0:T(1,128)} %copy.180), calls=%async_computation | async-start | bytes 524288 | tf_op jit(solution)/shard_map/while/body/eval_jaxpr/all_to_all | solution.py:34
  122.1 15.5 %all-to-all-start.1 = ((f32[128,1,512]{2,1,0:T(1,128)}), f32[128,1,512]{2,1,0:T(1,128)S(1)}, u32[]{:S(2)}, u32[]{:S(2)}) async-start(f32[128,1,512]{2,1,0:T(1,128)} %copy.181), calls=%async_computation.1 | async-start | bytes 524288 | tf_op jit(solution)/shard_map/while/body/eval_jaxpr/all_to_all | solution.py:34
  139.7 18.3 %all-to-all-start.2 = ((f32[128,2,512]{2,1,0:T(2,128)}), f32[128,2,512]{2,1,0:T(2,128)S(1)}, u32[]{:S(2)}, u32[]{:S(2)}) async-start(f32[128,2,512]{2,1,0:T(2,128)} %reshape.330), calls=%async_computation.2 | async-start | bytes 1048576 | tf_op jit(solution)/shard_map/while/body/eval_jaxpr/all_to_all | solution.py:34
  165.3 18.4 %all-to-all-start.3 = ((f32[128,2,512]{2,1,0:T(2,128)}), f32[128,2,512]{2,1,0:T(2,128)S(1)}, u32[]{:S(2)}, u32[]{:S(2)}) async-start(f32[128,2,512]{2,1,0:T(2,128)} %copy.184), calls=%async_computation.3 | async-start | bytes 1048576 | tf_op jit(solution)/shard_map/while/body/eval_jaxpr/all_to_all | solution.py:34
  188.9 15.6 %all-to-all-start = ((f32[128,1,512]{2,1,0:T(1,128)}), f32[128,1,512]{2,1,0:T(1,128)S(1)}, u32[]{:S(2)}, u32[]{:S(2)}) async-start(f32[128,1,512]{2,1,0:T(1,128)} %copy.180), calls=%async_computation | async-start | bytes 524288 | tf_op jit(solution)/shard_map/while/body/eval_jaxpr/all_to_all | solution.py:34
  207.1 15.5 %all-to-all-start.1 = ((f32[128,1,512]{2,1,0:T(1,128)}), f32[128,1,512]{2,1,0:T(1,128)S(1)}, u32[]{:S(2)}, u32[]{:S(2)}) async-start(f32[128,1,512]{2,1,0:T(1,128)} %copy.181), calls=%async_computation.1 | async-start | bytes 524288 | tf_op jit(solution)/shard_map/while/body/eval_jaxpr/all_to_all | solution.py:34
  224.7 18.3 %all-to-all-start.2 = ((f32[128,2,512]{2,1,0:T(2,128)}), f32[128,2,512]{2,1,0:T(2,128)S(1)}, u32[]{:S(2)}, u32[]{:S(2)}) async-start(f32[128,2,512]{2,1,0:T(2,128)} %reshape.330), calls=%async_computation.2 | async-start | bytes 1048576 | tf_op jit(solution)/shard_map/while/body/eval_jaxpr/all_to_all | solution.py:34
  250.3 18.4 %all-to-all-start.3 = ((f32[128,2,512]{2,1,0:T(2,128)}), f32[128,2,512]{2,1,0:T(2,128)S(1)}, u32[]{:S(2)}, u32[]{:S(2)}) async-start(f32[128,2,512]{2,1,0:T(2,128)} %copy.184), calls=%async_computation.3 | async-start | bytes 1048576 | tf_op jit(solution)/shard_map/while/body/eval_jaxpr/all_to_all | solution.py:34
  273.9 15.6 %all-to-all-start = ((f32[128,1,512]{2,1,0:T(1,128)}), f32[128,1,512]{2,1,0:T(1,128)S(1)}, u32[]{:S(2)}, u32[]{:S(2)}) async-start(f32[128,1,512]{2,1,0:T(1,128)} %copy.180), calls=%async_computation | async-start | bytes 524288 | tf_op jit(solution)/shard_map/while/body/eval_jaxpr/all_to_all | solution.py:34
  292.1 15.5 %all-to-all-start.1 = ((f32[128,1,512]{2,1,0:T(1,128)}), f32[128,1,512]{2,1,0:T(1,128)S(1)}, u32[]{:S(2)}, u32[]{:S(2)}) async-start(f32[128,1,512]{2,1,0:T(1,128)} %copy.181), calls=%async_computation.1 | async-start | bytes 524288 | tf_op jit(solution)/shard_map/while/body/eval_jaxpr/all_to_all | solution.py:34
  309.8 18.3 %all-to-all-start.2 = ((f32[128,2,512]{2,1,0:T(2,128)}), f32[128,2,512]{2,1,0:T(2,128)S(1)}, u32[]{:S(2)}, u32[]{:S(2)}) async-start(f32[128,2,512]{2,1,0:T(2,128)} %reshape.330), calls=%async_computation.2 | async-start | bytes 1048576 | tf_op jit(solution)/shard_map/while/body/eval_jaxpr/all_to_all | solution.py:34
  335.3 18.4 %all-to-all-start.3 = ((f32[128,2,512]{2,1,0:T(2,128)}), f32[128,2,512]{2,1,0:T(2,128)S(1)}, u32[]{:S(2)}, u32[]{:S(2)}) async-start(f32[128,2,512]{2,1,0:T(2,128)} %copy.184), calls=%async_computation.3 | async-start | bytes 1048576 | tf_op jit(solution)/shard_map/while/body/eval_jaxpr/all_to_all | solution.py:34
  354.2 18.9 %copy-start = (f32[2,512,512]{2,1,0:T(8,128)S(1)}, f32[2,512,512]{2,1,0:T(8,128)}, u32[]{:S(2)}) copy-start(f32[2,512,512]{2,1,0:T(8,128)} %get-tuple-element.686) | copy-start | bytes 6291460
  357.5 15.6 %all-to-all-start.4 = ((f32[128,1,512]{2,1,0:T(1,128)}), f32[128,1,512]{2,1,0:T(1,128)S(1)}, u32[]{:S(2)}, u32[]{:S(2)}) async-start(f32[128,1,512]{2,1,0:T(1,128)} %copy.129), calls=%async_computation.4 | async-start | bytes 524288 | tf_op jit(solution)/shard_map/all_to_all | solution.py:34
  374.5 15.5 %all-to-all-start.5 = ((f32[128,1,512]{2,1,0:T(1,128)}), f32[128,1,512]{2,1,0:T(1,128)S(1)}, u32[]{:S(2)}, u32[]{:S(2)}) async-start(f32[128,1,512]{2,1,0:T(1,128)} %copy.130), calls=%async_computation.5 | async-start | bytes 524288 | tf_op jit(solution)/shard_map/all_to_all | solution.py:34

commit v2 on v0

--- a/solution.py
+++ b/solution.py
@@ -114,23 +114,19 @@
 
     residue, update = residual(0, update, None, None)
     first = solve(0, residue)
-    coming, coming_targets = tiles(0, first)
+    kept = jnp.zeros((LEVELS, devices, block), jnp.float32)
+    kept = lax.dynamic_update_index_in_dim(kept, first, 0, 0)
 
-    def middle(current, carry):
-        update, coming, coming_targets, kept = carry
-        residue, update = residual(current, update, coming, coming_targets)
-        returned = solve(current, residue)
-        kept = lax.dynamic_update_index_in_dim(kept, returned, current - 1, 0)
+    def step(current, carry):
+        update, returned, kept = carry
         coming, coming_targets = tiles(current, returned)
-        return update, coming, coming_targets, kept
+        residue, update = residual(current + 1, update, coming, coming_targets)
+        returned = solve(current + 1, residue)
+        kept = lax.dynamic_update_index_in_dim(kept, returned, current + 1, 0)
+        return update, returned, kept
 
-    kept = jnp.zeros((tile_levels - 1, devices, block), jnp.float32)
-    update, coming, coming_targets, kept = lax.fori_loop(
-        1, tile_levels, middle, (update, coming, coming_targets, kept))
-    residue, _ = residual(LEVELS - 1, update, coming, coming_targets)
-    last = solve(LEVELS - 1, residue)
-
-    solved_rows = [first] + [kept[i] for i in range(tile_levels - 1)] + [last]
+    update, _, kept = lax.fori_loop(0, tile_levels, step, (update, first, kept))
+    solved_rows = [kept[i] for i in range(LEVELS)]
     solution = solved_rows[0][:, None, :]
     for current in range(1, LEVELS):
         solution = jnp.where(owner_at[current][:, :, None], solved_rows[current][:, None, :], solution)

time: 390 us -> 415 us (1.064)
  waiting for transfers between devices: 154 us -> 174 us
  local copies, waits for them, and re-layouts: 85 us -> 98.3 us
  other arithmetic: 14.1 us -> 5.06 us
  between operations: 4.68 us -> 0.45 us
    all_to_all x18, waiting for transfers between devices: 154 us -> 174 us  [a2a(): return lax.all_to_all(x, 'dev', split_axis=0, concat_axis=0, tiled=True)]
    reduce_sum x5, other arithmetic: 10 us -> 1.21 us  [residual(): jnp.sum(jnp.where(at_level(owner_at, current)[:, :, None], rhs - update,...]
    dynamic_update_slice x3 -> x5, local copies, waits for them, and re-layouts: 18.3 us -> 26.8 us  [the longest x4 25.2 us: step(): kept = lax.dynamic_update_index_in_dim(kept, returned, current + 1, 0)]
  transfers between devices with their start and end apart: 18 -> 18, of which waited for: 18 -> 18; matrix products, arithmetic and copies ran while one was open for 14% -> 8% of each run, Pallas kernels for 0% -> 0%
where the time goes in v2:
time: 415 us; the launch traced here: 413 us
  waiting for transfers between devices  174 us (42%)
  local copies, waits for them, and re-layouts  98.3 us (24%)
  starting transfers between devices  91.5 us (22%)
  matrix products  33.6 us (8%)
  loops' own time  9.65 us (2%)
  other arithmetic  5.06 us (1%)
    all_to_all x18, waiting for transfers between devices, a2a(): return lax.all_to_all(x, 'dev', split_axis=0, concat_axis=0, tiled=True)  174 us
    all_to_all x18, starting transfers between devices, a2a(): return lax.all_to_all(x, 'dev', split_axis=0, concat_axis=0, tiled=True)  91.5 us
    dynamic_update_slice x4, local copies, waits for them, and re-layouts, step(): kept = lax.dynamic_update_index_in_dim(kept, returned, current + 1, 0)  25.2 us
    gather x4, local copies, waits for them, and re-layouts, tiles(): jnp.take(factor_tiles, at_level(slot_tile, current), axis=0, mode='clip')  24.5 us
    dot_general x4, matrix products, tiles(): jnp.einsum('rtb,tbc->rtc', sources, factors, precision=product_precision,...  23 us
    another operation x1, loops' own time, per_device(): update, _, kept = lax.fori_loop(0, tile_levels, step, (update, first, kept))  9.65 us
    all_to_all x10, local copies, waits for them, and re-layouts, a2a(): return lax.all_to_all(x, 'dev', split_axis=0, concat_axis=0, tiled=True)  9.64 us
  transfers between devices with their start and end apart: 18, of which 18 were waited for; matrix products, arithmetic and copies ran while one was open for 8% of the time, Pallas kernels for 0%

profile of v2, /device:TPU:1, one launch (start us, length us, event | category | flops | bytes accessed | tf_op | source)
XLA Modules:
  0.0 413.0 jit_solution(11753035888533247567)
XLA Ops:
  9.7 11.5 %all-to-all-start.4 = ((f32[128,1,512]{2,1,0:T(1,128)}), f32[128,1,512]{2,1,0:T(1,128)S(1)}, u32[]{:S(2)}, u32[]{:S(2)}) async-start(f32[128,1,512]{2,1,0:T(1,128)} %all_to_all.66), calls=%async_computation.4 | async-start | bytes 524288 | tf_op jit(solution)/shard_map/all_to_all | solution.py:34
  21.4 10.6 %all-to-all-done.4 = f32[128,1,512]{2,1,0:T(1,128)S(1)} async-done(((f32[128,1,512]{2,1,0:T(1,128)}), f32[128,1,512]{2,1,0:T(1,128)S(1)}, u32[]{:S(2)}, u32[]{:S(2)}) %all-to-all-start.4) | async-done | bytes 262176 | tf_op jit(solution)/shard_map/all_to_all | solution.py:34
  33.4 4.7 %all-to-all-start.5 = ((f32[128,1,512]{2,1,0:T(1,128)}), f32[128,1,512]{2,1,0:T(1,128)S(1)}, u32[]{:S(2)}, u32[]{:S(2)}) async-start(f32[128,1,512]{2,1,0:T(1,128)} %copy.125), calls=%async_computation.5 | async-start | bytes 524288 | tf_op jit(solution)/shard_map/all_to_all | solution.py:34
  39.7 9.3 %all-to-all-done.5 = f32[128,1,512]{2,1,0:T(1,128)S(1)} async-done(((f32[128,1,512]{2,1,0:T(1,128)}), f32[128,1,512]{2,1,0:T(1,128)S(1)}, u32[]{:S(2)}, u32[]{:S(2)}) %all-to-all-start.5) | async-done | bytes 262176 | tf_op jit(solution)/shard_map/all_to_all | solution.py:34
  50.6 352.6 %while.20 = (s32[]{:T(128)}, f32[128,2,512]{2,0,1:T(8,128)S(1)}, f32[128,512]{1,0:T(8,128)S(1)}, f32[5,128,512]{2,0,1:T(8,128)}, s32[4,256]{1,0:T(4,128)S(1)}, /...) while((s32[]{:T(128)}, f32[128,2,512]{2,0,1:T(8,128)S(1)}, ...), condition=%wide.region_22.23_spmd.clone, body=%wide.region_18.22_spmd.clone.sunk | while | flops 1612810752 | bytes 34368300 | solution.py:128
  53.1 4.7 %all-to-all-start = ((f32[128,2,512]{2,1,0:T(2,128)}), f32[128,2,512]{2,1,0:T(2,128)S(1)}, u32[]{:S(2)}, u32[]{:S(2)}) async-start(f32[128,2,512]{2,1,0:T(2,128)} %reshape.374), calls=%async_computation | async-start | bytes 1048576 | tf_op jit(solution)/shard_map/while/body/eval_jaxpr/all_to_all | solution.py:34
  57.9 6.1 %gather_fusion = f32[4,512,512]{2,1,0:T(8,128)} fusion(f32[8,512,512]{2,1,0:T(8,128)} %get-tuple-element.727, s32[1024]{0:T(1024)S(1)} %pad_clamp_fusion.4), kind=kCustom, calls=%fused_computation.clone.clone.1 | custom fusion | bytes 8388624 | tf_op jit(solution)/shard_map/while/body/eval_jaxpr/jit(_take)/gather | solution.py:105
  64.2 7.2 %all-to-all-done = f32[128,2,512]{2,1,0:T(2,128)S(1)} async-done(((f32[128,2,512]{2,1,0:T(2,128)}), f32[128,2,512]{2,1,0:T(2,128)S(1)}, u32[]{:S(2)}, u32[]{:S(2)}) %all-to-all-start) | async-done | bytes 524320 | tf_op jit(solution)/shard_map/while/body/eval_jaxpr/all_to_all | solution.py:34
  71.9 5.8 %select_reduce_fusion.15 = (f32[512,128]{1,0:T(8,128)S(1)}, f32[512,128]{1,0:T(8,128)S(1)}) fusion(pred[4]{0:T(512)(128)(4,1)S(1)} %get-tuple-element.674, pred[4]{0:T(512)(128)(4,1)S(1)} %get-tuple-element.675, f32[4,512,512]{2,1,0:T(8,128)} %gather_fusion, f32[128,512]{1,0:T(8,128)S(1)} %get-tuple-element.678, ...), kind=kOutput, calls=%fused_computation.10.clone.1 | convolution fusion | flops 806486016 | bytes 5242892 | tf_op jit(solution)/shard_map/while/body/eval_jaxpr/rtb,tbc->rtc/dot_general | solution.py:108
  78.7 4.7 %all-to-all-start.1 = ((f32[128,2,512]{2,1,0:T(2,128)}), f32[128,2,512]{2,1,0:T(2,128)S(1)}, u32[]{:S(2)}, u32[]{:S(2)}) async-start(f32[128,2,512]{2,1,0:T(2,128)} %copy.204), calls=%async_computation.1 | async-start | bytes 1048576 | tf_op jit(solution)/shard_map/while/body/eval_jaxpr/all_to_all | solution.py:34
  83.6 13.5 %all-to-all-done.1 = f32[128,2,512]{2,1,0:T(2,128)S(1)} async-done(((f32[128,2,512]{2,1,0:T(2,128)}), f32[128,2,512]{2,1,0:T(2,128)S(1)}, u32[]{:S(2)}, u32[]{:S(2)}) %all-to-all-start.1) | async-done | bytes 524320 | tf_op jit(solution)/shard_map/while/body/eval_jaxpr/all_to_all | solution.py:34
  98.7 4.7 %all-to-all-start.2 = ((f32[128,1,512]{2,1,0:T(1,128)}), f32[128,1,512]{2,1,0:T(1,128)S(1)}, u32[]{:S(2)}, u32[]{:S(2)}) async-start(f32[128,1,512]{2,1,0:T(1,128)} %copy.206), calls=%async_computation.2 | async-start | bytes 524288 | tf_op jit(solution)/shard_map/while/body/eval_jaxpr/all_to_all | solution.py:34
  106.7 7.7 %all-to-all-done.2 = f32[128,1,512]{2,1,0:T(1,128)S(1)} async-done(((f32[128,1,512]{2,1,0:T(1,128)}), f32[128,1,512]{2,1,0:T(1,128)S(1)}, u32[]{:S(2)}, u32[]{:S(2)}) %all-to-all-start.2) | async-done | bytes 262176 | tf_op jit(solution)/shard_map/while/body/eval_jaxpr/all_to_all | solution.py:34
  122.3 10.2 %all-to-all-done.3 = f32[128,1,512]{2,1,0:T(1,128)S(1)} async-done(((f32[128,1,512]{2,1,0:T(1,128)}), f32[128,1,512]{2,1,0:T(1,128)S(1)}, u32[]{:S(2)}, u32[]{:S(2)}) %all-to-all-start.3) | async-done | bytes 262176 | tf_op jit(solution)/shard_map/while/body/eval_jaxpr/all_to_all | solution.py:34
  132.5 6.3 %dynamic_update_slice.18 = f32[5,128,512]{2,0,1:T(8,128)} dynamic-update-slice(f32[5,128,512]{2,0,1:T(8,128)} %get-tuple-element.704, f32[1,128,512]{2,0,1:T(1,128)S(1)} %bitcast.122, s32[]{:T(128)S(6)} %select_n.265, s32[]{:T(128)} %constant.148.clone.1..sunk, s32[]{:T(128)} %constant.148.clone.1..sunk) | dynamic-update-slice | bytes 524292 | tf_op jit(solution)/shard_map/while/body/eval_jaxpr/jit(dynamic_update_index_in_dim)/dynamic_update_slice | solution.py:125
  141.2 4.7 %all-to-all-start = ((f32[128,2,512]{2,1,0:T(2,128)}), f32[128,2,512]{2,1,0:T(2,128)S(1)}, u32[]{:S(2)}, u32[]{:S(2)}) async-start(f32[128,2,512]{2,1,0:T(2,128)} %reshape.374), calls=%async_computation | async-start | bytes 1048576 | tf_op jit(solution)/shard_map/while/body/eval_jaxpr/all_to_all | solution.py:34
  145.9 6.1 %gather_fusion = f32[4,512,512]{2,1,0:T(8,128)} fusion(f32[8,512,512]{2,1,0:T(8,128)} %get-tuple-element.727, s32[1024]{0:T(1024)S(1)} %pad_clamp_fusion.4), kind=kCustom, calls=%fused_computation.clone.clone.1 | custom fusion | bytes 8388624 | tf_op jit(solution)/shard_map/while/body/eval_jaxpr/jit(_take)/gather | solution.py:105
  152.2 7.2 %all-to-all-done = f32[128,2,512]{2,1,0:T(2,128)S(1)} async-done(((f32[128,2,512]{2,1,0:T(2,128)}), f32[128,2,512]{2,1,0:T(2,128)S(1)}, u32[]{:S(2)}, u32[]{:S(2)}) %all-to-all-start) | async-done | bytes 524320 | tf_op jit(solution)/shard_map/while/body/eval_jaxpr/all_to_all | solution.py:34
  159.9 5.8 %select_reduce_fusion.15 = (f32[512,128]{1,0:T(8,128)S(1)}, f32[512,128]{1,0:T(8,128)S(1)}) fusion(pred[4]{0:T(512)(128)(4,1)S(1)} %get-tuple-element.674, pred[4]{0:T(512)(128)(4,1)S(1)} %get-tuple-element.675, f32[4,512,512]{2,1,0:T(8,128)} %gather_fusion, f32[128,512]{1,0:T(8,128)S(1)} %get-tuple-element.678, ...), kind=kOutput, calls=%fused_computation.10.clone.1 | convolution fusion | flops 806486016 | bytes 5242892 | tf_op jit(solution)/shard_map/while/body/eval_jaxpr/rtb,tbc->rtc/dot_general | solution.py:108
  166.7 4.7 %all-to-all-start.1 = ((f32[128,2,512]{2,1,0:T(2,128)}), f32[128,2,512]{2,1,0:T(2,128)S(1)}, u32[]{:S(2)}, u32[]{:S(2)}) async-start(f32[128,2,512]{2,1,0:T(2,128)} %copy.204), calls=%async_computation.1 | async-start | bytes 1048576 | tf_op jit(solution)/shard_map/while/body/eval_jaxpr/all_to_all | solution.py:34
  171.6 13.5 %all-to-all-done.1 = f32[128,2,512]{2,1,0:T(2,128)S(1)} async-done(((f32[128,2,512]{2,1,0:T(2,128)}), f32[128,2,512]{2,1,0:T(2,128)S(1)}, u32[]{:S(2)}, u32[]{:S(2)}) %all-to-all-start.1) | async-done | bytes 524320 | tf_op jit(solution)/shard_map/while/body/eval_jaxpr/all_to_all | solution.py:34
  186.8 4.7 %all-to-all-start.2 = ((f32[128,1,512]{2,1,0:T(1,128)}), f32[128,1,512]{2,1,0:T(1,128)S(1)}, u32[]{:S(2)}, u32[]{:S(2)}) async-start(f32[128,1,512]{2,1,0:T(1,128)} %copy.206), calls=%async_computation.2 | async-start | bytes 524288 | tf_op jit(solution)/shard_map/while/body/eval_jaxpr/all_to_all | solution.py:34
  194.7 7.7 %all-to-all-done.2 = f32[128,1,512]{2,1,0:T(1,128)S(1)} async-done(((f32[128,1,512]{2,1,0:T(1,128)}), f32[128,1,512]{2,1,0:T(1,128)S(1)}, u32[]{:S(2)}, u32[]{:S(2)}) %all-to-all-start.2) | async-done | bytes 262176 | tf_op jit(solution)/shard_map/while/body/eval_jaxpr/all_to_all | solution.py:34
  205.0 4.7 %all-to-all-start.3 = ((f32[128,1,512]{2,1,0:T(1,128)}), f32[128,1,512]{2,1,0:T(1,128)S(1)}, u32[]{:S(2)}, u32[]{:S(2)}) async-start(f32[128,1,512]{2,1,0:T(1,128)} %copy.207), calls=%async_computation.3 | async-start | bytes 524288 | tf_op jit(solution)/shard_map/while/body/eval_jaxpr/all_to_all | solution.py:34
  210.3 10.2 %all-to-all-done.3 = f32[128,1,512]{2,1,0:T(1,128)S(1)} async-done(((f32[128,1,512]{2,1,0:T(1,128)}), f32[128,1,512]{2,1,0:T(1,128)S(1)}, u32[]{:S(2)}, u32[]{:S(2)}) %all-to-all-start.3) | async-done | bytes 262176 | tf_op jit(solution)/shard_map/while/body/eval_jaxpr/all_to_all | solution.py:34
  220.6 6.3 %dynamic_update_slice.18 = f32[5,128,512]{2,0,1:T(8,128)} dynamic-update-slice(f32[5,128,512]{2,0,1:T(8,128)} %get-tuple-element.704, f32[1,128,512]{2,0,1:T(1,128)S(1)} %bitcast.122, s32[]{:T(128)S(6)} %select_n.265, s32[]{:T(128)} %constant.148.clone.1..sunk, s32[]{:T(128)} %constant.148.clone.1..sunk) | dynamic-update-slice | bytes 524292 | tf_op jit(solution)/shard_map/while/body/eval_jaxpr/jit(dynamic_update_index_in_dim)/dynamic_update_slice | solution.py:125
  229.2 4.7 %all-to-all-start = ((f32[128,2,512]{2,1,0:T(2,128)}), f32[128,2,512]{2,1,0:T(2,128)S(1)}, u32[]{:S(2)}, u32[]{:S(2)}) async-start(f32[128,2,512]{2,1,0:T(2,128)} %reshape.374), calls=%async_computation | async-start | bytes 1048576 | tf_op jit(solution)/shard_map/while/body/eval_jaxpr/all_to_all | solution.py:34
  234.0 6.1 %gather_fusion = f32[4,512,512]{2,1,0:T(8,128)} fusion(f32[8,512,512]{2,1,0:T(8,128)} %get-tuple-element.727, s32[1024]{0:T(1024)S(1)} %pad_clamp_fusion.4), kind=kCustom, calls=%fused_computation.clone.clone.1 | custom fusion | bytes 8388624 | tf_op jit(solution)/shard_map/while/body/eval_jaxpr/jit(_take)/gather | solution.py:105
  240.3 7.2 %all-to-all-done = f32[128,2,512]{2,1,0:T(2,128)S(1)} async-done(((f32[128,2,512]{2,1,0:T(2,128)}), f32[128,2,512]{2,1,0:T(2,128)S(1)}, u32[]{:S(2)}, u32[]{:S(2)}) %all-to-all-start) | async-done | bytes 524320 | tf_op jit(solution)/shard_map/while/body/eval_jaxpr/all_to_all | solution.py:34
  248.0 5.8 %select_reduce_fusion.15 = (f32[512,128]{1,0:T(8,128)S(1)}, f32[512,128]{1,0:T(8,128)S(1)}) fusion(pred[4]{0:T(512)(128)(4,1)S(1)} %get-tuple-element.674, pred[4]{0:T(512)(128)(4,1)S(1)} %get-tuple-element.675, f32[4,512,512]{2,1,0:T(8,128)} %gather_fusion, f32[128,512]{1,0:T(8,128)S(1)} %get-tuple-element.678, ...), kind=kOutput, calls=%fused_computation.10.clone.1 | convolution fusion | flops 806486016 | bytes 5242892 | tf_op jit(solution)/shard_map/while/body/eval_jaxpr/rtb,tbc->rtc/dot_general | solution.py:108
  254.8 4.7 %all-to-all-start.1 = ((f32[128,2,512]{2,1,0:T(2,128)}), f32[128,2,512]{2,1,0:T(2,128)S(1)}, u32[]{:S(2)}, u32[]{:S(2)}) async-start(f32[128,2,512]{2,1,0:T(2,128)} %copy.204), calls=%async_computation.1 | async-start | bytes 1048576 | tf_op jit(solution)/shard_map/while/body/eval_jaxpr/all_to_all | solution.py:34
  259.7 13.5 %all-to-all-done.1 = f32[128,2,512]{2,1,0:T(2,128)S(1)} async-done(((f32[128,2,512]{2,1,0:T(2,128)}), f32[128,2,512]{2,1,0:T(2,128)S(1)}, u32[]{:S(2)}, u32[]{:S(2)}) %all-to-all-start.1) | async-done | bytes 524320 | tf_op jit(solution)/shard_map/while/body/eval_jaxpr/all_to_all | solution.py:34
  274.8 4.7 %all-to-all-start.2 = ((f32[128,1,512]{2,1,0:T(1,128)}), f32[128,1,512]{2,1,0:T(1,128)S(1)}, u32[]{:S(2)}, u32[]{:S(2)}) async-start(f32[128,1,512]{2,1,0:T(1,128)} %copy.206), calls=%async_computation.2 | async-start | bytes 524288 | tf_op jit(solution)/shard_map/while/body/eval_jaxpr/all_to_all | solution.py:34
  282.8 7.7 %all-to-all-done.2 = f32[128,1,512]{2,1,0:T(1,128)S(1)} async-done(((f32[128,1,512]{2,1,0:T(1,128)}), f32[128,1,512]{2,1,0:T(1,128)S(1)}, u32[]{:S(2)}, u32[]{:S(2)}) %all-to-all-start.2) | async-done | bytes 262176 | tf_op jit(solution)/shard_map/while/body/eval_jaxpr/all_to_all | solution.py:34
  298.3 10.2 %all-to-all-done.3 = f32[128,1,512]{2,1,0:T(1,128)S(1)} async-done(((f32[128,1,512]{2,1,0:T(1,128)}), f32[128,1,512]{2,1,0:T(1,128)S(1)}, u32[]{:S(2)}, u32[]{:S(2)}) %all-to-all-start.3) | async-done | bytes 262176 | tf_op jit(solution)/shard_map/while/body/eval_jaxpr/all_to_all | solution.py:34
  308.6 6.3 %dynamic_update_slice.18 = f32[5,128,512]{2,0,1:T(8,128)} dynamic-update-slice(f32[5,128,512]{2,0,1:T(8,128)} %get-tuple-element.704, f32[1,128,512]{2,0,1:T(1,128)S(1)} %bitcast.122, s32[]{:T(128)S(6)} %select_n.265, s32[]{:T(128)} %constant.148.clone.1..sunk, s32[]{:T(128)} %constant.148.clone.1..sunk) | dynamic-update-slice | bytes 524292 | tf_op jit(solution)/shard_map/while/body/eval_jaxpr/jit(dynamic_update_index_in_dim)/dynamic_update_slice | solution.py:125
  317.3 4.7 %all-to-all-start = ((f32[128,2,512]{2,1,0:T(2,128)}), f32[128,2,512]{2,1,0:T(2,128)S(1)}, u32[]{:S(2)}, u32[]{:S(2)}) async-start(f32[128,2,512]{2,1,0:T(2,128)} %reshape.374), calls=%async_computation | async-start | bytes 1048576 | tf_op jit(solution)/shard_map/while/body/eval_jaxpr/all_to_all | solution.py:34
  322.0 6.1 %gather_fusion = f32[4,512,512]{2,1,0:T(8,128)} fusion(f32[8,512,512]{2,1,0:T(8,128)} %get-tuple-element.727, s32[1024]{0:T(1024)S(1)} %pad_clamp_fusion.4), kind=kCustom, calls=%fused_computation.clone.clone.1 | custom fusion | bytes 8388624 | tf_op jit(solution)/shard_map/while/body/eval_jaxpr/jit(_take)/gather | solution.py:105
  328.3 7.2 %all-to-all-done = f32[128,2,512]{2,1,0:T(2,128)S(1)} async-done(((f32[128,2,512]{2,1,0:T(2,128)}), f32[128,2,512]{2,1,0:T(2,128)S(1)}, u32[]{:S(2)}, u32[]{:S(2)}) %all-to-all-start) | async-done | bytes 524320 | tf_op jit(solution)/shard_map/while/body/eval_jaxpr/all_to_all | solution.py:34
  336.0 5.8 %select_reduce_fusion.15 = (f32[512,128]{1,0:T(8,128)S(1)}, f32[512,128]{1,0:T(8,128)S(1)}) fusion(pred[4]{0:T(512)(128)(4,1)S(1)} %get-tuple-element.674, pred[4]{0:T(512)(128)(4,1)S(1)} %get-tuple-element.675, f32[4,512,512]{2,1,0:T(8,128)} %gather_fusion, f32[128,512]{1,0:T(8,128)S(1)} %get-tuple-element.678, ...), kind=kOutput, calls=%fused_computation.10.clone.1 | convolution fusion | flops 806486016 | bytes 5242892 | tf_op jit(solution)/shard_map/while/body/eval_jaxpr/rtb,tbc->rtc/dot_general | solution.py:108
  342.8 4.7 %all-to-all-start.1 = ((f32[128,2,512]{2,1,0:T(2,128)}), f32[128,2,512]{2,1,0:T(2,128)S(1)}, u32[]{:S(2)}, u32[]{:S(2)}) async-start(f32[128,2,512]{2,1,0:T(2,128)} %copy.204), calls=%async_computation.1 | async-start | bytes 1048576 | tf_op jit(solution)/shard_map/while/body/eval_jaxpr/all_to_all | solution.py:34
  347.7 13.5 %all-to-all-done.1 = f32[128,2,512]{2,1,0:T(2,128)S(1)} async-done(((f32[128,2,512]{2,1,0:T(2,128)}), f32[128,2,512]{2,1,0:T(2,128)S(1)}, u32[]{:S(2)}, u32[]{:S(2)}) %all-to-all-start.1) | async-done | bytes 524320 | tf_op jit(solution)/shard_map/while/body/eval_jaxpr/all_to_all | solution.py:34
  362.9 4.7 %all-to-all-start.2 = ((f32[128,1,512]{2,1,0:T(1,128)}), f32[128,1,512]{2,1,0:T(1,128)S(1)}, u32[]{:S(2)}, u32[]{:S(2)}) async-start(f32[128,1,512]{2,1,0:T(1,128)} %copy.206), calls=%async_computation.2 | async-start | bytes 524288 | tf_op jit(solution)/shard_map/while/body/eval_jaxpr/all_to_all | solution.py:34
  370.8 7.7 %all-to-all-done.2 = f32[128,1,512]{2,1,0:T(1,128)S(1)} async-done(((f32[128,1,512]{2,1,0:T(1,128)}), f32[128,1,512]{2,1,0:T(1,128)S(1)}, u32[]{:S(2)}, u32[]{:S(2)}) %all-to-all-start.2) | async-done | bytes 262176 | tf_op jit(solution)/shard_map/while/body/eval_jaxpr/all_to_all | solution.py:34
  381.1 4.7 %all-to-all-start.3 = ((f32[128,1,512]{2,1,0:T(1,128)}), f32[128,1,512]{2,1,0:T(1,128)S(1)}, u32[]{:S(2)}, u32[]{:S(2)}) async-start(f32[128,1,512]{2,1,0:T(1,128)} %copy.207), calls=%async_computation.3 | async-start | bytes 524288 | tf_op jit(solution)/shard_map/while/body/eval_jaxpr/all_to_all | solution.py:34
  386.4 10.2 %all-to-all-done.3 = f32[128,1,512]{2,1,0:T(1,128)S(1)} async-done(((f32[128,1,512]{2,1,0:T(1,128)}), f32[128,1,512]{2,1,0:T(1,128)S(1)}, u32[]{:S(2)}, u32[]{:S(2)}) %all-to-all-start.3) | async-done | bytes 262176 | tf_op jit(solution)/shard_map/while/body/eval_jaxpr/all_to_all | solution.py:34
  396.6 6.3 %dynamic_update_slice.18 = f32[5,128,512]{2,0,1:T(8,128)} dynamic-update-slice(f32[5,128,512]{2,0,1:T(8,128)} %get-tuple-element.704, f32[1,128,512]{2,0,1:T(1,128)S(1)} %bitcast.122, s32[]{:T(128)S(6)} %select_n.265, s32[]{:T(128)} %constant.148.clone.1..sunk, s32[]{:T(128)} %constant.148.clone.1..sunk) | dynamic-update-slice | bytes 524292 | tf_op jit(solution)/shard_map/while/body/eval_jaxpr/jit(dynamic_update_index_in_dim)/dynamic_update_slice | solution.py:125
  403.2 5.8 %fusion.37 = (f32[1,128,512]{2,0,1:T(1,128)S(1)}, f32[1,128,512]{2,0,1:T(1,128)S(1)}, f32[1,128,512]{2,0,1:T(1,128)S(1)}, f32[1,128,512]{2,0,1:T(1,128)S(1)}, f32[1,128,512]{2,0,1:T(1,128)S(1)}) fusion(f32[5,128,512]{2,0,1:T(8,128)} %get-tuple-element.379), kind=kLoop, calls=%fused_computation.110 | loop fusion | bytes 2621440 | tf_op jit(solution)/shard_map/slice | solution.py:129
  (202 shorter events, 67.9 us)
Async XLA Ops:
  1.9 30.1 %copy-start = (f32[2,512,512]{2,1,0:T(8,128)S(1)}, f32[2,512,512]{2,1,0:T(8,128)}, u32[]{:S(2)}) copy-start(f32[2,512,512]{2,1,0:T(8,128)} %param.9) | copy-start | bytes 6291460
  9.7 22.3 %all-to-all-start.4 = ((f32[128,1,512]{2,1,0:T(1,128)}), f32[128,1,512]{2,1,0:T(1,128)S(1)}, u32[]{:S(2)}, u32[]{:S(2)}) async-start(f32[128,1,512]{2,1,0:T(1,128)} %all_to_all.66), calls=%async_computation.4 | async-start | bytes 524288 | tf_op jit(solution)/shard_map/all_to_all | solution.py:34
  33.4 15.5 %all-to-all-start.5 = ((f32[128,1,512]{2,1,0:T(1,128)}), f32[128,1,512]{2,1,0:T(1,128)S(1)}, u32[]{:S(2)}, u32[]{:S(2)}) async-start(f32[128,1,512]{2,1,0:T(1,128)} %copy.125), calls=%async_computation.5 | async-start | bytes 524288 | tf_op jit(solution)/shard_map/all_to_all | solution.py:34
  53.1 18.3 %all-to-all-start = ((f32[128,2,512]{2,1,0:T(2,128)}), f32[128,2,512]{2,1,0:T(2,128)S(1)}, u32[]{:S(2)}, u32[]{:S(2)}) async-start(f32[128,2,512]{2,1,0:T(2,128)} %reshape.374), calls=%async_computation | async-start | bytes 1048576 | tf_op jit(solution)/shard_map/while/body/eval_jaxpr/all_to_all | solution.py:34
  78.7 18.4 %all-to-all-start.1 = ((f32[128,2,512]{2,1,0:T(2,128)}), f32[128,2,512]{2,1,0:T(2,128)S(1)}, u32[]{:S(2)}, u32[]{:S(2)}) async-start(f32[128,2,512]{2,1,0:T(2,128)} %copy.204), calls=%async_computation.1 | async-start | bytes 1048576 | tf_op jit(solution)/shard_map/while/body/eval_jaxpr/all_to_all | solution.py:34
  98.7 15.6 %all-to-all-start.2 = ((f32[128,1,512]{2,1,0:T(1,128)}), f32[128,1,512]{2,1,0:T(1,128)S(1)}, u32[]{:S(2)}, u32[]{:S(2)}) async-start(f32[128,1,512]{2,1,0:T(1,128)} %copy.206), calls=%async_computation.2 | async-start | bytes 524288 | tf_op jit(solution)/shard_map/while/body/eval_jaxpr/all_to_all | solution.py:34
  117.0 15.5 %all-to-all-start.3 = ((f32[128,1,512]{2,1,0:T(1,128)}), f32[128,1,512]{2,1,0:T(1,128)S(1)}, u32[]{:S(2)}, u32[]{:S(2)}) async-start(f32[128,1,512]{2,1,0:T(1,128)} %copy.207), calls=%async_computation.3 | async-start | bytes 524288 | tf_op jit(solution)/shard_map/while/body/eval_jaxpr/all_to_all | solution.py:34
  141.2 18.3 %all-to-all-start = ((f32[128,2,512]{2,1,0:T(2,128)}), f32[128,2,512]{2,1,0:T(2,128)S(1)}, u32[]{:S(2)}, u32[]{:S(2)}) async-start(f32[128,2,512]{2,1,0:T(2,128)} %reshape.374), calls=%async_computation | async-start | bytes 1048576 | tf_op jit(solution)/shard_map/while/body/eval_jaxpr/all_to_all | solution.py:34
  166.7 18.4 %all-to-all-start.1 = ((f32[128,2,512]{2,1,0:T(2,128)}), f32[128,2,512]{2,1,0:T(2,128)S(1)}, u32[]{:S(2)}, u32[]{:S(2)}) async-start(f32[128,2,512]{2,1,0:T(2,128)} %copy.204), calls=%async_computation.1 | async-start | bytes 1048576 | tf_op jit(solution)/shard_map/while/body/eval_jaxpr/all_to_all | solution.py:34
  186.8 15.6 %all-to-all-start.2 = ((f32[128,1,512]{2,1,0:T(1,128)}), f32[128,1,512]{2,1,0:T(1,128)S(1)}, u32[]{:S(2)}, u32[]{:S(2)}) async-start(f32[128,1,512]{2,1,0:T(1,128)} %copy.206), calls=%async_computation.2 | async-start | bytes 524288 | tf_op jit(solution)/shard_map/while/body/eval_jaxpr/all_to_all | solution.py:34
  205.0 15.5 %all-to-all-start.3 = ((f32[128,1,512]{2,1,0:T(1,128)}), f32[128,1,512]{2,1,0:T(1,128)S(1)}, u32[]{:S(2)}, u32[]{:S(2)}) async-start(f32[128,1,512]{2,1,0:T(1,128)} %copy.207), calls=%async_computation.3 | async-start | bytes 524288 | tf_op jit(solution)/shard_map/while/body/eval_jaxpr/all_to_all | solution.py:34
  229.2 18.3 %all-to-all-start = ((f32[128,2,512]{2,1,0:T(2,128)}), f32[128,2,512]{2,1,0:T(2,128)S(1)}, u32[]{:S(2)}, u32[]{:S(2)}) async-start(f32[128,2,512]{2,1,0:T(2,128)} %reshape.374), calls=%async_computation | async-start | bytes 1048576 | tf_op jit(solution)/shard_map/while/body/eval_jaxpr/all_to_all | solution.py:34
  254.8 18.4 %all-to-all-start.1 = ((f32[128,2,512]{2,1,0:T(2,128)}), f32[128,2,512]{2,1,0:T(2,128)S(1)}, u32[]{:S(2)}, u32[]{:S(2)}) async-start(f32[128,2,512]{2,1,0:T(2,128)} %copy.204), calls=%async_computation.1 | async-start | bytes 1048576 | tf_op jit(solution)/shard_map/while/body/eval_jaxpr/all_to_all | solution.py:34
  274.8 15.6 %all-to-all-start.2 = ((f32[128,1,512]{2,1,0:T(1,128)}), f32[128,1,512]{2,1,0:T(1,128)S(1)}, u32[]{:S(2)}, u32[]{:S(2)}) async-start(f32[128,1,512]{2,1,0:T(1,128)} %copy.206), calls=%async_computation.2 | async-start | bytes 524288 | tf_op jit(solution)/shard_map/while/body/eval_jaxpr/all_to_all | solution.py:34
  293.1 15.5 %all-to-all-start.3 = ((f32[128,1,512]{2,1,0:T(1,128)}), f32[128,1,512]{2,1,0:T(1,128)S(1)}, u32[]{:S(2)}, u32[]{:S(2)}) async-start(f32[128,1,512]{2,1,0:T(1,128)} %copy.207), calls=%async_computation.3 | async-start | bytes 524288 | tf_op jit(solution)/shard_map/while/body/eval_jaxpr/all_to_all | solution.py:34
  317.3 18.3 %all-to-all-start = ((f32[128,2,512]{2,1,0:T(2,128)}), f32[128,2,512]{2,1,0:T(2,128)S(1)}, u32[]{:S(2)}, u32[]{:S(2)}) async-start(f32[128,2,512]{2,1,0:T(2,128)} %reshape.374), calls=%async_computation | async-start | bytes 1048576 | tf_op jit(solution)/shard_map/while/body/eval_jaxpr/all_to_all | solution.py:34
  342.8 18.4 %all-to-all-start.1 = ((f32[128,2,512]{2,1,0:T(2,128)}), f32[128,2,512]{2,1,0:T(2,128)S(1)}, u32[]{:S(2)}, u32[]{:S(2)}) async-start(f32[128,2,512]{2,1,0:T(2,128)} %copy.204), calls=%async_computation.1 | async-start | bytes 1048576 | tf_op jit(solution)/shard_map/while/body/eval_jaxpr/all_to_all | solution.py:34
  362.9 15.6 %all-to-all-start.2 = ((f32[128,1,512]{2,1,0:T(1,128)}), f32[128,1,512]{2,1,0:T(1,128)S(1)}, u32[]{:S(2)}, u32[]{:S(2)}) async-start(f32[128,1,512]{2,1,0:T(1,128)} %copy.206), calls=%async_computation.2 | async-start | bytes 524288 | tf_op jit(solution)/shard_map/while/body/eval_jaxpr/all_to_all | solution.py:34
  381.1 15.5 %all-to-all-start.3 = ((f32[128,1,512]{2,1,0:T(1,128)}), f32[128,1,512]{2,1,0:T(1,128)S(1)}, u32[]{:S(2)}, u32[]{:S(2)}) async-start(f32[128,1,512]{2,1,0:T(1,128)} %copy.207), calls=%async_computation.3 | async-start | bytes 524288 | tf_op jit(solution)/shard_map/while/body/eval_jaxpr/all_to_all | solution.py:34

commit v3 on v0

--- a/solution.py
+++ b/solution.py
@@ -117,23 +117,19 @@
     coming, coming_targets = tiles(0, first)
 
     def middle(current, carry):
-        update, coming, coming_targets, kept = carry
+        update, coming, coming_targets, solution = carry
         residue, update = residual(current, update, coming, coming_targets)
         returned = solve(current, residue)
-        kept = lax.dynamic_update_index_in_dim(kept, returned, current - 1, 0)
+        solution = jnp.where(at_level(owner_at, current)[:, :, None], returned[:, None, :], solution)
         coming, coming_targets = tiles(current, returned)
-        return update, coming, coming_targets, kept
+        return update, coming, coming_targets, solution
 
-    kept = jnp.zeros((tile_levels - 1, devices, block), jnp.float32)
-    update, coming, coming_targets, kept = lax.fori_loop(
-        1, tile_levels, middle, (update, coming, coming_targets, kept))
+    solution = jnp.broadcast_to(first[:, None, :], (devices, per_owner, block))
+    update, coming, coming_targets, solution = lax.fori_loop(
+        1, tile_levels, middle, (update, coming, coming_targets, solution))
     residue, _ = residual(LEVELS - 1, update, coming, coming_targets)
     last = solve(LEVELS - 1, residue)
-
-    solved_rows = [first] + [kept[i] for i in range(tile_levels - 1)] + [last]
-    solution = solved_rows[0][:, None, :]
-    for current in range(1, LEVELS):
-        solution = jnp.where(owner_at[current][:, :, None], solved_rows[current][:, None, :], solution)
+    solution = jnp.where(owner_at[LEVELS - 1][:, :, None], last[:, None, :], solution)
     return solution.reshape(1, supernodes, block)
 
 

time: 390 us -> 385 us (0.987)
  local copies, waits for them, and re-layouts: 85 us -> 61.4 us
  blocking collectives: 0 us -> 15.4 us
  waiting for transfers between devices: 154 us -> 165 us
  starting transfers between devices: 91.5 us -> 86.8 us
    dynamic_update_slice x3 -> x0, local copies, waits for them, and re-layouts: 18.3 us -> none  [middle(): kept = lax.dynamic_update_index_in_dim(kept, returned, current - 1, 0)]
    all_to_all x0 -> x1, blocking collectives: none -> 15.4 us  [a2a(): return lax.all_to_all(x, 'dev', split_axis=0, concat_axis=0, tiled=True)]
    all_to_all x18 -> x17, waiting for transfers between devices: 154 us -> 165 us  [a2a(): return lax.all_to_all(x, 'dev', split_axis=0, concat_axis=0, tiled=True)]
    reduce_sum x5, other arithmetic: 10 us -> 5.1 us  [residual(): jnp.sum(jnp.where(at_level(owner_at, current)[:, :, None], rhs - update,...]
    all_to_all x18 -> x17, starting transfers between devices: 91.5 us -> 86.8 us  [a2a(): return lax.all_to_all(x, 'dev', split_axis=0, concat_axis=0, tiled=True)]
  transfers between devices with their start and end apart: 18 -> 17, of which waited for: 18 -> 17; matrix products, arithmetic and copies ran while one was open for 14% -> 8% of each run, Pallas kernels for 0% -> 0%
where the time goes in v3:
time: 385 us; the launch traced here: 384 us
  waiting for transfers between devices  165 us (43%)
  starting transfers between devices  86.8 us (23%)
  local copies, waits for them, and re-layouts  61.4 us (16%)
  matrix products  32.6 us (8%)
  blocking collectives  15.4 us (4%)
  other arithmetic  11.2 us (3%)
  loops' own time  7.25 us (2%)
  between operations  4.33 us (1%)
    all_to_all x17, waiting for transfers between devices, a2a(): return lax.all_to_all(x, 'dev', split_axis=0, concat_axis=0, tiled=True)  165 us
    all_to_all x17, starting transfers between devices, a2a(): return lax.all_to_all(x, 'dev', split_axis=0, concat_axis=0, tiled=True)  86.8 us
    gather x4, local copies, waits for them, and re-layouts, tiles(): jnp.take(factor_tiles, at_level(slot_tile, current), axis=0, mode='clip')  24.5 us
    dot_general x4, matrix products, tiles(): jnp.einsum('rtb,tbc->rtc', sources, factors, precision=product_precision,...  23 us
    all_to_all x1, blocking collectives, a2a(): return lax.all_to_all(x, 'dev', split_axis=0, concat_axis=0, tiled=True)  15.4 us
    all_to_all x10, local copies, waits for them, and re-layouts, a2a(): return lax.all_to_all(x, 'dev', split_axis=0, concat_axis=0, tiled=True)  8.94 us
  transfers between devices with their start and end apart: 17, of which 17 were waited for; matrix products, arithmetic and copies ran while one was open for 8% of the time, Pallas kernels for 0%

profile of v3, /device:TPU:1, one launch (start us, length us, event | category | flops | bytes accessed | tf_op | source)
XLA Modules:
  0.0 383.6 jit_solution(17020683031265811894)
XLA Ops:
  10.0 11.5 %all-to-all-start.4 = ((f32[128,1,512]{2,1,0:T(1,128)}), f32[128,1,512]{2,1,0:T(1,128)S(1)}, u32[]{:S(2)}, u32[]{:S(2)}) async-start(f32[128,1,512]{2,1,0:T(1,128)} %all_to_all.86), calls=%async_computation.4 | async-start | bytes 524288 | tf_op jit(solution)/shard_map/all_to_all | solution.py:34
  24.0 8.3 %all-to-all-done.4 = f32[128,1,512]{2,1,0:T(1,128)S(1)} async-done(((f32[128,1,512]{2,1,0:T(1,128)}), f32[128,1,512]{2,1,0:T(1,128)S(1)}, u32[]{:S(2)}, u32[]{:S(2)}) %all-to-all-start.4) | async-done | bytes 262176 | tf_op jit(solution)/shard_map/all_to_all | solution.py:34
  33.7 4.7 %all-to-all-start.5 = ((f32[128,1,512]{2,1,0:T(1,128)}), f32[128,1,512]{2,1,0:T(1,128)S(1)}, u32[]{:S(2)}, u32[]{:S(2)}) async-start(f32[128,1,512]{2,1,0:T(1,128)} %copy.139), calls=%async_computation.5 | async-start | bytes 524288 | tf_op jit(solution)/shard_map/all_to_all | solution.py:34
  39.0 10.3 %all-to-all-done.5 = f32[128,1,512]{2,1,0:T(1,128)S(1)} async-done(((f32[128,1,512]{2,1,0:T(1,128)}), f32[128,1,512]{2,1,0:T(1,128)S(1)}, u32[]{:S(2)}, u32[]{:S(2)}) %all-to-all-start.5) | async-done | bytes 262176 | tf_op jit(solution)/shard_map/all_to_all | solution.py:34
  51.4 4.7 %all-to-all-start.6 = ((f32[128,2,512]{2,1,0:T(2,128)}), f32[128,2,512]{2,1,0:T(2,128)S(1)}, u32[]{:S(2)}, u32[]{:S(2)}) async-start(f32[128,2,512]{2,1,0:T(2,128)} %reshape.191), calls=%async_computation.6 | async-start | bytes 1048576 | tf_op jit(solution)/shard_map/all_to_all | solution.py:34
  56.1 6.1 %gather_fusion.2 = f32[4,512,512]{2,1,0:T(8,128)} fusion(f32[8,512,512]{2,1,0:T(8,128)} %param.10, s32[1024]{0:T(1024)S(1)} %pad_clamp_fusion.3), kind=kCustom, calls=%fused_computation.2 | custom fusion | bytes 8388624 | tf_op jit(solution)/shard_map/jit(_take)/gather | solution.py:105
  62.6 7.1 %all-to-all-done.6 = f32[128,2,512]{2,1,0:T(2,128)S(1)} async-done(((f32[128,2,512]{2,1,0:T(2,128)}), f32[128,2,512]{2,1,0:T(2,128)S(1)}, u32[]{:S(2)}, u32[]{:S(2)}) %all-to-all-start.6) | async-done | bytes 524320 | tf_op jit(solution)/shard_map/all_to_all | solution.py:34
  70.1 5.8 %select_reduce_fusion.4 = (f32[512,128]{1,0:T(8,128)S(1)}, f32[512,128]{1,0:T(8,128)S(1)}) fusion(pred[4]{0:T(512)(128)(4,1)S(1)} %get-tuple-element.571, pred[4]{0:T(512)(128)(4,1)S(1)} %get-tuple-element.572, f32[4,512,512]{2,1,0:T(8,128)} %gather_fusion.2, f32[128,512]{1,0:T(8,128)S(1)} %bitcast.145, f32[128,512]{1,0:T(8,128)S(1)} %bitcast.144, ...), kind=kOutput, calls=%fused_computation.57 | convolution fusion | flops 806486016 | bytes 5242892 | tf_op jit(solution)/shard_map/rtb,tbc->rtc/dot_general | solution.py:108
  76.9 4.7 %all-to-all-start.7 = ((f32[128,2,512]{2,1,0:T(2,128)}), f32[128,2,512]{2,1,0:T(2,128)S(1)}, u32[]{:S(2)}, u32[]{:S(2)}) async-start(f32[128,2,512]{2,1,0:T(2,128)} %copy.145), calls=%async_computation.7 | async-start | bytes 1048576 | tf_op jit(solution)/shard_map/all_to_all | solution.py:34
  81.7 13.6 %all-to-all-done.7 = f32[128,2,512]{2,1,0:T(2,128)S(1)} async-done(((f32[128,2,512]{2,1,0:T(2,128)}), f32[128,2,512]{2,1,0:T(2,128)S(1)}, u32[]{:S(2)}, u32[]{:S(2)}) %all-to-all-start.7) | async-done | bytes 524320 | tf_op jit(solution)/shard_map/all_to_all | solution.py:34
  95.8 250.8 %while.22 = (s32[]{:T(128)}, f32[128,2,512]{2,1,0:T(2,128)S(1)}, f32[256,512]{1,0:T(8,128)S(1)}, s32[256]{0:T(256)S(1)}, f32[128,2,512]{2,1,0:T(2,128)S(1)}, /*i...) while((s32[]{:T(128)}, f32[128,2,512]{2,1,0:T(2,128)S(1)}, ...), condition=%wide.region_24.25_spmd.clone, body=%wide.region_20.24_spmd.clone.sunk | while | flops 1612810240 | bytes 35675224 | solution.py:128
  99.3 4.7 %all-to-all-start = ((f32[128,1,512]{2,1,0:T(1,128)}), f32[128,1,512]{2,1,0:T(1,128)S(1)}, u32[]{:S(2)}, u32[]{:S(2)}) async-start(f32[128,1,512]{2,1,0:T(1,128)} %copy.211), calls=%async_computation | async-start | bytes 524288 | tf_op jit(solution)/shard_map/while/body/eval_jaxpr/all_to_all | solution.py:34
  106.8 8.2 %all-to-all-done = f32[128,1,512]{2,1,0:T(1,128)S(1)} async-done(((f32[128,1,512]{2,1,0:T(1,128)}), f32[128,1,512]{2,1,0:T(1,128)S(1)}, u32[]{:S(2)}, u32[]{:S(2)}) %all-to-all-start) | async-done | bytes 262176 | tf_op jit(solution)/shard_map/while/body/eval_jaxpr/all_to_all | solution.py:34
  115.0 1.6 convolution_bitcast_fusion.4
  117.6 4.7 %all-to-all-start.1 = ((f32[128,1,512]{2,1,0:T(1,128)}), f32[128,1,512]{2,1,0:T(1,128)S(1)}, u32[]{:S(2)}, u32[]{:S(2)}) async-start(f32[128,1,512]{2,1,0:T(1,128)} %copy.212), calls=%async_computation.1 | async-start | bytes 524288 | tf_op jit(solution)/shard_map/while/body/eval_jaxpr/all_to_all | solution.py:34
  122.6 10.5 %all-to-all-done.1 = f32[128,1,512]{2,1,0:T(1,128)S(1)} async-done(((f32[128,1,512]{2,1,0:T(1,128)}), f32[128,1,512]{2,1,0:T(1,128)S(1)}, u32[]{:S(2)}, u32[]{:S(2)}) %all-to-all-start.1) | async-done | bytes 262176 | tf_op jit(solution)/shard_map/while/body/eval_jaxpr/all_to_all | solution.py:34
  135.2 4.7 %all-to-all-start.2 = ((f32[128,2,512]{2,1,0:T(2,128)}), f32[128,2,512]{2,1,0:T(2,128)S(1)}, u32[]{:S(2)}, u32[]{:S(2)}) async-start(f32[128,2,512]{2,1,0:T(2,128)} %reshape.260), calls=%async_computation.2 | async-start | bytes 1048576 | tf_op jit(solution)/shard_map/while/body/eval_jaxpr/all_to_all | solution.py:34
  140.0 6.1 %gather_fusion = f32[4,512,512]{2,1,0:T(8,128)} fusion(f32[8,512,512]{2,1,0:T(8,128)} %get-tuple-element.799, s32[1024]{0:T(1024)S(1)} %pad_clamp_fusion.6), kind=kCustom, calls=%fused_computation.clone.clone.1 | custom fusion | bytes 8388624 | tf_op jit(solution)/shard_map/while/body/eval_jaxpr/jit(_take)/gather | solution.py:105
  146.3 7.2 %all-to-all-done.2 = f32[128,2,512]{2,1,0:T(2,128)S(1)} async-done(((f32[128,2,512]{2,1,0:T(2,128)}), f32[128,2,512]{2,1,0:T(2,128)S(1)}, u32[]{:S(2)}, u32[]{:S(2)}) %all-to-all-start.2) | async-done | bytes 524320 | tf_op jit(solution)/shard_map/while/body/eval_jaxpr/all_to_all | solution.py:34
  154.0 5.8 %select_reduce_fusion.19 = (f32[512,128]{1,0:T(8,128)S(1)}, f32[512,128]{1,0:T(8,128)S(1)}) fusion(pred[4]{0:T(512)(128)(4,1)S(1)} %get-tuple-element.741, pred[4]{0:T(512)(128)(4,1)S(1)} %get-tuple-element.742, f32[4,512,512]{2,1,0:T(8,128)} %gather_fusion, f32[128,512]{1,0:T(8,128)S(1)} %get-tuple-element.746, ...), kind=kOutput, calls=%fused_computation.10.clone.1 | convolution fusion | flops 806486016 | bytes 5242892 | tf_op jit(solution)/shard_map/while/body/eval_jaxpr/rtb,tbc->rtc/dot_general | solution.py:108
  160.8 4.7 %all-to-all-start.3 = ((f32[128,2,512]{2,1,0:T(2,128)}), f32[128,2,512]{2,1,0:T(2,128)S(1)}, u32[]{:S(2)}, u32[]{:S(2)}) async-start(f32[128,2,512]{2,1,0:T(2,128)} %copy.215), calls=%async_computation.3 | async-start | bytes 1048576 | tf_op jit(solution)/shard_map/while/body/eval_jaxpr/all_to_all | solution.py:34
  166.3 12.9 %all-to-all-done.3 = f32[128,2,512]{2,1,0:T(2,128)S(1)} async-done(((f32[128,2,512]{2,1,0:T(2,128)}), f32[128,2,512]{2,1,0:T(2,128)S(1)}, u32[]{:S(2)}, u32[]{:S(2)}) %all-to-all-start.3) | async-done | bytes 524320 | tf_op jit(solution)/shard_map/while/body/eval_jaxpr/all_to_all | solution.py:34
  182.8 4.7 %all-to-all-start = ((f32[128,1,512]{2,1,0:T(1,128)}), f32[128,1,512]{2,1,0:T(1,128)S(1)}, u32[]{:S(2)}, u32[]{:S(2)}) async-start(f32[128,1,512]{2,1,0:T(1,128)} %copy.211), calls=%async_computation | async-start | bytes 524288 | tf_op jit(solution)/shard_map/while/body/eval_jaxpr/all_to_all | solution.py:34
  190.3 8.1 %all-to-all-done = f32[128,1,512]{2,1,0:T(1,128)S(1)} async-done(((f32[128,1,512]{2,1,0:T(1,128)}), f32[128,1,512]{2,1,0:T(1,128)S(1)}, u32[]{:S(2)}, u32[]{:S(2)}) %all-to-all-start) | async-done | bytes 262176 | tf_op jit(solution)/shard_map/while/body/eval_jaxpr/all_to_all | solution.py:34
  198.4 1.6 convolution_bitcast_fusion.4
  201.0 4.7 %all-to-all-start.1 = ((f32[128,1,512]{2,1,0:T(1,128)}), f32[128,1,512]{2,1,0:T(1,128)S(1)}, u32[]{:S(2)}, u32[]{:S(2)}) async-start(f32[128,1,512]{2,1,0:T(1,128)} %copy.212), calls=%async_computation.1 | async-start | bytes 524288 | tf_op jit(solution)/shard_map/while/body/eval_jaxpr/all_to_all | solution.py:34
  206.1 10.5 %all-to-all-done.1 = f32[128,1,512]{2,1,0:T(1,128)S(1)} async-done(((f32[128,1,512]{2,1,0:T(1,128)}), f32[128,1,512]{2,1,0:T(1,128)S(1)}, u32[]{:S(2)}, u32[]{:S(2)}) %all-to-all-start.1) | async-done | bytes 262176 | tf_op jit(solution)/shard_map/while/body/eval_jaxpr/all_to_all | solution.py:34
  218.7 4.7 %all-to-all-start.2 = ((f32[128,2,512]{2,1,0:T(2,128)}), f32[128,2,512]{2,1,0:T(2,128)S(1)}, u32[]{:S(2)}, u32[]{:S(2)}) async-start(f32[128,2,512]{2,1,0:T(2,128)} %reshape.260), calls=%async_computation.2 | async-start | bytes 1048576 | tf_op jit(solution)/shard_map/while/body/eval_jaxpr/all_to_all | solution.py:34
  223.4 6.1 %gather_fusion = f32[4,512,512]{2,1,0:T(8,128)} fusion(f32[8,512,512]{2,1,0:T(8,128)} %get-tuple-element.799, s32[1024]{0:T(1024)S(1)} %pad_clamp_fusion.6), kind=kCustom, calls=%fused_computation.clone.clone.1 | custom fusion | bytes 8388624 | tf_op jit(solution)/shard_map/while/body/eval_jaxpr/jit(_take)/gather | solution.py:105
  229.8 7.2 %all-to-all-done.2 = f32[128,2,512]{2,1,0:T(2,128)S(1)} async-done(((f32[128,2,512]{2,1,0:T(2,128)}), f32[128,2,512]{2,1,0:T(2,128)S(1)}, u32[]{:S(2)}, u32[]{:S(2)}) %all-to-all-start.2) | async-done | bytes 524320 | tf_op jit(solution)/shard_map/while/body/eval_jaxpr/all_to_all | solution.py:34
  237.4 5.8 %select_reduce_fusion.19 = (f32[512,128]{1,0:T(8,128)S(1)}, f32[512,128]{1,0:T(8,128)S(1)}) fusion(pred[4]{0:T(512)(128)(4,1)S(1)} %get-tuple-element.741, pred[4]{0:T(512)(128)(4,1)S(1)} %get-tuple-element.742, f32[4,512,512]{2,1,0:T(8,128)} %gather_fusion, f32[128,512]{1,0:T(8,128)S(1)} %get-tuple-element.746, ...), kind=kOutput, calls=%fused_computation.10.clone.1 | convolution fusion | flops 806486016 | bytes 5242892 | tf_op jit(solution)/shard_map/while/body/eval_jaxpr/rtb,tbc->rtc/dot_general | solution.py:108
  244.2 4.7 %all-to-all-start.3 = ((f32[128,2,512]{2,1,0:T(2,128)}), f32[128,2,512]{2,1,0:T(2,128)S(1)}, u32[]{:S(2)}, u32[]{:S(2)}) async-start(f32[128,2,512]{2,1,0:T(2,128)} %copy.215), calls=%async_computation.3 | async-start | bytes 1048576 | tf_op jit(solution)/shard_map/while/body/eval_jaxpr/all_to_all | solution.py:34
  249.7 12.9 %all-to-all-done.3 = f32[128,2,512]{2,1,0:T(2,128)S(1)} async-done(((f32[128,2,512]{2,1,0:T(2,128)}), f32[128,2,512]{2,1,0:T(2,128)S(1)}, u32[]{:S(2)}, u32[]{:S(2)}) %all-to-all-start.3) | async-done | bytes 524320 | tf_op jit(solution)/shard_map/while/body/eval_jaxpr/all_to_all | solution.py:34
  266.3 4.7 %all-to-all-start = ((f32[128,1,512]{2,1,0:T(1,128)}), f32[128,1,512]{2,1,0:T(1,128)S(1)}, u32[]{:S(2)}, u32[]{:S(2)}) async-start(f32[128,1,512]{2,1,0:T(1,128)} %copy.211), calls=%async_computation | async-start | bytes 524288 | tf_op jit(solution)/shard_map/while/body/eval_jaxpr/all_to_all | solution.py:34
  273.7 8.2 %all-to-all-done = f32[128,1,512]{2,1,0:T(1,128)S(1)} async-done(((f32[128,1,512]{2,1,0:T(1,128)}), f32[128,1,512]{2,1,0:T(1,128)S(1)}, u32[]{:S(2)}, u32[]{:S(2)}) %all-to-all-start) | async-done | bytes 262176 | tf_op jit(solution)/shard_map/while/body/eval_jaxpr/all_to_all | solution.py:34
  281.9 1.6 convolution_bitcast_fusion.4
  284.5 4.7 %all-to-all-start.1 = ((f32[128,1,512]{2,1,0:T(1,128)}), f32[128,1,512]{2,1,0:T(1,128)S(1)}, u32[]{:S(2)}, u32[]{:S(2)}) async-start(f32[128,1,512]{2,1,0:T(1,128)} %copy.212), calls=%async_computation.1 | async-start | bytes 524288 | tf_op jit(solution)/shard_map/while/body/eval_jaxpr/all_to_all | solution.py:34
  289.5 10.5 %all-to-all-done.1 = f32[128,1,512]{2,1,0:T(1,128)S(1)} async-done(((f32[128,1,512]{2,1,0:T(1,128)}), f32[128,1,512]{2,1,0:T(1,128)S(1)}, u32[]{:S(2)}, u32[]{:S(2)}) %all-to-all-start.1) | async-done | bytes 262176 | tf_op jit(solution)/shard_map/while/body/eval_jaxpr/all_to_all | solution.py:34
  302.2 4.7 %all-to-all-start.2 = ((f32[128,2,512]{2,1,0:T(2,128)}), f32[128,2,512]{2,1,0:T(2,128)S(1)}, u32[]{:S(2)}, u32[]{:S(2)}) async-start(f32[128,2,512]{2,1,0:T(2,128)} %reshape.260), calls=%async_computation.2 | async-start | bytes 1048576 | tf_op jit(solution)/shard_map/while/body/eval_jaxpr/all_to_all | solution.py:34
  306.9 6.1 %gather_fusion = f32[4,512,512]{2,1,0:T(8,128)} fusion(f32[8,512,512]{2,1,0:T(8,128)} %get-tuple-element.799, s32[1024]{0:T(1024)S(1)} %pad_clamp_fusion.6), kind=kCustom, calls=%fused_computation.clone.clone.1 | custom fusion | bytes 8388624 | tf_op jit(solution)/shard_map/while/body/eval_jaxpr/jit(_take)/gather | solution.py:105
  313.2 7.2 %all-to-all-done.2 = f32[128,2,512]{2,1,0:T(2,128)S(1)} async-done(((f32[128,2,512]{2,1,0:T(2,128)}), f32[128,2,512]{2,1,0:T(2,128)S(1)}, u32[]{:S(2)}, u32[]{:S(2)}) %all-to-all-start.2) | async-done | bytes 524320 | tf_op jit(solution)/shard_map/while/body/eval_jaxpr/all_to_all | solution.py:34
  320.9 5.8 %select_reduce_fusion.19 = (f32[512,128]{1,0:T(8,128)S(1)}, f32[512,128]{1,0:T(8,128)S(1)}) fusion(pred[4]{0:T(512)(128)(4,1)S(1)} %get-tuple-element.741, pred[4]{0:T(512)(128)(4,1)S(1)} %get-tuple-element.742, f32[4,512,512]{2,1,0:T(8,128)} %gather_fusion, f32[128,512]{1,0:T(8,128)S(1)} %get-tuple-element.746, ...), kind=kOutput, calls=%fused_computation.10.clone.1 | convolution fusion | flops 806486016 | bytes 5242892 | tf_op jit(solution)/shard_map/while/body/eval_jaxpr/rtb,tbc->rtc/dot_general | solution.py:108
  327.7 4.7 %all-to-all-start.3 = ((f32[128,2,512]{2,1,0:T(2,128)}), f32[128,2,512]{2,1,0:T(2,128)S(1)}, u32[]{:S(2)}, u32[]{:S(2)}) async-start(f32[128,2,512]{2,1,0:T(2,128)} %copy.215), calls=%async_computation.3 | async-start | bytes 1048576 | tf_op jit(solution)/shard_map/while/body/eval_jaxpr/all_to_all | solution.py:34
  333.2 12.9 %all-to-all-done.3 = f32[128,2,512]{2,1,0:T(2,128)S(1)} async-done(((f32[128,2,512]{2,1,0:T(2,128)}), f32[128,2,512]{2,1,0:T(2,128)S(1)}, u32[]{:S(2)}, u32[]{:S(2)}) %all-to-all-start.3) | async-done | bytes 524320 | tf_op jit(solution)/shard_map/while/body/eval_jaxpr/all_to_all | solution.py:34
  348.8 4.7 %all-to-all-start.8 = ((f32[128,1,512]{2,1,0:T(1,128)}), f32[128,1,512]{2,1,0:T(1,128)S(1)}, u32[]{:S(2)}, u32[]{:S(2)}) async-start(f32[128,1,512]{2,1,0:T(1,128)} %copy.157), calls=%async_computation.8 | async-start | bytes 524288 | tf_op jit(solution)/shard_map/all_to_all | solution.py:34
  355.3 9.0 %all-to-all-done.8 = f32[128,1,512]{2,1,0:T(1,128)S(1)} async-done(((f32[128,1,512]{2,1,0:T(1,128)}), f32[128,1,512]{2,1,0:T(1,128)S(1)}, u32[]{:S(2)}, u32[]{:S(2)}) %all-to-all-start.8) | async-done | bytes 262176 | tf_op jit(solution)/shard_map/all_to_all | solution.py:34
  364.4 1.6 convolution_bitcast_fusion.1
  366.3 15.4 %all_to_all.125 = f32[128,1,512]{2,1,0:T(1,128)S(1)} all-to-all(f32[128,1,512]{2,1,0:T(1,128)S(1)} %copy.158), channel_id=1, replica_groups=mesh['dev'=128] {'dev'}, dimensions={0} | all-to-all | bytes 524288 | tf_op jit(solution)/shard_map/all_to_all | solution.py:34
  (166 shorter events, 51.1 us)
Async XLA Ops:
  0.0 32.3 %copy-start = (f32[2,512,512]{2,1,0:T(8,128)S(1)}, f32[2,512,512]{2,1,0:T(8,128)}, u32[]{:S(2)}) copy-start(f32[2,512,512]{2,1,0:T(8,128)} %param.9) | copy-start | bytes 6291460
  10.0 22.3 %all-to-all-start.4 = ((f32[128,1,512]{2,1,0:T(1,128)}), f32[128,1,512]{2,1,0:T(1,128)S(1)}, u32[]{:S(2)}, u32[]{:S(2)}) async-start(f32[128,1,512]{2,1,0:T(1,128)} %all_to_all.86), calls=%async_computation.4 | async-start | bytes 524288 | tf_op jit(solution)/shard_map/all_to_all | solution.py:34
  33.7 15.5 %all-to-all-start.5 = ((f32[128,1,512]{2,1,0:T(1,128)}), f32[128,1,512]{2,1,0:T(1,128)S(1)}, u32[]{:S(2)}, u32[]{:S(2)}) async-start(f32[128,1,512]{2,1,0:T(1,128)} %copy.139), calls=%async_computation.5 | async-start | bytes 524288 | tf_op jit(solution)/shard_map/all_to_all | solution.py:34
  51.4 18.3 %all-to-all-start.6 = ((f32[128,2,512]{2,1,0:T(2,128)}), f32[128,2,512]{2,1,0:T(2,128)S(1)}, u32[]{:S(2)}, u32[]{:S(2)}) async-start(f32[128,2,512]{2,1,0:T(2,128)} %reshape.191), calls=%async_computation.6 | async-start | bytes 1048576 | tf_op jit(solution)/shard_map/all_to_all | solution.py:34
  76.9 18.4 %all-to-all-start.7 = ((f32[128,2,512]{2,1,0:T(2,128)}), f32[128,2,512]{2,1,0:T(2,128)S(1)}, u32[]{:S(2)}, u32[]{:S(2)}) async-start(f32[128,2,512]{2,1,0:T(2,128)} %copy.145), calls=%async_computation.7 | async-start | bytes 1048576 | tf_op jit(solution)/shard_map/all_to_all | solution.py:34
  99.3 15.6 %all-to-all-start = ((f32[128,1,512]{2,1,0:T(1,128)}), f32[128,1,512]{2,1,0:T(1,128)S(1)}, u32[]{:S(2)}, u32[]{:S(2)}) async-start(f32[128,1,512]{2,1,0:T(1,128)} %copy.211), calls=%async_computation | async-start | bytes 524288 | tf_op jit(solution)/shard_map/while/body/eval_jaxpr/all_to_all | solution.py:34
  117.6 15.5 %all-to-all-start.1 = ((f32[128,1,512]{2,1,0:T(1,128)}), f32[128,1,512]{2,1,0:T(1,128)S(1)}, u32[]{:S(2)}, u32[]{:S(2)}) async-start(f32[128,1,512]{2,1,0:T(1,128)} %copy.212), calls=%async_computation.1 | async-start | bytes 524288 | tf_op jit(solution)/shard_map/while/body/eval_jaxpr/all_to_all | solution.py:34
  135.2 18.3 %all-to-all-start.2 = ((f32[128,2,512]{2,1,0:T(2,128)}), f32[128,2,512]{2,1,0:T(2,128)S(1)}, u32[]{:S(2)}, u32[]{:S(2)}) async-start(f32[128,2,512]{2,1,0:T(2,128)} %reshape.260), calls=%async_computation.2 | async-start | bytes 1048576 | tf_op jit(solution)/shard_map/while/body/eval_jaxpr/all_to_all | solution.py:34
  160.8 18.4 %all-to-all-start.3 = ((f32[128,2,512]{2,1,0:T(2,128)}), f32[128,2,512]{2,1,0:T(2,128)S(1)}, u32[]{:S(2)}, u32[]{:S(2)}) async-start(f32[128,2,512]{2,1,0:T(2,128)} %copy.215), calls=%async_computation.3 | async-start | bytes 1048576 | tf_op jit(solution)/shard_map/while/body/eval_jaxpr/all_to_all | solution.py:34
  182.8 15.6 %all-to-all-start = ((f32[128,1,512]{2,1,0:T(1,128)}), f32[128,1,512]{2,1,0:T(1,128)S(1)}, u32[]{:S(2)}, u32[]{:S(2)}) async-start(f32[128,1,512]{2,1,0:T(1,128)} %copy.211), calls=%async_computation | async-start | bytes 524288 | tf_op jit(solution)/shard_map/while/body/eval_jaxpr/all_to_all | solution.py:34
  201.0 15.5 %all-to-all-start.1 = ((f32[128,1,512]{2,1,0:T(1,128)}), f32[128,1,512]{2,1,0:T(1,128)S(1)}, u32[]{:S(2)}, u32[]{:S(2)}) async-start(f32[128,1,512]{2,1,0:T(1,128)} %copy.212), calls=%async_computation.1 | async-start | bytes 524288 | tf_op jit(solution)/shard_map/while/body/eval_jaxpr/all_to_all | solution.py:34
  218.7 18.3 %all-to-all-start.2 = ((f32[128,2,512]{2,1,0:T(2,128)}), f32[128,2,512]{2,1,0:T(2,128)S(1)}, u32[]{:S(2)}, u32[]{:S(2)}) async-start(f32[128,2,512]{2,1,0:T(2,128)} %reshape.260), calls=%async_computation.2 | async-start | bytes 1048576 | tf_op jit(solution)/shard_map/while/body/eval_jaxpr/all_to_all | solution.py:34
  244.2 18.4 %all-to-all-start.3 = ((f32[128,2,512]{2,1,0:T(2,128)}), f32[128,2,512]{2,1,0:T(2,128)S(1)}, u32[]{:S(2)}, u32[]{:S(2)}) async-start(f32[128,2,512]{2,1,0:T(2,128)} %copy.215), calls=%async_computation.3 | async-start | bytes 1048576 | tf_op jit(solution)/shard_map/while/body/eval_jaxpr/all_to_all | solution.py:34
  266.3 15.6 %all-to-all-start = ((f32[128,1,512]{2,1,0:T(1,128)}), f32[128,1,512]{2,1,0:T(1,128)S(1)}, u32[]{:S(2)}, u32[]{:S(2)}) async-start(f32[128,1,512]{2,1,0:T(1,128)} %copy.211), calls=%async_computation | async-start | bytes 524288 | tf_op jit(solution)/shard_map/while/body/eval_jaxpr/all_to_all | solution.py:34
  284.5 15.5 %all-to-all-start.1 = ((f32[128,1,512]{2,1,0:T(1,128)}), f32[128,1,512]{2,1,0:T(1,128)S(1)}, u32[]{:S(2)}, u32[]{:S(2)}) async-start(f32[128,1,512]{2,1,0:T(1,128)} %copy.212), calls=%async_computation.1 | async-start | bytes 524288 | tf_op jit(solution)/shard_map/while/body/eval_jaxpr/all_to_all | solution.py:34
  302.2 18.3 %all-to-all-start.2 = ((f32[128,2,512]{2,1,0:T(2,128)}), f32[128,2,512]{2,1,0:T(2,128)S(1)}, u32[]{:S(2)}, u32[]{:S(2)}) async-start(f32[128,2,512]{2,1,0:T(2,128)} %reshape.260), calls=%async_computation.2 | async-start | bytes 1048576 | tf_op jit(solution)/shard_map/while/body/eval_jaxpr/all_to_all | solution.py:34
  327.7 18.4 %all-to-all-start.3 = ((f32[128,2,512]{2,1,0:T(2,128)}), f32[128,2,512]{2,1,0:T(2,128)S(1)}, u32[]{:S(2)}, u32[]{:S(2)}) async-start(f32[128,2,512]{2,1,0:T(2,128)} %copy.215), calls=%async_computation.3 | async-start | bytes 1048576 | tf_op jit(solution)/shard_map/while/body/eval_jaxpr/all_to_all | solution.py:34
  348.8 15.6 %all-to-all-start.8 = ((f32[128,1,512]{2,1,0:T(1,128)}), f32[128,1,512]{2,1,0:T(1,128)S(1)}, u32[]{:S(2)}, u32[]{:S(2)}) async-start(f32[128,1,512]{2,1,0:T(1,128)} %copy.157), calls=%async_computation.8 | async-start | bytes 524288 | tf_op jit(solution)/shard_map/all_to_all | solution.py:34

commit v4 on v3

--- a/solution.py
+++ b/solution.py
@@ -7,7 +7,7 @@
 ACTIVE = 4
 
 product_precision = lax.Precision.HIGH
-select_precision = lax.Precision.HIGHEST
+select_precision = lax.Precision.HIGH
 
 
 def prefix_count(mask):

time: 385 us -> 385 us (level)
  no operation moved by 1% of the time
where the time goes in v4:
time: 385 us; the launch traced here: 383 us
  waiting for transfers between devices  165 us (43%)
  starting transfers between devices  86.8 us (23%)
  local copies, waits for them, and re-layouts  61.4 us (16%)
  matrix products  32.1 us (8%)
  blocking collectives  15.4 us (4%)
  other arithmetic  11.2 us (3%)
  loops' own time  7.07 us (2%)
  between operations  4.33 us (1%)
    all_to_all x17, waiting for transfers between devices, a2a(): return lax.all_to_all(x, 'dev', split_axis=0, concat_axis=0, tiled=True)  165 us
    all_to_all x17, starting transfers between devices, a2a(): return lax.all_to_all(x, 'dev', split_axis=0, concat_axis=0, tiled=True)  86.8 us
    gather x4, local copies, waits for them, and re-layouts, tiles(): jnp.take(factor_tiles, at_level(slot_tile, current), axis=0, mode='clip')  24.5 us
    dot_general x4, matrix products, tiles(): jnp.einsum('rtb,tbc->rtc', sources, factors, precision=product_precision,...  23 us
    all_to_all x1, blocking collectives, a2a(): return lax.all_to_all(x, 'dev', split_axis=0, concat_axis=0, tiled=True)  15.4 us
    all_to_all x10, local copies, waits for them, and re-layouts, a2a(): return lax.all_to_all(x, 'dev', split_axis=0, concat_axis=0, tiled=True)  8.94 us
  transfers between devices with their start and end apart: 17, of which 17 were waited for; matrix products, arithmetic and copies ran while one was open for 8% of the time, Pallas kernels for 0%

profile of v4, /device:TPU:1, one launch (start us, length us, event | category | flops | bytes accessed | tf_op | source)
XLA Modules:
  0.0 382.9 jit_solution(85535530076484752)
XLA Ops:
  10.0 11.5 %all-to-all-start.4 = ((f32[128,1,512]{2,1,0:T(1,128)}), f32[128,1,512]{2,1,0:T(1,128)S(1)}, u32[]{:S(2)}, u32[]{:S(2)}) async-start(f32[128,1,512]{2,1,0:T(1,128)} %all_to_all.86), calls=%async_computation.4 | async-start | bytes 524288 | tf_op jit(solution)/shard_map/all_to_all | solution.py:34
  24.0 8.3 %all-to-all-done.4 = f32[128,1,512]{2,1,0:T(1,128)S(1)} async-done(((f32[128,1,512]{2,1,0:T(1,128)}), f32[128,1,512]{2,1,0:T(1,128)S(1)}, u32[]{:S(2)}, u32[]{:S(2)}) %all-to-all-start.4) | async-done | bytes 262176 | tf_op jit(solution)/shard_map/all_to_all | solution.py:34
  33.7 4.7 %all-to-all-start.5 = ((f32[128,1,512]{2,1,0:T(1,128)}), f32[128,1,512]{2,1,0:T(1,128)S(1)}, u32[]{:S(2)}, u32[]{:S(2)}) async-start(f32[128,1,512]{2,1,0:T(1,128)} %copy.139), calls=%async_computation.5 | async-start | bytes 524288 | tf_op jit(solution)/shard_map/all_to_all | solution.py:34
  39.0 10.3 %all-to-all-done.5 = f32[128,1,512]{2,1,0:T(1,128)S(1)} async-done(((f32[128,1,512]{2,1,0:T(1,128)}), f32[128,1,512]{2,1,0:T(1,128)S(1)}, u32[]{:S(2)}, u32[]{:S(2)}) %all-to-all-start.5) | async-done | bytes 262176 | tf_op jit(solution)/shard_map/all_to_all | solution.py:34
  51.4 4.7 %all-to-all-start.6 = ((f32[128,2,512]{2,1,0:T(2,128)}), f32[128,2,512]{2,1,0:T(2,128)S(1)}, u32[]{:S(2)}, u32[]{:S(2)}) async-start(f32[128,2,512]{2,1,0:T(2,128)} %reshape.191), calls=%async_computation.6 | async-start | bytes 1048576 | tf_op jit(solution)/shard_map/all_to_all | solution.py:34
  56.1 6.1 %gather_fusion.2 = f32[4,512,512]{2,1,0:T(8,128)} fusion(f32[8,512,512]{2,1,0:T(8,128)} %param.10, s32[1024]{0:T(1024)S(1)} %pad_clamp_fusion.3), kind=kCustom, calls=%fused_computation.2 | custom fusion | bytes 8388624 | tf_op jit(solution)/shard_map/jit(_take)/gather | solution.py:105
  62.6 7.1 %all-to-all-done.6 = f32[128,2,512]{2,1,0:T(2,128)S(1)} async-done(((f32[128,2,512]{2,1,0:T(2,128)}), f32[128,2,512]{2,1,0:T(2,128)S(1)}, u32[]{:S(2)}, u32[]{:S(2)}) %all-to-all-start.6) | async-done | bytes 524320 | tf_op jit(solution)/shard_map/all_to_all | solution.py:34
  70.1 5.8 %select_reduce_fusion.4 = (f32[512,128]{1,0:T(8,128)S(1)}, f32[512,128]{1,0:T(8,128)S(1)}) fusion(pred[4]{0:T(512)(128)(4,1)S(1)} %get-tuple-element.571, pred[4]{0:T(512)(128)(4,1)S(1)} %get-tuple-element.572, f32[4,512,512]{2,1,0:T(8,128)} %gather_fusion.2, f32[128,512]{1,0:T(8,128)S(1)} %bitcast.145, f32[128,512]{1,0:T(8,128)S(1)} %bitcast.144, ...), kind=kOutput, calls=%fused_computation.57 | convolution fusion | flops 806486016 | bytes 5242892 | tf_op jit(solution)/shard_map/rtb,tbc->rtc/dot_general | solution.py:108
  76.9 4.7 %all-to-all-start.7 = ((f32[128,2,512]{2,1,0:T(2,128)}), f32[128,2,512]{2,1,0:T(2,128)S(1)}, u32[]{:S(2)}, u32[]{:S(2)}) async-start(f32[128,2,512]{2,1,0:T(2,128)} %copy.145), calls=%async_computation.7 | async-start | bytes 1048576 | tf_op jit(solution)/shard_map/all_to_all | solution.py:34
  81.7 13.6 %all-to-all-done.7 = f32[128,2,512]{2,1,0:T(2,128)S(1)} async-done(((f32[128,2,512]{2,1,0:T(2,128)}), f32[128,2,512]{2,1,0:T(2,128)S(1)}, u32[]{:S(2)}, u32[]{:S(2)}) %all-to-all-start.7) | async-done | bytes 524320 | tf_op jit(solution)/shard_map/all_to_all | solution.py:34
  95.8 250.1 %while.22 = (s32[]{:T(128)}, f32[128,2,512]{2,1,0:T(2,128)S(1)}, f32[256,512]{1,0:T(8,128)S(1)}, s32[256]{0:T(256)S(1)}, f32[128,2,512]{2,1,0:T(2,128)S(1)}, /*i...) while((s32[]{:T(128)}, f32[128,2,512]{2,1,0:T(2,128)S(1)}, ...), condition=%wide.region_24.25_spmd.clone, body=%wide.region_20.24_spmd.clone.sunk | while | flops 1310820352 | bytes 35675224 | solution.py:128
  99.0 4.7 %all-to-all-start = ((f32[128,1,512]{2,1,0:T(1,128)}), f32[128,1,512]{2,1,0:T(1,128)S(1)}, u32[]{:S(2)}, u32[]{:S(2)}) async-start(f32[128,1,512]{2,1,0:T(1,128)} %copy.211), calls=%async_computation | async-start | bytes 524288 | tf_op jit(solution)/shard_map/while/body/eval_jaxpr/all_to_all | solution.py:34
  106.5 8.2 %all-to-all-done = f32[128,1,512]{2,1,0:T(1,128)S(1)} async-done(((f32[128,1,512]{2,1,0:T(1,128)}), f32[128,1,512]{2,1,0:T(1,128)S(1)}, u32[]{:S(2)}, u32[]{:S(2)}) %all-to-all-start) | async-done | bytes 262176 | tf_op jit(solution)/shard_map/while/body/eval_jaxpr/all_to_all | solution.py:34
  114.6 1.6 convolution_bitcast_fusion.4
  117.2 4.7 %all-to-all-start.1 = ((f32[128,1,512]{2,1,0:T(1,128)}), f32[128,1,512]{2,1,0:T(1,128)S(1)}, u32[]{:S(2)}, u32[]{:S(2)}) async-start(f32[128,1,512]{2,1,0:T(1,128)} %copy.212), calls=%async_computation.1 | async-start | bytes 524288 | tf_op jit(solution)/shard_map/while/body/eval_jaxpr/all_to_all | solution.py:34
  122.2 10.5 %all-to-all-done.1 = f32[128,1,512]{2,1,0:T(1,128)S(1)} async-done(((f32[128,1,512]{2,1,0:T(1,128)}), f32[128,1,512]{2,1,0:T(1,128)S(1)}, u32[]{:S(2)}, u32[]{:S(2)}) %all-to-all-start.1) | async-done | bytes 262176 | tf_op jit(solution)/shard_map/while/body/eval_jaxpr/all_to_all | solution.py:34
  134.9 4.7 %all-to-all-start.2 = ((f32[128,2,512]{2,1,0:T(2,128)}), f32[128,2,512]{2,1,0:T(2,128)S(1)}, u32[]{:S(2)}, u32[]{:S(2)}) async-start(f32[128,2,512]{2,1,0:T(2,128)} %reshape.260), calls=%async_computation.2 | async-start | bytes 1048576 | tf_op jit(solution)/shard_map/while/body/eval_jaxpr/all_to_all | solution.py:34
  139.6 6.1 %gather_fusion = f32[4,512,512]{2,1,0:T(8,128)} fusion(f32[8,512,512]{2,1,0:T(8,128)} %get-tuple-element.799, s32[1024]{0:T(1024)S(1)} %pad_clamp_fusion.6), kind=kCustom, calls=%fused_computation.clone.clone.1 | custom fusion | bytes 8388624 | tf_op jit(solution)/shard_map/while/body/eval_jaxpr/jit(_take)/gather | solution.py:105
  145.9 7.2 %all-to-all-done.2 = f32[128,2,512]{2,1,0:T(2,128)S(1)} async-done(((f32[128,2,512]{2,1,0:T(2,128)}), f32[128,2,512]{2,1,0:T(2,128)S(1)}, u32[]{:S(2)}, u32[]{:S(2)}) %all-to-all-start.2) | async-done | bytes 524320 | tf_op jit(solution)/shard_map/while/body/eval_jaxpr/all_to_all | solution.py:34
  153.6 5.8 %select_reduce_fusion.19 = (f32[512,128]{1,0:T(8,128)S(1)}, f32[512,128]{1,0:T(8,128)S(1)}) fusion(pred[4]{0:T(512)(128)(4,1)S(1)} %get-tuple-element.741, pred[4]{0:T(512)(128)(4,1)S(1)} %get-tuple-element.742, f32[4,512,512]{2,1,0:T(8,128)} %gather_fusion, f32[128,512]{1,0:T(8,128)S(1)} %get-tuple-element.746, ...), kind=kOutput, calls=%fused_computation.10.clone.1 | convolution fusion | flops 806486016 | bytes 5242892 | tf_op jit(solution)/shard_map/while/body/eval_jaxpr/rtb,tbc->rtc/dot_general | solution.py:108
  160.4 4.7 %all-to-all-start.3 = ((f32[128,2,512]{2,1,0:T(2,128)}), f32[128,2,512]{2,1,0:T(2,128)S(1)}, u32[]{:S(2)}, u32[]{:S(2)}) async-start(f32[128,2,512]{2,1,0:T(2,128)} %copy.215), calls=%async_computation.3 | async-start | bytes 1048576 | tf_op jit(solution)/shard_map/while/body/eval_jaxpr/all_to_all | solution.py:34
  165.9 12.9 %all-to-all-done.3 = f32[128,2,512]{2,1,0:T(2,128)S(1)} async-done(((f32[128,2,512]{2,1,0:T(2,128)}), f32[128,2,512]{2,1,0:T(2,128)S(1)}, u32[]{:S(2)}, u32[]{:S(2)}) %all-to-all-start.3) | async-done | bytes 524320 | tf_op jit(solution)/shard_map/while/body/eval_jaxpr/all_to_all | solution.py:34
  182.3 4.7 %all-to-all-start = ((f32[128,1,512]{2,1,0:T(1,128)}), f32[128,1,512]{2,1,0:T(1,128)S(1)}, u32[]{:S(2)}, u32[]{:S(2)}) async-start(f32[128,1,512]{2,1,0:T(1,128)} %copy.211), calls=%async_computation | async-start | bytes 524288 | tf_op jit(solution)/shard_map/while/body/eval_jaxpr/all_to_all | solution.py:34
  189.8 8.2 %all-to-all-done = f32[128,1,512]{2,1,0:T(1,128)S(1)} async-done(((f32[128,1,512]{2,1,0:T(1,128)}), f32[128,1,512]{2,1,0:T(1,128)S(1)}, u32[]{:S(2)}, u32[]{:S(2)}) %all-to-all-start) | async-done | bytes 262176 | tf_op jit(solution)/shard_map/while/body/eval_jaxpr/all_to_all | solution.py:34
  197.9 1.6 convolution_bitcast_fusion.4
  200.5 4.7 %all-to-all-start.1 = ((f32[128,1,512]{2,1,0:T(1,128)}), f32[128,1,512]{2,1,0:T(1,128)S(1)}, u32[]{:S(2)}, u32[]{:S(2)}) async-start(f32[128,1,512]{2,1,0:T(1,128)} %copy.212), calls=%async_computation.1 | async-start | bytes 524288 | tf_op jit(solution)/shard_map/while/body/eval_jaxpr/all_to_all | solution.py:34
  205.5 10.5 %all-to-all-done.1 = f32[128,1,512]{2,1,0:T(1,128)S(1)} async-done(((f32[128,1,512]{2,1,0:T(1,128)}), f32[128,1,512]{2,1,0:T(1,128)S(1)}, u32[]{:S(2)}, u32[]{:S(2)}) %all-to-all-start.1) | async-done | bytes 262176 | tf_op jit(solution)/shard_map/while/body/eval_jaxpr/all_to_all | solution.py:34
  218.2 4.7 %all-to-all-start.2 = ((f32[128,2,512]{2,1,0:T(2,128)}), f32[128,2,512]{2,1,0:T(2,128)S(1)}, u32[]{:S(2)}, u32[]{:S(2)}) async-start(f32[128,2,512]{2,1,0:T(2,128)} %reshape.260), calls=%async_computation.2 | async-start | bytes 1048576 | tf_op jit(solution)/shard_map/while/body/eval_jaxpr/all_to_all | solution.py:34
  222.9 6.1 %gather_fusion = f32[4,512,512]{2,1,0:T(8,128)} fusion(f32[8,512,512]{2,1,0:T(8,128)} %get-tuple-element.799, s32[1024]{0:T(1024)S(1)} %pad_clamp_fusion.6), kind=kCustom, calls=%fused_computation.clone.clone.1 | custom fusion | bytes 8388624 | tf_op jit(solution)/shard_map/while/body/eval_jaxpr/jit(_take)/gather | solution.py:105
  229.2 7.2 %all-to-all-done.2 = f32[128,2,512]{2,1,0:T(2,128)S(1)} async-done(((f32[128,2,512]{2,1,0:T(2,128)}), f32[128,2,512]{2,1,0:T(2,128)S(1)}, u32[]{:S(2)}, u32[]{:S(2)}) %all-to-all-start.2) | async-done | bytes 524320 | tf_op jit(solution)/shard_map/while/body/eval_jaxpr/all_to_all | solution.py:34
  236.9 5.8 %select_reduce_fusion.19 = (f32[512,128]{1,0:T(8,128)S(1)}, f32[512,128]{1,0:T(8,128)S(1)}) fusion(pred[4]{0:T(512)(128)(4,1)S(1)} %get-tuple-element.741, pred[4]{0:T(512)(128)(4,1)S(1)} %get-tuple-element.742, f32[4,512,512]{2,1,0:T(8,128)} %gather_fusion, f32[128,512]{1,0:T(8,128)S(1)} %get-tuple-element.746, ...), kind=kOutput, calls=%fused_computation.10.clone.1 | convolution fusion | flops 806486016 | bytes 5242892 | tf_op jit(solution)/shard_map/while/body/eval_jaxpr/rtb,tbc->rtc/dot_general | solution.py:108
  243.7 4.7 %all-to-all-start.3 = ((f32[128,2,512]{2,1,0:T(2,128)}), f32[128,2,512]{2,1,0:T(2,128)S(1)}, u32[]{:S(2)}, u32[]{:S(2)}) async-start(f32[128,2,512]{2,1,0:T(2,128)} %copy.215), calls=%async_computation.3 | async-start | bytes 1048576 | tf_op jit(solution)/shard_map/while/body/eval_jaxpr/all_to_all | solution.py:34
  249.2 12.9 %all-to-all-done.3 = f32[128,2,512]{2,1,0:T(2,128)S(1)} async-done(((f32[128,2,512]{2,1,0:T(2,128)}), f32[128,2,512]{2,1,0:T(2,128)S(1)}, u32[]{:S(2)}, u32[]{:S(2)}) %all-to-all-start.3) | async-done | bytes 524320 | tf_op jit(solution)/shard_map/while/body/eval_jaxpr/all_to_all | solution.py:34
  265.6 4.7 %all-to-all-start = ((f32[128,1,512]{2,1,0:T(1,128)}), f32[128,1,512]{2,1,0:T(1,128)S(1)}, u32[]{:S(2)}, u32[]{:S(2)}) async-start(f32[128,1,512]{2,1,0:T(1,128)} %copy.211), calls=%async_computation | async-start | bytes 524288 | tf_op jit(solution)/shard_map/while/body/eval_jaxpr/all_to_all | solution.py:34
  273.1 8.2 %all-to-all-done = f32[128,1,512]{2,1,0:T(1,128)S(1)} async-done(((f32[128,1,512]{2,1,0:T(1,128)}), f32[128,1,512]{2,1,0:T(1,128)S(1)}, u32[]{:S(2)}, u32[]{:S(2)}) %all-to-all-start) | async-done | bytes 262176 | tf_op jit(solution)/shard_map/while/body/eval_jaxpr/all_to_all | solution.py:34
  281.2 1.6 convolution_bitcast_fusion.4
  283.8 4.7 %all-to-all-start.1 = ((f32[128,1,512]{2,1,0:T(1,128)}), f32[128,1,512]{2,1,0:T(1,128)S(1)}, u32[]{:S(2)}, u32[]{:S(2)}) async-start(f32[128,1,512]{2,1,0:T(1,128)} %copy.212), calls=%async_computation.1 | async-start | bytes 524288 | tf_op jit(solution)/shard_map/while/body/eval_jaxpr/all_to_all | solution.py:34
  288.8 10.5 %all-to-all-done.1 = f32[128,1,512]{2,1,0:T(1,128)S(1)} async-done(((f32[128,1,512]{2,1,0:T(1,128)}), f32[128,1,512]{2,1,0:T(1,128)S(1)}, u32[]{:S(2)}, u32[]{:S(2)}) %all-to-all-start.1) | async-done | bytes 262176 | tf_op jit(solution)/shard_map/while/body/eval_jaxpr/all_to_all | solution.py:34
  301.5 4.7 %all-to-all-start.2 = ((f32[128,2,512]{2,1,0:T(2,128)}), f32[128,2,512]{2,1,0:T(2,128)S(1)}, u32[]{:S(2)}, u32[]{:S(2)}) async-start(f32[128,2,512]{2,1,0:T(2,128)} %reshape.260), calls=%async_computation.2 | async-start | bytes 1048576 | tf_op jit(solution)/shard_map/while/body/eval_jaxpr/all_to_all | solution.py:34
  306.2 6.1 %gather_fusion = f32[4,512,512]{2,1,0:T(8,128)} fusion(f32[8,512,512]{2,1,0:T(8,128)} %get-tuple-element.799, s32[1024]{0:T(1024)S(1)} %pad_clamp_fusion.6), kind=kCustom, calls=%fused_computation.clone.clone.1 | custom fusion | bytes 8388624 | tf_op jit(solution)/shard_map/while/body/eval_jaxpr/jit(_take)/gather | solution.py:105
  312.5 7.2 %all-to-all-done.2 = f32[128,2,512]{2,1,0:T(2,128)S(1)} async-done(((f32[128,2,512]{2,1,0:T(2,128)}), f32[128,2,512]{2,1,0:T(2,128)S(1)}, u32[]{:S(2)}, u32[]{:S(2)}) %all-to-all-start.2) | async-done | bytes 524320 | tf_op jit(solution)/shard_map/while/body/eval_jaxpr/all_to_all | solution.py:34
  320.2 5.8 %select_reduce_fusion.19 = (f32[512,128]{1,0:T(8,128)S(1)}, f32[512,128]{1,0:T(8,128)S(1)}) fusion(pred[4]{0:T(512)(128)(4,1)S(1)} %get-tuple-element.741, pred[4]{0:T(512)(128)(4,1)S(1)} %get-tuple-element.742, f32[4,512,512]{2,1,0:T(8,128)} %gather_fusion, f32[128,512]{1,0:T(8,128)S(1)} %get-tuple-element.746, ...), kind=kOutput, calls=%fused_computation.10.clone.1 | convolution fusion | flops 806486016 | bytes 5242892 | tf_op jit(solution)/shard_map/while/body/eval_jaxpr/rtb,tbc->rtc/dot_general | solution.py:108
  327.0 4.7 %all-to-all-start.3 = ((f32[128,2,512]{2,1,0:T(2,128)}), f32[128,2,512]{2,1,0:T(2,128)S(1)}, u32[]{:S(2)}, u32[]{:S(2)}) async-start(f32[128,2,512]{2,1,0:T(2,128)} %copy.215), calls=%async_computation.3 | async-start | bytes 1048576 | tf_op jit(solution)/shard_map/while/body/eval_jaxpr/all_to_all | solution.py:34
  332.5 12.9 %all-to-all-done.3 = f32[128,2,512]{2,1,0:T(2,128)S(1)} async-done(((f32[128,2,512]{2,1,0:T(2,128)}), f32[128,2,512]{2,1,0:T(2,128)S(1)}, u32[]{:S(2)}, u32[]{:S(2)}) %all-to-all-start.3) | async-done | bytes 524320 | tf_op jit(solution)/shard_map/while/body/eval_jaxpr/all_to_all | solution.py:34
  348.0 4.7 %all-to-all-start.8 = ((f32[128,1,512]{2,1,0:T(1,128)}), f32[128,1,512]{2,1,0:T(1,128)S(1)}, u32[]{:S(2)}, u32[]{:S(2)}) async-start(f32[128,1,512]{2,1,0:T(1,128)} %copy.157), calls=%async_computation.8 | async-start | bytes 524288 | tf_op jit(solution)/shard_map/all_to_all | solution.py:34
  354.6 9.1 %all-to-all-done.8 = f32[128,1,512]{2,1,0:T(1,128)S(1)} async-done(((f32[128,1,512]{2,1,0:T(1,128)}), f32[128,1,512]{2,1,0:T(1,128)S(1)}, u32[]{:S(2)}, u32[]{:S(2)}) %all-to-all-start.8) | async-done | bytes 262176 | tf_op jit(solution)/shard_map/all_to_all | solution.py:34
  363.6 1.6 convolution_bitcast_fusion.1
  365.6 15.4 %all_to_all.125 = f32[128,1,512]{2,1,0:T(1,128)S(1)} all-to-all(f32[128,1,512]{2,1,0:T(1,128)S(1)} %copy.158), channel_id=1, replica_groups=mesh['dev'=128] {'dev'}, dimensions={0} | all-to-all | bytes 524288 | tf_op jit(solution)/shard_map/all_to_all | solution.py:34
  (166 shorter events, 50.6 us)
Async XLA Ops:
  0.0 32.3 %copy-start = (f32[2,512,512]{2,1,0:T(8,128)S(1)}, f32[2,512,512]{2,1,0:T(8,128)}, u32[]{:S(2)}) copy-start(f32[2,512,512]{2,1,0:T(8,128)} %param.9) | copy-start | bytes 6291460
  10.0 22.3 %all-to-all-start.4 = ((f32[128,1,512]{2,1,0:T(1,128)}), f32[128,1,512]{2,1,0:T(1,128)S(1)}, u32[]{:S(2)}, u32[]{:S(2)}) async-start(f32[128,1,512]{2,1,0:T(1,128)} %all_to_all.86), calls=%async_computation.4 | async-start | bytes 524288 | tf_op jit(solution)/shard_map/all_to_all | solution.py:34
  33.7 15.5 %all-to-all-start.5 = ((f32[128,1,512]{2,1,0:T(1,128)}), f32[128,1,512]{2,1,0:T(1,128)S(1)}, u32[]{:S(2)}, u32[]{:S(2)}) async-start(f32[128,1,512]{2,1,0:T(1,128)} %copy.139), calls=%async_computation.5 | async-start | bytes 524288 | tf_op jit(solution)/shard_map/all_to_all | solution.py:34
  51.4 18.3 %all-to-all-start.6 = ((f32[128,2,512]{2,1,0:T(2,128)}), f32[128,2,512]{2,1,0:T(2,128)S(1)}, u32[]{:S(2)}, u32[]{:S(2)}) async-start(f32[128,2,512]{2,1,0:T(2,128)} %reshape.191), calls=%async_computation.6 | async-start | bytes 1048576 | tf_op jit(solution)/shard_map/all_to_all | solution.py:34
  76.9 18.4 %all-to-all-start.7 = ((f32[128,2,512]{2,1,0:T(2,128)}), f32[128,2,512]{2,1,0:T(2,128)S(1)}, u32[]{:S(2)}, u32[]{:S(2)}) async-start(f32[128,2,512]{2,1,0:T(2,128)} %copy.145), calls=%async_computation.7 | async-start | bytes 1048576 | tf_op jit(solution)/shard_map/all_to_all | solution.py:34
  99.0 15.6 %all-to-all-start = ((f32[128,1,512]{2,1,0:T(1,128)}), f32[128,1,512]{2,1,0:T(1,128)S(1)}, u32[]{:S(2)}, u32[]{:S(2)}) async-start(f32[128,1,512]{2,1,0:T(1,128)} %copy.211), calls=%async_computation | async-start | bytes 524288 | tf_op jit(solution)/shard_map/while/body/eval_jaxpr/all_to_all | solution.py:34
  117.2 15.5 %all-to-all-start.1 = ((f32[128,1,512]{2,1,0:T(1,128)}), f32[128,1,512]{2,1,0:T(1,128)S(1)}, u32[]{:S(2)}, u32[]{:S(2)}) async-start(f32[128,1,512]{2,1,0:T(1,128)} %copy.212), calls=%async_computation.1 | async-start | bytes 524288 | tf_op jit(solution)/shard_map/while/body/eval_jaxpr/all_to_all | solution.py:34
  134.9 18.3 %all-to-all-start.2 = ((f32[128,2,512]{2,1,0:T(2,128)}), f32[128,2,512]{2,1,0:T(2,128)S(1)}, u32[]{:S(2)}, u32[]{:S(2)}) async-start(f32[128,2,512]{2,1,0:T(2,128)} %reshape.260), calls=%async_computation.2 | async-start | bytes 1048576 | tf_op jit(solution)/shard_map/while/body/eval_jaxpr/all_to_all | solution.py:34
  160.4 18.4 %all-to-all-start.3 = ((f32[128,2,512]{2,1,0:T(2,128)}), f32[128,2,512]{2,1,0:T(2,128)S(1)}, u32[]{:S(2)}, u32[]{:S(2)}) async-start(f32[128,2,512]{2,1,0:T(2,128)} %copy.215), calls=%async_computation.3 | async-start | bytes 1048576 | tf_op jit(solution)/shard_map/while/body/eval_jaxpr/all_to_all | solution.py:34
  182.3 15.6 %all-to-all-start = ((f32[128,1,512]{2,1,0:T(1,128)}), f32[128,1,512]{2,1,0:T(1,128)S(1)}, u32[]{:S(2)}, u32[]{:S(2)}) async-start(f32[128,1,512]{2,1,0:T(1,128)} %copy.211), calls=%async_computation | async-start | bytes 524288 | tf_op jit(solution)/shard_map/while/body/eval_jaxpr/all_to_all | solution.py:34
  200.5 15.5 %all-to-all-start.1 = ((f32[128,1,512]{2,1,0:T(1,128)}), f32[128,1,512]{2,1,0:T(1,128)S(1)}, u32[]{:S(2)}, u32[]{:S(2)}) async-start(f32[128,1,512]{2,1,0:T(1,128)} %copy.212), calls=%async_computation.1 | async-start | bytes 524288 | tf_op jit(solution)/shard_map/while/body/eval_jaxpr/all_to_all | solution.py:34
  218.2 18.3 %all-to-all-start.2 = ((f32[128,2,512]{2,1,0:T(2,128)}), f32[128,2,512]{2,1,0:T(2,128)S(1)}, u32[]{:S(2)}, u32[]{:S(2)}) async-start(f32[128,2,512]{2,1,0:T(2,128)} %reshape.260), calls=%async_computation.2 | async-start | bytes 1048576 | tf_op jit(solution)/shard_map/while/body/eval_jaxpr/all_to_all | solution.py:34
  243.7 18.4 %all-to-all-start.3 = ((f32[128,2,512]{2,1,0:T(2,128)}), f32[128,2,512]{2,1,0:T(2,128)S(1)}, u32[]{:S(2)}, u32[]{:S(2)}) async-start(f32[128,2,512]{2,1,0:T(2,128)} %copy.215), calls=%async_computation.3 | async-start | bytes 1048576 | tf_op jit(solution)/shard_map/while/body/eval_jaxpr/all_to_all | solution.py:34
  265.6 15.6 %all-to-all-start = ((f32[128,1,512]{2,1,0:T(1,128)}), f32[128,1,512]{2,1,0:T(1,128)S(1)}, u32[]{:S(2)}, u32[]{:S(2)}) async-start(f32[128,1,512]{2,1,0:T(1,128)} %copy.211), calls=%async_computation | async-start | bytes 524288 | tf_op jit(solution)/shard_map/while/body/eval_jaxpr/all_to_all | solution.py:34
  283.8 15.5 %all-to-all-start.1 = ((f32[128,1,512]{2,1,0:T(1,128)}), f32[128,1,512]{2,1,0:T(1,128)S(1)}, u32[]{:S(2)}, u32[]{:S(2)}) async-start(f32[128,1,512]{2,1,0:T(1,128)} %copy.212), calls=%async_computation.1 | async-start | bytes 524288 | tf_op jit(solution)/shard_map/while/body/eval_jaxpr/all_to_all | solution.py:34
  301.5 18.3 %all-to-all-start.2 = ((f32[128,2,512]{2,1,0:T(2,128)}), f32[128,2,512]{2,1,0:T(2,128)S(1)}, u32[]{:S(2)}, u32[]{:S(2)}) async-start(f32[128,2,512]{2,1,0:T(2,128)} %reshape.260), calls=%async_computation.2 | async-start | bytes 1048576 | tf_op jit(solution)/shard_map/while/body/eval_jaxpr/all_to_all | solution.py:34
  327.0 18.4 %all-to-all-start.3 = ((f32[128,2,512]{2,1,0:T(2,128)}), f32[128,2,512]{2,1,0:T(2,128)S(1)}, u32[]{:S(2)}, u32[]{:S(2)}) async-start(f32[128,2,512]{2,1,0:T(2,128)} %copy.215), calls=%async_computation.3 | async-start | bytes 1048576 | tf_op jit(solution)/shard_map/while/body/eval_jaxpr/all_to_all | solution.py:34
  348.0 15.6 %all-to-all-start.8 = ((f32[128,1,512]{2,1,0:T(1,128)}), f32[128,1,512]{2,1,0:T(1,128)S(1)}, u32[]{:S(2)}, u32[]{:S(2)}) async-start(f32[128,1,512]{2,1,0:T(1,128)} %copy.157), calls=%async_computation.8 | async-start | bytes 524288 | tf_op jit(solution)/shard_map/all_to_all | solution.py:34

commit v5 on v3

--- a/solution.py
+++ b/solution.py
@@ -120,16 +120,17 @@
         update, coming, coming_targets, solution = carry
         residue, update = residual(current, update, coming, coming_targets)
         returned = solve(current, residue)
-        solution = jnp.where(at_level(owner_at, current)[:, :, None], returned[:, None, :], solution)
+        solution = jnp.where(at_level(row_at, current)[:, None], jnp.repeat(returned, per_owner, axis=0), solution)
         coming, coming_targets = tiles(current, returned)
         return update, coming, coming_targets, solution
 
-    solution = jnp.broadcast_to(first[:, None, :], (devices, per_owner, block))
+    row_at = owner_at.reshape(LEVELS, supernodes)
+    solution = jnp.repeat(first, per_owner, axis=0)
     update, coming, coming_targets, solution = lax.fori_loop(
         1, tile_levels, middle, (update, coming, coming_targets, solution))
     residue, _ = residual(LEVELS - 1, update, coming, coming_targets)
     last = solve(LEVELS - 1, residue)
-    solution = jnp.where(owner_at[LEVELS - 1][:, :, None], last[:, None, :], solution)
+    solution = jnp.where(row_at[LEVELS - 1][:, None], jnp.repeat(last, per_owner, axis=0), solution)
     return solution.reshape(1, supernodes, block)
 
 

time: 385 us -> 387 us (level)
  blocking collectives: 15.4 us -> 0 us
  waiting for transfers between devices: 165 us -> 175 us
  starting transfers between devices: 86.8 us -> 92.4 us
    all_to_all x1 -> x0, blocking collectives: 15.4 us -> none  [a2a(): return lax.all_to_all(x, 'dev', split_axis=0, concat_axis=0, tiled=True)]
    all_to_all x17 -> x18, waiting for transfers between devices: 165 us -> 175 us  [a2a(): return lax.all_to_all(x, 'dev', split_axis=0, concat_axis=0, tiled=True)]
    all_to_all x17 -> x18, starting transfers between devices: 86.8 us -> 92.4 us  [a2a(): return lax.all_to_all(x, 'dev', split_axis=0, concat_axis=0, tiled=True)]
  transfers between devices with their start and end apart: 17 -> 18, of which waited for: 17 -> 18; matrix products, arithmetic and copies ran while one was open for 8% -> 8% of each run, Pallas kernels for 0% -> 0%
where the time goes in v5:
time: 387 us; the launch traced here: 385 us
  waiting for transfers between devices  175 us (45%)
  starting transfers between devices  92.4 us (24%)
  local copies, waits for them, and re-layouts  63.7 us (16%)
  matrix products  32.6 us (8%)
  other arithmetic  9.44 us (2%)
  loops' own time  7.32 us (2%)
  between operations  4.37 us (1%)
    all_to_all x18, waiting for transfers between devices, a2a(): return lax.all_to_all(x, 'dev', split_axis=0, concat_axis=0, tiled=True)  175 us
    all_to_all x18, starting transfers between devices, a2a(): return lax.all_to_all(x, 'dev', split_axis=0, concat_axis=0, tiled=True)  92.4 us
    gather x4, local copies, waits for them, and re-layouts, tiles(): jnp.take(factor_tiles, at_level(slot_tile, current), axis=0, mode='clip')  24.5 us
    dot_general x4, matrix products, tiles(): jnp.einsum('rtb,tbc->rtc', sources, factors, precision=product_precision,...  23 us
    all_to_all x10, local copies, waits for them, and re-layouts, a2a(): return lax.all_to_all(x, 'dev', split_axis=0, concat_axis=0, tiled=True)  9.64 us
  transfers between devices with their start and end apart: 18, of which 18 were waited for; matrix products, arithmetic and copies ran while one was open for 8% of the time, Pallas kernels for 0%

profile of v5, /device:TPU:1, one launch (start us, length us, event | category | flops | bytes accessed | tf_op | source)
XLA Modules:
  0.0 384.8 jit_solution(612602019568201846)
XLA Ops:
  10.1 11.5 %all-to-all-start.4 = ((f32[128,1,512]{2,1,0:T(1,128)}), f32[128,1,512]{2,1,0:T(1,128)S(1)}, u32[]{:S(2)}, u32[]{:S(2)}) async-start(f32[128,1,512]{2,1,0:T(1,128)} %all_to_all.88), calls=%async_computation.4 | async-start | bytes 524288 | tf_op jit(solution)/shard_map/all_to_all | solution.py:34
  24.2 8.2 %all-to-all-done.4 = f32[128,1,512]{2,1,0:T(1,128)S(1)} async-done(((f32[128,1,512]{2,1,0:T(1,128)}), f32[128,1,512]{2,1,0:T(1,128)S(1)}, u32[]{:S(2)}, u32[]{:S(2)}) %all-to-all-start.4) | async-done | bytes 262176 | tf_op jit(solution)/shard_map/all_to_all | solution.py:34
  33.8 4.7 %all-to-all-start.5 = ((f32[128,1,512]{2,1,0:T(1,128)}), f32[128,1,512]{2,1,0:T(1,128)S(1)}, u32[]{:S(2)}, u32[]{:S(2)}) async-start(f32[128,1,512]{2,1,0:T(1,128)} %copy.139), calls=%async_computation.5 | async-start | bytes 524288 | tf_op jit(solution)/shard_map/all_to_all | solution.py:34
  39.1 6.1 %gather_fusion.2 = f32[4,512,512]{2,1,0:T(8,128)} fusion(f32[8,512,512]{2,1,0:T(8,128)} %param.10, s32[1024]{0:T(1024)S(1)} %pad_clamp_fusion.3), kind=kCustom, calls=%fused_computation.2 | custom fusion | bytes 8388624 | tf_op jit(solution)/shard_map/jit(_take)/gather | solution.py:105
  45.2 4.2 %all-to-all-done.5 = f32[128,1,512]{2,1,0:T(1,128)S(1)} async-done(((f32[128,1,512]{2,1,0:T(1,128)}), f32[128,1,512]{2,1,0:T(1,128)S(1)}, u32[]{:S(2)}, u32[]{:S(2)}) %all-to-all-start.5) | async-done | bytes 262176 | tf_op jit(solution)/shard_map/all_to_all | solution.py:34
  51.5 5.6 %all-to-all-start.6 = ((f32[128,2,512]{2,1,0:T(2,128)}), f32[128,2,512]{2,1,0:T(2,128)S(1)}, u32[]{:S(2)}, u32[]{:S(2)}) async-start(f32[128,2,512]{2,1,0:T(2,128)} %reshape.208), calls=%async_computation.6 | async-start | bytes 1048576 | tf_op jit(solution)/shard_map/all_to_all | solution.py:34
  57.3 13.3 %all-to-all-done.6 = f32[128,2,512]{2,1,0:T(2,128)S(1)} async-done(((f32[128,2,512]{2,1,0:T(2,128)}), f32[128,2,512]{2,1,0:T(2,128)S(1)}, u32[]{:S(2)}, u32[]{:S(2)}) %all-to-all-start.6) | async-done | bytes 524320 | tf_op jit(solution)/shard_map/all_to_all | solution.py:34
  71.1 5.8 %select_reduce_fusion.4 = (f32[512,128]{1,0:T(8,128)S(1)}, f32[512,128]{1,0:T(8,128)S(1)}) fusion(pred[4]{0:T(512)(128)(4,1)S(1)} %get-tuple-element.602, pred[4]{0:T(512)(128)(4,1)S(1)} %get-tuple-element.603, f32[4,512,512]{2,1,0:T(8,128)} %gather_fusion.2, f32[128,512]{1,0:T(8,128)S(1)} %bitcast.147, f32[128,512]{1,0:T(8,128)S(1)} %bitcast.146, ...), kind=kOutput, calls=%fused_computation.58 | convolution fusion | flops 806486016 | bytes 5242892 | tf_op jit(solution)/shard_map/rtb,tbc->rtc/dot_general | solution.py:108
  77.9 4.7 %all-to-all-start.7 = ((f32[128,2,512]{2,1,0:T(2,128)}), f32[128,2,512]{2,1,0:T(2,128)S(1)}, u32[]{:S(2)}, u32[]{:S(2)}) async-start(f32[128,2,512]{2,1,0:T(2,128)} %copy.145), calls=%async_computation.7 | async-start | bytes 1048576 | tf_op jit(solution)/shard_map/all_to_all | solution.py:34
  83.2 13.0 %all-to-all-done.7 = f32[128,2,512]{2,1,0:T(2,128)S(1)} async-done(((f32[128,2,512]{2,1,0:T(2,128)}), f32[128,2,512]{2,1,0:T(2,128)S(1)}, u32[]{:S(2)}, u32[]{:S(2)}) %all-to-all-start.7) | async-done | bytes 524320 | tf_op jit(solution)/shard_map/all_to_all | solution.py:34
  96.6 250.8 %while.22 = (s32[]{:T(128)}, f32[128,2,512]{2,1,0:T(2,128)S(1)}, f32[256,512]{1,0:T(8,128)S(1)}, s32[256]{0:T(256)S(1)}, f32[256,512]{1,0:T(8,128)S(1)}, /*index...) while((s32[]{:T(128)}, f32[128,2,512]{2,1,0:T(2,128)S(1)}, ...), condition=%wide.region_24.25_spmd.clone, body=%wide.region_20.24_spmd.clone.sunk | while | flops 1612810240 | bytes 37772900 | solution.py:129
  100.2 4.7 %all-to-all-start = ((f32[128,1,512]{2,1,0:T(1,128)}), f32[128,1,512]{2,1,0:T(1,128)S(1)}, u32[]{:S(2)}, u32[]{:S(2)}) async-start(f32[128,1,512]{2,1,0:T(1,128)} %copy.211), calls=%async_computation | async-start | bytes 524288 | tf_op jit(solution)/shard_map/while/body/eval_jaxpr/all_to_all | solution.py:34
  107.6 8.2 %all-to-all-done = f32[128,1,512]{2,1,0:T(1,128)S(1)} async-done(((f32[128,1,512]{2,1,0:T(1,128)}), f32[128,1,512]{2,1,0:T(1,128)S(1)}, u32[]{:S(2)}, u32[]{:S(2)}) %all-to-all-start) | async-done | bytes 262176 | tf_op jit(solution)/shard_map/while/body/eval_jaxpr/all_to_all | solution.py:34
  115.8 1.6 convolution_bitcast_fusion.4
  118.4 4.7 %all-to-all-start.1 = ((f32[128,1,512]{2,1,0:T(1,128)}), f32[128,1,512]{2,1,0:T(1,128)S(1)}, u32[]{:S(2)}, u32[]{:S(2)}) async-start(f32[128,1,512]{2,1,0:T(1,128)} %copy.212), calls=%async_computation.1 | async-start | bytes 524288 | tf_op jit(solution)/shard_map/while/body/eval_jaxpr/all_to_all | solution.py:34
  123.4 10.5 %all-to-all-done.1 = f32[128,1,512]{2,1,0:T(1,128)S(1)} async-done(((f32[128,1,512]{2,1,0:T(1,128)}), f32[128,1,512]{2,1,0:T(1,128)S(1)}, u32[]{:S(2)}, u32[]{:S(2)}) %all-to-all-start.1) | async-done | bytes 262176 | tf_op jit(solution)/shard_map/while/body/eval_jaxpr/all_to_all | solution.py:34
  136.0 4.7 %all-to-all-start.2 = ((f32[128,2,512]{2,1,0:T(2,128)}), f32[128,2,512]{2,1,0:T(2,128)S(1)}, u32[]{:S(2)}, u32[]{:S(2)}) async-start(f32[128,2,512]{2,1,0:T(2,128)} %reshape.282), calls=%async_computation.2 | async-start | bytes 1048576 | tf_op jit(solution)/shard_map/while/body/eval_jaxpr/all_to_all | solution.py:34
  140.8 6.1 %gather_fusion = f32[4,512,512]{2,1,0:T(8,128)} fusion(f32[8,512,512]{2,1,0:T(8,128)} %get-tuple-element.841, s32[1024]{0:T(1024)S(1)} %pad_clamp_fusion.6), kind=kCustom, calls=%fused_computation.clone.clone.1 | custom fusion | bytes 8388624 | tf_op jit(solution)/shard_map/while/body/eval_jaxpr/jit(_take)/gather | solution.py:105
  147.1 7.2 %all-to-all-done.2 = f32[128,2,512]{2,1,0:T(2,128)S(1)} async-done(((f32[128,2,512]{2,1,0:T(2,128)}), f32[128,2,512]{2,1,0:T(2,128)S(1)}, u32[]{:S(2)}, u32[]{:S(2)}) %all-to-all-start.2) | async-done | bytes 524320 | tf_op jit(solution)/shard_map/while/body/eval_jaxpr/all_to_all | solution.py:34
  154.8 5.8 %select_reduce_fusion.19 = (f32[512,128]{1,0:T(8,128)S(1)}, f32[512,128]{1,0:T(8,128)S(1)}) fusion(pred[4]{0:T(512)(128)(4,1)S(1)} %get-tuple-element.781, pred[4]{0:T(512)(128)(4,1)S(1)} %get-tuple-element.782, f32[4,512,512]{2,1,0:T(8,128)} %gather_fusion, f32[128,512]{1,0:T(8,128)S(1)} %get-tuple-element.786, ...), kind=kOutput, calls=%fused_computation.10.clone.1 | convolution fusion | flops 806486016 | bytes 5242892 | tf_op jit(solution)/shard_map/while/body/eval_jaxpr/rtb,tbc->rtc/dot_general | solution.py:108
  161.6 4.7 %all-to-all-start.3 = ((f32[128,2,512]{2,1,0:T(2,128)}), f32[128,2,512]{2,1,0:T(2,128)S(1)}, u32[]{:S(2)}, u32[]{:S(2)}) async-start(f32[128,2,512]{2,1,0:T(2,128)} %copy.215), calls=%async_computation.3 | async-start | bytes 1048576 | tf_op jit(solution)/shard_map/while/body/eval_jaxpr/all_to_all | solution.py:34
  167.0 12.9 %all-to-all-done.3 = f32[128,2,512]{2,1,0:T(2,128)S(1)} async-done(((f32[128,2,512]{2,1,0:T(2,128)}), f32[128,2,512]{2,1,0:T(2,128)S(1)}, u32[]{:S(2)}, u32[]{:S(2)}) %all-to-all-start.3) | async-done | bytes 524320 | tf_op jit(solution)/shard_map/while/body/eval_jaxpr/all_to_all | solution.py:34
  183.6 4.7 %all-to-all-start = ((f32[128,1,512]{2,1,0:T(1,128)}), f32[128,1,512]{2,1,0:T(1,128)S(1)}, u32[]{:S(2)}, u32[]{:S(2)}) async-start(f32[128,1,512]{2,1,0:T(1,128)} %copy.211), calls=%async_computation | async-start | bytes 524288 | tf_op jit(solution)/shard_map/while/body/eval_jaxpr/all_to_all | solution.py:34
  191.1 8.2 %all-to-all-done = f32[128,1,512]{2,1,0:T(1,128)S(1)} async-done(((f32[128,1,512]{2,1,0:T(1,128)}), f32[128,1,512]{2,1,0:T(1,128)S(1)}, u32[]{:S(2)}, u32[]{:S(2)}) %all-to-all-start) | async-done | bytes 262176 | tf_op jit(solution)/shard_map/while/body/eval_jaxpr/all_to_all | solution.py:34
  201.9 4.7 %all-to-all-start.1 = ((f32[128,1,512]{2,1,0:T(1,128)}), f32[128,1,512]{2,1,0:T(1,128)S(1)}, u32[]{:S(2)}, u32[]{:S(2)}) async-start(f32[128,1,512]{2,1,0:T(1,128)} %copy.212), calls=%async_computation.1 | async-start | bytes 524288 | tf_op jit(solution)/shard_map/while/body/eval_jaxpr/all_to_all | solution.py:34
  206.9 10.5 %all-to-all-done.1 = f32[128,1,512]{2,1,0:T(1,128)S(1)} async-done(((f32[128,1,512]{2,1,0:T(1,128)}), f32[128,1,512]{2,1,0:T(1,128)S(1)}, u32[]{:S(2)}, u32[]{:S(2)}) %all-to-all-start.1) | async-done | bytes 262176 | tf_op jit(solution)/shard_map/while/body/eval_jaxpr/all_to_all | solution.py:34
  219.5 4.7 %all-to-all-start.2 = ((f32[128,2,512]{2,1,0:T(2,128)}), f32[128,2,512]{2,1,0:T(2,128)S(1)}, u32[]{:S(2)}, u32[]{:S(2)}) async-start(f32[128,2,512]{2,1,0:T(2,128)} %reshape.282), calls=%async_computation.2 | async-start | bytes 1048576 | tf_op jit(solution)/shard_map/while/body/eval_jaxpr/all_to_all | solution.py:34
  224.2 6.1 %gather_fusion = f32[4,512,512]{2,1,0:T(8,128)} fusion(f32[8,512,512]{2,1,0:T(8,128)} %get-tuple-element.841, s32[1024]{0:T(1024)S(1)} %pad_clamp_fusion.6), kind=kCustom, calls=%fused_computation.clone.clone.1 | custom fusion | bytes 8388624 | tf_op jit(solution)/shard_map/while/body/eval_jaxpr/jit(_take)/gather | solution.py:105
  230.6 7.2 %all-to-all-done.2 = f32[128,2,512]{2,1,0:T(2,128)S(1)} async-done(((f32[128,2,512]{2,1,0:T(2,128)}), f32[128,2,512]{2,1,0:T(2,128)S(1)}, u32[]{:S(2)}, u32[]{:S(2)}) %all-to-all-start.2) | async-done | bytes 524320 | tf_op jit(solution)/shard_map/while/body/eval_jaxpr/all_to_all | solution.py:34
  238.2 5.8 %select_reduce_fusion.19 = (f32[512,128]{1,0:T(8,128)S(1)}, f32[512,128]{1,0:T(8,128)S(1)}) fusion(pred[4]{0:T(512)(128)(4,1)S(1)} %get-tuple-element.781, pred[4]{0:T(512)(128)(4,1)S(1)} %get-tuple-element.782, f32[4,512,512]{2,1,0:T(8,128)} %gather_fusion, f32[128,512]{1,0:T(8,128)S(1)} %get-tuple-element.786, ...), kind=kOutput, calls=%fused_computation.10.clone.1 | convolution fusion | flops 806486016 | bytes 5242892 | tf_op jit(solution)/shard_map/while/body/eval_jaxpr/rtb,tbc->rtc/dot_general | solution.py:108
  245.0 4.7 %all-to-all-start.3 = ((f32[128,2,512]{2,1,0:T(2,128)}), f32[128,2,512]{2,1,0:T(2,128)S(1)}, u32[]{:S(2)}, u32[]{:S(2)}) async-start(f32[128,2,512]{2,1,0:T(2,128)} %copy.215), calls=%async_computation.3 | async-start | bytes 1048576 | tf_op jit(solution)/shard_map/while/body/eval_jaxpr/all_to_all | solution.py:34
  250.5 12.9 %all-to-all-done.3 = f32[128,2,512]{2,1,0:T(2,128)S(1)} async-done(((f32[128,2,512]{2,1,0:T(2,128)}), f32[128,2,512]{2,1,0:T(2,128)S(1)}, u32[]{:S(2)}, u32[]{:S(2)}) %all-to-all-start.3) | async-done | bytes 524320 | tf_op jit(solution)/shard_map/while/body/eval_jaxpr/all_to_all | solution.py:34
  267.1 4.7 %all-to-all-start = ((f32[128,1,512]{2,1,0:T(1,128)}), f32[128,1,512]{2,1,0:T(1,128)S(1)}, u32[]{:S(2)}, u32[]{:S(2)}) async-start(f32[128,1,512]{2,1,0:T(1,128)} %copy.211), calls=%async_computation | async-start | bytes 524288 | tf_op jit(solution)/shard_map/while/body/eval_jaxpr/all_to_all | solution.py:34
  274.6 8.2 %all-to-all-done = f32[128,1,512]{2,1,0:T(1,128)S(1)} async-done(((f32[128,1,512]{2,1,0:T(1,128)}), f32[128,1,512]{2,1,0:T(1,128)S(1)}, u32[]{:S(2)}, u32[]{:S(2)}) %all-to-all-start) | async-done | bytes 262176 | tf_op jit(solution)/shard_map/while/body/eval_jaxpr/all_to_all | solution.py:34
  282.7 1.6 convolution_bitcast_fusion.4
  285.3 4.7 %all-to-all-start.1 = ((f32[128,1,512]{2,1,0:T(1,128)}), f32[128,1,512]{2,1,0:T(1,128)S(1)}, u32[]{:S(2)}, u32[]{:S(2)}) async-start(f32[128,1,512]{2,1,0:T(1,128)} %copy.212), calls=%async_computation.1 | async-start | bytes 524288 | tf_op jit(solution)/shard_map/while/body/eval_jaxpr/all_to_all | solution.py:34
  290.3 10.5 %all-to-all-done.1 = f32[128,1,512]{2,1,0:T(1,128)S(1)} async-done(((f32[128,1,512]{2,1,0:T(1,128)}), f32[128,1,512]{2,1,0:T(1,128)S(1)}, u32[]{:S(2)}, u32[]{:S(2)}) %all-to-all-start.1) | async-done | bytes 262176 | tf_op jit(solution)/shard_map/while/body/eval_jaxpr/all_to_all | solution.py:34
  303.0 4.7 %all-to-all-start.2 = ((f32[128,2,512]{2,1,0:T(2,128)}), f32[128,2,512]{2,1,0:T(2,128)S(1)}, u32[]{:S(2)}, u32[]{:S(2)}) async-start(f32[128,2,512]{2,1,0:T(2,128)} %reshape.282), calls=%async_computation.2 | async-start | bytes 1048576 | tf_op jit(solution)/shard_map/while/body/eval_jaxpr/all_to_all | solution.py:34
  307.7 6.1 %gather_fusion = f32[4,512,512]{2,1,0:T(8,128)} fusion(f32[8,512,512]{2,1,0:T(8,128)} %get-tuple-element.841, s32[1024]{0:T(1024)S(1)} %pad_clamp_fusion.6), kind=kCustom, calls=%fused_computation.clone.clone.1 | custom fusion | bytes 8388624 | tf_op jit(solution)/shard_map/while/body/eval_jaxpr/jit(_take)/gather | solution.py:105
  314.0 7.2 %all-to-all-done.2 = f32[128,2,512]{2,1,0:T(2,128)S(1)} async-done(((f32[128,2,512]{2,1,0:T(2,128)}), f32[128,2,512]{2,1,0:T(2,128)S(1)}, u32[]{:S(2)}, u32[]{:S(2)}) %all-to-all-start.2) | async-done | bytes 524320 | tf_op jit(solution)/shard_map/while/body/eval_jaxpr/all_to_all | solution.py:34
  321.7 5.8 %select_reduce_fusion.19 = (f32[512,128]{1,0:T(8,128)S(1)}, f32[512,128]{1,0:T(8,128)S(1)}) fusion(pred[4]{0:T(512)(128)(4,1)S(1)} %get-tuple-element.781, pred[4]{0:T(512)(128)(4,1)S(1)} %get-tuple-element.782, f32[4,512,512]{2,1,0:T(8,128)} %gather_fusion, f32[128,512]{1,0:T(8,128)S(1)} %get-tuple-element.786, ...), kind=kOutput, calls=%fused_computation.10.clone.1 | convolution fusion | flops 806486016 | bytes 5242892 | tf_op jit(solution)/shard_map/while/body/eval_jaxpr/rtb,tbc->rtc/dot_general | solution.py:108
  328.5 4.7 %all-to-all-start.3 = ((f32[128,2,512]{2,1,0:T(2,128)}), f32[128,2,512]{2,1,0:T(2,128)S(1)}, u32[]{:S(2)}, u32[]{:S(2)}) async-start(f32[128,2,512]{2,1,0:T(2,128)} %copy.215), calls=%async_computation.3 | async-start | bytes 1048576 | tf_op jit(solution)/shard_map/while/body/eval_jaxpr/all_to_all | solution.py:34
  334.0 12.9 %all-to-all-done.3 = f32[128,2,512]{2,1,0:T(2,128)S(1)} async-done(((f32[128,2,512]{2,1,0:T(2,128)}), f32[128,2,512]{2,1,0:T(2,128)S(1)}, u32[]{:S(2)}, u32[]{:S(2)}) %all-to-all-start.3) | async-done | bytes 524320 | tf_op jit(solution)/shard_map/while/body/eval_jaxpr/all_to_all | solution.py:34
  349.6 4.7 %all-to-all-start.8 = ((f32[128,1,512]{2,1,0:T(1,128)}), f32[128,1,512]{2,1,0:T(1,128)S(1)}, u32[]{:S(2)}, u32[]{:S(2)}) async-start(f32[128,1,512]{2,1,0:T(1,128)} %copy.157), calls=%async_computation.8 | async-start | bytes 524288 | tf_op jit(solution)/shard_map/all_to_all | solution.py:34
  356.1 9.1 %all-to-all-done.8 = f32[128,1,512]{2,1,0:T(1,128)S(1)} async-done(((f32[128,1,512]{2,1,0:T(1,128)}), f32[128,1,512]{2,1,0:T(1,128)S(1)}, u32[]{:S(2)}, u32[]{:S(2)}) %all-to-all-start.8) | async-done | bytes 262176 | tf_op jit(solution)/shard_map/all_to_all | solution.py:34
  365.2 1.6 convolution_bitcast_fusion.1
  367.8 4.7 %all-to-all-start.9 = ((f32[128,1,512]{2,1,0:T(1,128)}), f32[128,1,512]{2,1,0:T(1,128)S(1)}, u32[]{:S(2)}, u32[]{:S(2)}) async-start(f32[128,1,512]{2,1,0:T(1,128)} %copy.158), calls=%async_computation.9 | async-start | bytes 524288 | tf_op jit(solution)/shard_map/all_to_all | solution.py:34
  372.7 10.7 %all-to-all-done.9 = f32[128,1,512]{2,1,0:T(1,128)S(1)} async-done(((f32[128,1,512]{2,1,0:T(1,128)}), f32[128,1,512]{2,1,0:T(1,128)S(1)}, u32[]{:S(2)}, u32[]{:S(2)}) %all-to-all-start.9) | async-done | bytes 262176 | tf_op jit(solution)/shard_map/all_to_all | solution.py:34
  (182 shorter events, 53.4 us)
Async XLA Ops:
  0.0 32.4 %copy-start = (f32[2,512,512]{2,1,0:T(8,128)S(1)}, f32[2,512,512]{2,1,0:T(8,128)}, u32[]{:S(2)}) copy-start(f32[2,512,512]{2,1,0:T(8,128)} %param.9) | copy-start | bytes 6291460
  10.1 22.3 %all-to-all-start.4 = ((f32[128,1,512]{2,1,0:T(1,128)}), f32[128,1,512]{2,1,0:T(1,128)S(1)}, u32[]{:S(2)}, u32[]{:S(2)}) async-start(f32[128,1,512]{2,1,0:T(1,128)} %all_to_all.88), calls=%async_computation.4 | async-start | bytes 524288 | tf_op jit(solution)/shard_map/all_to_all | solution.py:34
  33.8 15.5 %all-to-all-start.5 = ((f32[128,1,512]{2,1,0:T(1,128)}), f32[128,1,512]{2,1,0:T(1,128)S(1)}, u32[]{:S(2)}, u32[]{:S(2)}) async-start(f32[128,1,512]{2,1,0:T(1,128)} %copy.139), calls=%async_computation.5 | async-start | bytes 524288 | tf_op jit(solution)/shard_map/all_to_all | solution.py:34
  45.2 12.1 %copy-start.1 = (s32[256]{0:T(256)S(1)}, s32[256]{0:T(256)}, u32[]{:S(2)}) copy-start(s32[256]{0:T(256)} %param.11) | copy-start | bytes 3076
  51.5 19.2 %all-to-all-start.6 = ((f32[128,2,512]{2,1,0:T(2,128)}), f32[128,2,512]{2,1,0:T(2,128)S(1)}, u32[]{:S(2)}, u32[]{:S(2)}) async-start(f32[128,2,512]{2,1,0:T(2,128)} %reshape.208), calls=%async_computation.6 | async-start | bytes 1048576 | tf_op jit(solution)/shard_map/all_to_all | solution.py:34
  77.9 18.4 %all-to-all-start.7 = ((f32[128,2,512]{2,1,0:T(2,128)}), f32[128,2,512]{2,1,0:T(2,128)S(1)}, u32[]{:S(2)}, u32[]{:S(2)}) async-start(f32[128,2,512]{2,1,0:T(2,128)} %copy.145), calls=%async_computation.7 | async-start | bytes 1048576 | tf_op jit(solution)/shard_map/all_to_all | solution.py:34
  100.2 15.6 %all-to-all-start = ((f32[128,1,512]{2,1,0:T(1,128)}), f32[128,1,512]{2,1,0:T(1,128)S(1)}, u32[]{:S(2)}, u32[]{:S(2)}) async-start(f32[128,1,512]{2,1,0:T(1,128)} %copy.211), calls=%async_computation | async-start | bytes 524288 | tf_op jit(solution)/shard_map/while/body/eval_jaxpr/all_to_all | solution.py:34
  118.4 15.5 %all-to-all-start.1 = ((f32[128,1,512]{2,1,0:T(1,128)}), f32[128,1,512]{2,1,0:T(1,128)S(1)}, u32[]{:S(2)}, u32[]{:S(2)}) async-start(f32[128,1,512]{2,1,0:T(1,128)} %copy.212), calls=%async_computation.1 | async-start | bytes 524288 | tf_op jit(solution)/shard_map/while/body/eval_jaxpr/all_to_all | solution.py:34
  136.0 18.3 %all-to-all-start.2 = ((f32[128,2,512]{2,1,0:T(2,128)}), f32[128,2,512]{2,1,0:T(2,128)S(1)}, u32[]{:S(2)}, u32[]{:S(2)}) async-start(f32[128,2,512]{2,1,0:T(2,128)} %reshape.282), calls=%async_computation.2 | async-start | bytes 1048576 | tf_op jit(solution)/shard_map/while/body/eval_jaxpr/all_to_all | solution.py:34
  161.6 18.4 %all-to-all-start.3 = ((f32[128,2,512]{2,1,0:T(2,128)}), f32[128,2,512]{2,1,0:T(2,128)S(1)}, u32[]{:S(2)}, u32[]{:S(2)}) async-start(f32[128,2,512]{2,1,0:T(2,128)} %copy.215), calls=%async_computation.3 | async-start | bytes 1048576 | tf_op jit(solution)/shard_map/while/body/eval_jaxpr/all_to_all | solution.py:34
  183.6 15.6 %all-to-all-start = ((f32[128,1,512]{2,1,0:T(1,128)}), f32[128,1,512]{2,1,0:T(1,128)S(1)}, u32[]{:S(2)}, u32[]{:S(2)}) async-start(f32[128,1,512]{2,1,0:T(1,128)} %copy.211), calls=%async_computation | async-start | bytes 524288 | tf_op jit(solution)/shard_map/while/body/eval_jaxpr/all_to_all | solution.py:34
  201.9 15.5 %all-to-all-start.1 = ((f32[128,1,512]{2,1,0:T(1,128)}), f32[128,1,512]{2,1,0:T(1,128)S(1)}, u32[]{:S(2)}, u32[]{:S(2)}) async-start(f32[128,1,512]{2,1,0:T(1,128)} %copy.212), calls=%async_computation.1 | async-start | bytes 524288 | tf_op jit(solution)/shard_map/while/body/eval_jaxpr/all_to_all | solution.py:34
  219.5 18.3 %all-to-all-start.2 = ((f32[128,2,512]{2,1,0:T(2,128)}), f32[128,2,512]{2,1,0:T(2,128)S(1)}, u32[]{:S(2)}, u32[]{:S(2)}) async-start(f32[128,2,512]{2,1,0:T(2,128)} %reshape.282), calls=%async_computation.2 | async-start | bytes 1048576 | tf_op jit(solution)/shard_map/while/body/eval_jaxpr/all_to_all | solution.py:34
  245.0 18.4 %all-to-all-start.3 = ((f32[128,2,512]{2,1,0:T(2,128)}), f32[128,2,512]{2,1,0:T(2,128)S(1)}, u32[]{:S(2)}, u32[]{:S(2)}) async-start(f32[128,2,512]{2,1,0:T(2,128)} %copy.215), calls=%async_computation.3 | async-start | bytes 1048576 | tf_op jit(solution)/shard_map/while/body/eval_jaxpr/all_to_all | solution.py:34
  267.1 15.6 %all-to-all-start = ((f32[128,1,512]{2,1,0:T(1,128)}), f32[128,1,512]{2,1,0:T(1,128)S(1)}, u32[]{:S(2)}, u32[]{:S(2)}) async-start(f32[128,1,512]{2,1,0:T(1,128)} %copy.211), calls=%async_computation | async-start | bytes 524288 | tf_op jit(solution)/shard_map/while/body/eval_jaxpr/all_to_all | solution.py:34
  285.3 15.5 %all-to-all-start.1 = ((f32[128,1,512]{2,1,0:T(1,128)}), f32[128,1,512]{2,1,0:T(1,128)S(1)}, u32[]{:S(2)}, u32[]{:S(2)}) async-start(f32[128,1,512]{2,1,0:T(1,128)} %copy.212), calls=%async_computation.1 | async-start | bytes 524288 | tf_op jit(solution)/shard_map/while/body/eval_jaxpr/all_to_all | solution.py:34
  303.0 18.3 %all-to-all-start.2 = ((f32[128,2,512]{2,1,0:T(2,128)}), f32[128,2,512]{2,1,0:T(2,128)S(1)}, u32[]{:S(2)}, u32[]{:S(2)}) async-start(f32[128,2,512]{2,1,0:T(2,128)} %reshape.282), calls=%async_computation.2 | async-start | bytes 1048576 | tf_op jit(solution)/shard_map/while/body/eval_jaxpr/all_to_all | solution.py:34
  328.5 18.4 %all-to-all-start.3 = ((f32[128,2,512]{2,1,0:T(2,128)}), f32[128,2,512]{2,1,0:T(2,128)S(1)}, u32[]{:S(2)}, u32[]{:S(2)}) async-start(f32[128,2,512]{2,1,0:T(2,128)} %copy.215), calls=%async_computation.3 | async-start | bytes 1048576 | tf_op jit(solution)/shard_map/while/body/eval_jaxpr/all_to_all | solution.py:34
  349.6 15.6 %all-to-all-start.8 = ((f32[128,1,512]{2,1,0:T(1,128)}), f32[128,1,512]{2,1,0:T(1,128)S(1)}, u32[]{:S(2)}, u32[]{:S(2)}) async-start(f32[128,1,512]{2,1,0:T(1,128)} %copy.157), calls=%async_computation.8 | async-start | bytes 524288 | tf_op jit(solution)/shard_map/all_to_all | solution.py:34
  367.8 15.5 %all-to-all-start.9 = ((f32[128,1,512]{2,1,0:T(1,128)}), f32[128,1,512]{2,1,0:T(1,128)S(1)}, u32[]{:S(2)}, u32[]{:S(2)}) async-start(f32[128,1,512]{2,1,0:T(1,128)} %copy.158), calls=%async_computation.9 | async-start | bytes 524288 | tf_op jit(solution)/shard_map/all_to_all | solution.py:34
